TPU v7x, 32 devices: a whole 2x2x4 slice. The times are simulated.
32 devices in a mesh: groups: 2 (over y), wide: 4 (over z), narrow: 2 (over x), slab: 2 (over core).
Axes of the slice: x: 2, y: 2, z: 4, core: 2. Of those that a mesh axis runs over, the one named last changes fastest.
Arguments:
- obs_latitude: float32 [256, 128], P(('groups', 'wide')), parts along dimension 0, may hold values from -0.1 to 0.1
- obs_offset: float32 [256, 128], P(('groups', 'wide')), parts along dimension 0, may hold values from -16 to 17
- innovation: float32 [256, 128], P(('groups', 'wide')), parts along dimension 0, may hold values from -6 to 6
- obs_error: float32 [256, 128], P(('groups', 'wide')), parts along dimension 0, may hold values from 0.5 to 1.5
- region_sizes: int32 [256], P(('groups', 'wide')), parts along dimension 0, may hold values from 1 to 128, as said below
- tile_columns: int32 [256, 4], P(('groups', 'wide')), parts along dimension 0, may hold values from 0 to 127, as said below
- slab_list: int32 [256, 4], P(('groups', 'wide')), parts along dimension 0, may hold values from 0 to 31, as said below
- slab_order: int32 [64], P('groups'), parts along dimension 0, may hold values from 0 to 31, each once
- grid_latitude: float32 [32, 512], replicated, may hold values from -0.1 to 0.1
- grid_offset: float32 [32, 512], replicated, may hold values from -4 to 5
- ridge_weight: float32 [16], P('narrow'), may hold values from 0.1 to 2
- huber_cut: float32 [16], P('narrow'), may hold values from 0.5 to 2.5
- step_size: float32 [16], P('narrow'), may hold values from 0.3 to 0.6
Outputs:
- obs_weights: float32 [256, 16, 128], P(('groups', 'wide'), 'narrow'), parts along dimension 0
- grid_increment: float32 [64, 16, 512], P(('groups', 'wide', 'slab'), 'narrow'), parts along dimension 0
There are 2 independent parts, one for each index of `groups`. A program takes and returns all parts, laid end to end along the dimension named above; an argument that names none is the same for every part. Nothing has to cross between parts.
Inputs may be any that keep to these rules, and one draw needn't show every extreme that they name: `tile_columns`: the 4 entries of a row a are distinct regions (a + o) mod 128 with offsets o from -16 to 16. `slab_list`: the 4 entries of a row a are distinct slabs (a * 32 // 128 + o) mod 32 with offsets o from -4 to 4. `slab_order`: a permutation of the slabs. `region_sizes`: in each analysis case the largest is exactly 128.
All inputs are finite; a program needn't handle non-finite values.
Results may differ from a plain program's by a relative error of at most 0.0001.
Values sent between devices are 32-bit elements; how exact they have to be, the bound alone decides.
No kernel may reach another device: no remote copies, remote signals or barrier semaphores. Data moves between devices by JAX's collectives and lax.ppermute only.
A program may use at most 64 MiB of HBM per device.

v0:
```python
import jax
import jax.numpy as jnp
from jax import lax
from jax.experimental import pallas as pl
from jax.experimental.pallas import tpu as pltpu
from jax.sharding import PartitionSpec as P

ITERS = 2
SLAB_REACH = 4

DECAY_RATE = 1.0 / 0.15
FULL_TURN = 6.283185307179586
HIGHEST = lax.Precision.HIGHEST
ROWS = 8
GROUP = 4


def with_halo(cells, axis, width):
    count = lax.axis_size(axis)
    head = lax.slice_in_dim(cells, 0, width, axis=0)
    tail = lax.slice_in_dim(cells, cells.shape[0] - width, cells.shape[0], axis=0)
    return jnp.concatenate(
        [
            lax.ppermute(tail, axis, [(i, (i + 1) % count) for i in range(count)]),
            cells,
            lax.ppermute(head, axis, [((i + 1) % count, i) for i in range(count)]),
        ],
        axis=0,
    )


def gather_slots(x, axis):
    count = lax.axis_size(axis)
    parts = [x]
    for s in range(1, count):
        parts.append(lax.ppermute(x, axis, [(i, (i + s) % count) for i in range(count)]))
    return jnp.concatenate(parts, axis=0)


def unit_rows(latitude, longitude):
    c = jnp.cos(latitude)
    zero = jnp.zeros_like(latitude)
    return jnp.stack(
        [c * jnp.cos(longitude), c * jnp.sin(longitude), jnp.sin(latitude)] + [zero] * (ROWS - 3),
        axis=-2,
    )


def corr_block(col_t, row):
    dx = col_t[:, 0:1] - row[0:1, :]
    dy = col_t[:, 1:2] - row[1:2, :]
    dz = col_t[:, 2:3] - row[2:3, :]
    d2 = dx * dx + dy * dy + dz * dz
    return jnp.exp(jnp.sqrt(d2) * (-DECAY_RATE))


def contract_lanes(w, c):
    return lax.dot_general(
        w, c, (((1,), (1,)), ((), ())), precision=HIGHEST, preferred_element_type=jnp.float32
    )


def make_update_kernel(margin, tile_scale):
    def update_kernel(
        cols_ref, own_ref, halo_ref, w_ref, obs_ref, diag_ref, thr_ref, live_ref, step_ref,
        out_ref, buf0, buf1,
    ):
        reg_dev, _, cap = own_ref.shape
        tiles = cols_ref.shape[0] // reg_dev

        def fill(a, buf):
            own_t = own_ref[a].T
            for t in range(tiles):
                b = cols_ref[a * tiles + t]
                buf[:, t * cap : (t + 1) * cap] = corr_block(own_t, halo_ref[b])

        def use(a, buf):
            weights = jnp.concatenate(
                [w_ref[cols_ref[a * tiles + t]] for t in range(tiles)], axis=1
            )
            cov = contract_lanes(weights, buf[...])
            current = w_ref[a + margin]
            diag = diag_ref[a]
            thr = thr_ref[a]
            applied = cov * tile_scale + diag * current
            residual = (obs_ref[a] - applied) * live_ref[a]
            factor = thr / jnp.maximum(jnp.abs(residual), thr)
            out_ref[a] = current + step_ref[...] * factor * residual / diag

        fill(0, buf0)

        def pair(i, carry):
            a = 2 * i
            use(a, buf0)
            fill(a + 1, buf1)
            use(a + 1, buf1)
            fill(jnp.minimum(a + 2, reg_dev - 1), buf0)
            return carry

        lax.fori_loop(0, reg_dev // 2, pair, 0)

    return update_kernel


def update(cols, own_sites, halo_sites, halo_w, observed, diagonal, threshold, live, step, margin, tile_scale):
    reg_dev, _, cap = own_sites.shape
    assert reg_dev % 2 == 0
    tiles = cols.shape[0] // reg_dev
    vmem = pl.BlockSpec(memory_space=pltpu.VMEM)
    return pl.pallas_call(
        make_update_kernel(margin, tile_scale),
        out_shape=jax.ShapeDtypeStruct(diagonal.shape, jnp.float32),
        in_specs=[pl.BlockSpec(memory_space=pltpu.SMEM)] + [vmem] * 8,
        out_specs=vmem,
        scratch_shapes=[pltpu.VMEM((cap, tiles * cap), jnp.float32)] * 2,
    )(cols, own_sites, halo_sites, halo_w, observed, diagonal, threshold, live, step)


def make_grid_kernel(per_slab, reg_dev, n_wide, cap, regions):
    window = (2 * SLAB_REACH + 1) * per_slab

    def grid_kernel(
        me_ref, own_slabs_ref, list_ref, sites_ref, w_ref, gsites_ref, out_ref,
        sel_ref, slab_ref, buf0, buf1,
    ):
        n_own = out_ref.shape[0]
        gpr = list_ref.shape[0] // regions
        me = me_ref[0]
        total = jnp.int32(0)
        for j in range(n_own):
            slab = own_slabs_ref[j]
            start = (slab - SLAB_REACH) * per_slab + regions

            def scan(r, count):
                a = lax.rem(start + r, regions)
                owner = a // reg_dev
                slot = lax.rem(me - owner + n_wide, n_wide) * reg_dev + lax.rem(a, reg_dev)
                listed = list_ref[slot * gpr] == slab
                for e in range(1, gpr):
                    listed = jnp.logical_or(listed, list_ref[slot * gpr + e] == slab)
                sel_ref[count] = slot
                return count + listed.astype(jnp.int32)

            first_group = total // GROUP
            total = lax.fori_loop(0, window, scan, total)
            for e in range(GROUP):
                sel_ref[total + e] = regions
            total = (total + GROUP - 1) // GROUP * GROUP

            def mark(g, carry):
                slab_ref[g] = j
                return carry

            lax.fori_loop(first_group, total // GROUP, mark, 0)
        n_groups = total // GROUP
        for e in range(GROUP):
            sel_ref[total + e] = regions
        slab_ref[n_groups] = 0
        n_pairs = (n_groups + 1) // 2
        last = 2 * n_pairs - 1
        out_ref[...] = jnp.zeros(out_ref.shape, jnp.float32)

        def fill(g, buf):
            g_t = gsites_ref[slab_ref[g]].T
            for e in range(GROUP):
                slot = sel_ref[g * GROUP + e]
                buf[:, e * cap : (e + 1) * cap] = corr_block(g_t, sites_ref[slot])

        def use(g, buf):
            j = slab_ref[g]
            weights = jnp.concatenate(
                [w_ref[sel_ref[g * GROUP + e]] for e in range(GROUP)], axis=1
            )
            out_ref[j] = out_ref[j] + contract_lanes(weights, buf[...])

        fill(0, buf0)

        def pair(i, carry):
            g = 2 * i
            use(g, buf0)
            fill(g + 1, buf1)
            use(g + 1, buf1)
            fill(jnp.minimum(g + 2, last), buf0)
            return carry

        lax.fori_loop(0, n_pairs, pair, 0)
        out_ref[...] = out_ref[...] / cap

    return grid_kernel, window


def grid_stage(me, own_slabs, list_slots, site_slots, w_slots, gsites, reg_dev, n_wide, regions, slab_count):
    solves, cap = w_slots.shape[1:]
    n_own, _, gpts = gsites.shape
    kernel, window = make_grid_kernel(regions // slab_count, reg_dev, n_wide, cap, regions)
    vmem = pl.BlockSpec(memory_space=pltpu.VMEM)
    smem = pl.BlockSpec(memory_space=pltpu.SMEM)
    sel_len = n_own * (window + GROUP) + 2 * GROUP
    return pl.pallas_call(
        kernel,
        out_shape=jax.ShapeDtypeStruct((n_own, solves, gpts), jnp.float32),
        in_specs=[smem, smem, smem, vmem, vmem, vmem],
        out_specs=vmem,
        scratch_shapes=[
            pltpu.SMEM((sel_len,), jnp.int32),
            pltpu.SMEM((sel_len // GROUP + 2,), jnp.int32),
            pltpu.VMEM((gpts, GROUP * cap), jnp.float32),
            pltpu.VMEM((gpts, GROUP * cap), jnp.float32),
        ],
    )(me, own_slabs, list_slots, site_slots, w_slots, gsites)


def body(
    obs_latitude,
    obs_offset,
    innovation,
    obs_error,
    region_sizes,
    tile_columns,
    slab_list,
    slab_order,
    grid_latitude,
    grid_offset,
    ridge_weight,
    huber_cut,
    step_size,
):
    reg_dev, capacity = innovation.shape
    n_wide = lax.axis_size("wide")
    regions = reg_dev * n_wide
    margin = reg_dev // 2
    me = lax.axis_index("wide")
    first_row = me * reg_dev
    row_ids = first_row + jnp.arange(reg_dev, dtype=jnp.int32)
    obs_lon = FULL_TURN * (row_ids[:, None].astype(jnp.float32) + obs_offset) / regions
    obs_sites = unit_rows(obs_latitude, obs_lon)
    gpr = slab_list.shape[1]
    packed = jnp.concatenate(
        [
            obs_sites[:, :4, :],
            jnp.pad(slab_list.astype(jnp.float32), ((0, 0), (0, capacity - gpr)))[:, None, :],
        ],
        axis=1,
    )
    slots = gather_slots(packed, "wide")
    spare = jnp.zeros((ROWS, ROWS, capacity), jnp.float32)
    site_slots = jnp.concatenate(
        [jnp.pad(slots[:, :3, :], ((0, 0), (0, ROWS - 3), (0, 0))), spare], axis=0
    )
    list_slots = slots[:, 4, :gpr].astype(jnp.int32).reshape(-1)
    left = site_slots[2 * reg_dev - margin : 2 * reg_dev]
    right = site_slots[(n_wide - 1) * reg_dev : (n_wide - 1) * reg_dev + margin]
    sites_wide = jnp.concatenate([left, obs_sites, right], axis=0)
    live_mask = (jnp.arange(capacity, dtype=jnp.int32)[None, :] < region_sizes[:, None]).astype(
        jnp.float32
    )
    solves = ridge_weight.shape[0]
    diagonal = (obs_error * obs_error)[:, None, :] + ridge_weight[None, :, None]
    observed = (innovation * live_mask)[:, None, :]
    threshold = huber_cut[None, :, None] * obs_error[:, None, :]
    obs_weights = observed / diagonal
    live = live_mask[:, None, :]
    step = jnp.broadcast_to(step_size[:, None], (solves, capacity))
    local_cols = ((tile_columns - first_row + margin) % regions).reshape(-1)
    tile_scale = 2.0 / (capacity * tile_columns.shape[1])
    for sweep_index in range(ITERS):
        weights_wide = with_halo(obs_weights, "wide", margin)
        obs_weights = update(
            local_cols, obs_sites, sites_wide, weights_wide, observed, diagonal, threshold,
            live, step, margin, tile_scale,
        )
    w_slots = jnp.concatenate(
        [gather_slots(obs_weights, "wide"), jnp.zeros((ROWS, solves, capacity), jnp.float32)], axis=0
    )

    slab_count = slab_order.shape[0]
    n_slab = lax.axis_size("slab")
    n_own = slab_count // (n_wide * n_slab)
    pos0 = (me * n_slab + lax.axis_index("slab")) * n_own
    own_slabs = lax.dynamic_slice_in_dim(slab_order, pos0, n_own, 0)
    g_lat = grid_latitude[own_slabs]
    g_lon = FULL_TURN * (own_slabs[:, None].astype(jnp.float32) + grid_offset[own_slabs]) / slab_count
    gsites = unit_rows(g_lat, g_lon)
    grid_increment = grid_stage(
        me.astype(jnp.int32).reshape(1),
        own_slabs,
        list_slots,
        site_slots,
        w_slots,
        gsites,
        reg_dev,
        n_wide,
        regions,
        slab_count,
    )
    return (obs_weights, grid_increment)


def solution(mesh):
    in_specs = (
        P(("groups", "wide"), None),
        P(("groups", "wide"), None),
        P(("groups", "wide"), None),
        P(("groups", "wide"), None),
        P(("groups", "wide")),
        P(("groups", "wide"), None),
        P(("groups", "wide"), None),
        P("groups"),
        P(),
        P(),
        P("narrow"),
        P("narrow"),
        P("narrow"),
    )
    out_specs = (
        P(("groups", "wide"), "narrow", None),
        P(("groups", "wide", "slab"), "narrow", None),
    )
    return jax.shard_map(body, mesh=mesh, in_specs=in_specs, out_specs=out_specs, check_vma=False)
```

profile of v0, /device:TPU:12, one launch (start us, length us, event | category | flops | bytes accessed | tf_op | source)
XLA Modules:
  0.0 108.7 jit_solution(14543206893824816382)
XLA Ops:
  0.7 0.8 fusion.6
  2.3 0.7 copy-done.9
  3.8 2.6 %collective-permute-start.1 = (f32[32,5,128]{2,1,0:T(8,128)S(1)}, f32[32,5,128]{2,1,0:T(8,128)S(1)}, u32[]{:S(2)}, u32[]{:S(2)}) collective-permute-start(f32[32,5,128]{2,1,0:T(8,128)S(1)} %concatenate.23), channel_id=1, source_target_pairs={{0,8},{4,12},{8,0},{12,4},{1,9},{5,13},{9,1},{13,5},{2,10},{6,14},... | collective-permute-start | bytes 245768 | tf_op jit(solution)/shard_map/ppermute | solution.py:36
  6.4 2.5 %collective-permute-start = (f32[32,5,128]{2,1,0:T(8,128)S(1)}, f32[32,5,128]{2,1,0:T(8,128)S(1)}, u32[]{:S(2)}, u32[]{:S(2)}) collective-permute-start(f32[32,5,128]{2,1,0:T(8,128)S(1)} %concatenate.23), channel_id=1, source_target_pairs={{0,4},{4,8},{8,12},{12,0},{1,5},{5,9},{9,13},{13,1},{2,6},{6,10},{... | collective-permute-start | bytes 245768 | tf_op jit(solution)/shard_map/ppermute | solution.py:36
  9.6 0.7 broadcast_add_fusion
  10.4 2.0 %collective-permute-start.3 = (f32[16,8,128]{2,1,0:T(8,128)S(1)}, f32[16,8,128]{2,1,0:T(8,128)S(1)}, u32[]{:S(2)}, u32[]{:S(2)}) collective-permute-start(f32[16,8,128]{2,1,0:T(8,128)S(1)} %get-tuple-element.8), channel_id=1, source_target_pairs={{0,4},{4,8},{8,12},{12,0},{1,5},{5,9},{9,13},{13,1},{2,6},{6,10},{... | collective-permute-start | bytes 196616 | tf_op jit(solution)/shard_map/ppermute | solution.py:24
  12.4 0.7 compare_convert_fusion.live_ref
  13.1 0.7 broadcast_multiply_fusion.thr_ref
  18.5 1.5 %collective-permute-done.4 = f32[16,8,128]{2,1,0:T(8,128)S(1)} collective-permute-done((f32[16,8,128]{2,1,0:T(8,128)S(1)}, f32[16,8,128]{2,1,0:T(8,128)S(1)}, u32[]{:S(2)}, u32[]{:S(2)}) %collective-permute-start.4) | collective-permute-done | bytes 65568 | tf_op jit(solution)/shard_map/ppermute | solution.py:26
  20.1 0.7 pad_maximum_fusion.2.w_ref
  21.0 0.7 pad_maximum_fusion.1.halo_ref
  23.0 16.2 %shard_map.140 = f32[32,8,128]{2,1,0:T(8,128)} custom-call(s32[128]{0:T(128)} %reshape.135.cols_ref, f32[32,8,128]{2,1,0:T(8,128)} %copy-done.1, f32[64,8,128]{2,1,0:T(8,128)} %pad_maximum_fusion.1.halo_ref, f32[64,8,128]{2,1,0:T(8,128)} %pad_maximum_fusion.2.w_ref, f32[32,1,128]{2,1,0:T(1,128)} %bitcast.8, f32[32,8,128]{2,1,0:T(8,128)} %get-tuple-element.14.diag_ref, ...), custom_call_target="tpu_custom_call" | custom-call | tf_op jit(solution)/shard_map/pallas_call | solution.py:110
  39.2 0.9 fusion.4
  40.1 2.5 %collective-permute-start.5 = (f32[16,8,128]{2,1,0:T(8,128)S(1)}, f32[16,8,128]{2,1,0:T(8,128)S(1)}, u32[]{:S(2)}, u32[]{:S(2)}) collective-permute-start(f32[16,8,128]{2,1,0:T(8,128)S(1)} %get-tuple-element.6), channel_id=1, source_target_pairs={{0,4},{4,8},{8,12},{12,0},{1,5},{5,9},{9,13},{13,1},{2,6},{6,10},{... | collective-permute-start | bytes 196616 | tf_op jit(solution)/shard_map/ppermute | solution.py:24
  43.7 1.8 %collective-permute-done.6 = f32[16,8,128]{2,1,0:T(8,128)S(1)} collective-permute-done((f32[16,8,128]{2,1,0:T(8,128)S(1)}, f32[16,8,128]{2,1,0:T(8,128)S(1)}, u32[]{:S(2)}, u32[]{:S(2)}) %collective-permute-start.6) | collective-permute-done | bytes 65568 | tf_op jit(solution)/shard_map/ppermute | solution.py:26
  45.6 0.7 pad_maximum_fusion.3.w_ref
  46.3 16.2 %shard_map.141 = f32[32,8,128]{2,1,0:T(8,128)} custom-call(s32[128]{0:T(128)} %reshape.135.cols_ref, f32[32,8,128]{2,1,0:T(8,128)} %copy-done.1, f32[64,8,128]{2,1,0:T(8,128)} %pad_maximum_fusion.1.halo_ref, f32[64,8,128]{2,1,0:T(8,128)} %pad_maximum_fusion.3.w_ref, f32[32,1,128]{2,1,0:T(1,128)} %bitcast.9, f32[32,8,128]{2,1,0:T(8,128)} %get-tuple-element.14.diag_ref, ...), custom_call_target="tpu_custom_call" | custom-call | tf_op jit(solution)/shard_map/pallas_call | solution.py:110
  62.5 1.5 %collective-permute-start.7 = (f32[32,8,128]{2,1,0:T(8,128)}, f32[32,8,128]{2,1,0:T(8,128)S(1)}, u32[]{:S(2)}, u32[]{:S(2)}) collective-permute-start(f32[32,8,128]{2,1,0:T(8,128)} %shard_map.141), channel_id=1, source_target_pairs={{0,4},{4,8},{8,12},{12,0},{1,5},{5,9},{9,13},{13,1},{2,6},{6,10},{... | collective-permute-start | bytes 393224 | tf_op jit(solution)/shard_map/ppermute | solution.py:36
  64.9 0.8 concatenate.28.sites_ref
  65.8 4.0 %collective-permute-start.8 = (f32[32,8,128]{2,1,0:T(8,128)S(1)}, f32[32,8,128]{2,1,0:T(8,128)S(1)}, u32[]{:S(2)}, u32[]{:S(2)}) collective-permute-start(f32[32,8,128]{2,1,0:T(8,128)S(1)} %copy-done.4), channel_id=1, source_target_pairs={{0,8},{4,12},{8,0},{12,4},{1,9},{5,13},{9,1},{13,5},{2,10},{6,14},... | collective-permute-start | bytes 393224 | tf_op jit(solution)/shard_map/ppermute | solution.py:36
  70.2 5.1 %collective-permute-done.8 = f32[32,8,128]{2,1,0:T(8,128)S(1)} collective-permute-done((f32[32,8,128]{2,1,0:T(8,128)S(1)}, f32[32,8,128]{2,1,0:T(8,128)S(1)}, u32[]{:S(2)}, u32[]{:S(2)}) %collective-permute-start.8) | collective-permute-done | bytes 131104 | tf_op jit(solution)/shard_map/ppermute | solution.py:36
  75.3 2.7 %collective-permute-done.9 = f32[32,8,128]{2,1,0:T(8,128)S(1)} collective-permute-done((f32[32,8,128]{2,1,0:T(8,128)S(1)}, f32[32,8,128]{2,1,0:T(8,128)S(1)}, u32[]{:S(2)}, u32[]{:S(2)}) %collective-permute-start.9) | collective-permute-done | bytes 131104 | tf_op jit(solution)/shard_map/ppermute | solution.py:36
  78.0 0.8 copy-done.3
  78.8 29.9 %shard_map.142 = f32[4,8,512]{2,1,0:T(8,128)} custom-call(s32[1]{0:T(128)} %bitcast.7.me_ref, s32[4]{0:T(128)} %copy-done.11, s32[512]{0:T(512)} %convert_element_type.40.list_ref, f32[136,8,128]{2,1,0:T(8,128)} %concatenate.28.sites_ref, f32[136,8,128]{2,1,0:T(8,128)} %copy-done.3, f32[4,8,512]{2,1,0:T(8,128)} %stack.30.gsites_ref), custom_call_target="tpu_custom_call" | custom-call | tf_op jit(solution)/shard_map/pallas_call | solution.py:199
  (82 shorter events, 11.0 us)
Async XLA Ops:
  0.6 14.5 %copy-start = (f32[32,512]{1,0:T(8,128)S(1)}, f32[32,512]{1,0:T(8,128)}, u32[]{:S(2)}) copy-start(f32[32,512]{1,0:T(8,128)} %param.21) | copy-start | bytes 196612
  1.5 0.7 copy-start.12
  2.3 0.7 copy-start.9
  3.1 5.7 %copy-start.6 = (f32[32,128]{1,0:T(8,128)S(1)}, f32[32,128]{1,0:T(8,128)}, u32[]{:S(2)}) copy-start(f32[32,128]{1,0:T(8,128)} %param.16) | copy-start | bytes 49156
  3.3 5.6 %copy-start.8 = (f32[32,128]{1,0:T(8,128)S(1)}, f32[32,128]{1,0:T(8,128)}, u32[]{:S(2)}) copy-start(f32[32,128]{1,0:T(8,128)} %param.15) | copy-start | bytes 49156
  3.3 5.6 %copy-start.10 = (s32[32]{0:T(128)S(1)}, s32[32]{0:T(128)}, u32[]{:S(2)}) copy-start(s32[32]{0:T(128)} %param.17) | copy-start | bytes 388
  3.3 17.5 %collective-permute-start.2 = (f32[32,5,128]{2,1,0:T(8,128)S(1)}, f32[32,5,128]{2,1,0:T(8,128)S(1)}, u32[]{:S(2)}, u32[]{:S(2)}) collective-permute-start(f32[32,5,128]{2,1,0:T(8,128)S(1)} %concatenate.23), channel_id=1, source_target_pairs={{0,12},{4,0},{8,4},{12,8},{1,13},{5,1},{9,5},{13,9},{2,14},{6,2},{... | collective-permute-start | bytes 245768 | tf_op jit(solution)/shard_map/ppermute | solution.py:36
  3.8 17.0 %collective-permute-start.1 = (f32[32,5,128]{2,1,0:T(8,128)S(1)}, f32[32,5,128]{2,1,0:T(8,128)S(1)}, u32[]{:S(2)}, u32[]{:S(2)}) collective-permute-start(f32[32,5,128]{2,1,0:T(8,128)S(1)} %concatenate.23), channel_id=1, source_target_pairs={{0,8},{4,12},{8,0},{12,4},{1,9},{5,13},{9,1},{13,5},{2,10},{6,14},... | collective-permute-start | bytes 245768 | tf_op jit(solution)/shard_map/ppermute | solution.py:36
  6.4 14.4 %collective-permute-start = (f32[32,5,128]{2,1,0:T(8,128)S(1)}, f32[32,5,128]{2,1,0:T(8,128)S(1)}, u32[]{:S(2)}, u32[]{:S(2)}) collective-permute-start(f32[32,5,128]{2,1,0:T(8,128)S(1)} %concatenate.23), channel_id=1, source_target_pairs={{0,4},{4,8},{8,12},{12,0},{1,5},{5,9},{9,13},{13,1},{2,6},{6,10},{... | collective-permute-start | bytes 245768 | tf_op jit(solution)/shard_map/ppermute | solution.py:36
  9.6 0.7 copy-start.5
  10.3 9.7 %collective-permute-start.4 = (f32[16,8,128]{2,1,0:T(8,128)S(1)}, f32[16,8,128]{2,1,0:T(8,128)S(1)}, u32[]{:S(2)}, u32[]{:S(2)}) collective-permute-start(f32[16,8,128]{2,1,0:T(8,128)S(1)} %get-tuple-element.9), channel_id=1, source_target_pairs={{4,0},{8,4},{12,8},{0,12},{5,1},{9,5},{13,9},{1,13},{6,2},{10,6},{... | collective-permute-start | bytes 196616 | tf_op jit(solution)/shard_map/ppermute | solution.py:26
  10.4 2.7 %copy-start.15 = (f32[8]{0:T(128)S(1)}, f32[8]{0:T(128)}, u32[]{:S(2)}) copy-start(f32[8]{0:T(128)} %param.24) | copy-start | bytes 100
  10.4 9.7 %collective-permute-start.3 = (f32[16,8,128]{2,1,0:T(8,128)S(1)}, f32[16,8,128]{2,1,0:T(8,128)S(1)}, u32[]{:S(2)}, u32[]{:S(2)}) collective-permute-start(f32[16,8,128]{2,1,0:T(8,128)S(1)} %get-tuple-element.8), channel_id=1, source_target_pairs={{0,4},{4,8},{8,12},{12,0},{1,5},{5,9},{9,13},{13,1},{2,6},{6,10},{... | collective-permute-start | bytes 196616 | tf_op jit(solution)/shard_map/ppermute | solution.py:24
  15.7 0.7 copy-start.13
  17.1 0.8 copy-start.7
  17.9 3.1 %copy-start.1 = (f32[32,8,128]{2,1,0:T(8,128)}, f32[32,8,128]{2,1,0:T(8,128)S(1)}, u32[]{:S(2)}) copy-start(f32[32,8,128]{2,1,0:T(8,128)S(1)} %stack.28.own_ref) | copy-start | bytes 393220
  40.0 5.5 %collective-permute-start.6 = (f32[16,8,128]{2,1,0:T(8,128)S(1)}, f32[16,8,128]{2,1,0:T(8,128)S(1)}, u32[]{:S(2)}, u32[]{:S(2)}) collective-permute-start(f32[16,8,128]{2,1,0:T(8,128)S(1)} %get-tuple-element.7), channel_id=1, source_target_pairs={{4,0},{8,4},{12,8},{0,12},{5,1},{9,5},{13,9},{1,13},{6,2},{10,6},{... | collective-permute-start | bytes 196616 | tf_op jit(solution)/shard_map/ppermute | solution.py:26
  40.1 5.5 %collective-permute-start.5 = (f32[16,8,128]{2,1,0:T(8,128)S(1)}, f32[16,8,128]{2,1,0:T(8,128)S(1)}, u32[]{:S(2)}, u32[]{:S(2)}) collective-permute-start(f32[16,8,128]{2,1,0:T(8,128)S(1)} %get-tuple-element.6), channel_id=1, source_target_pairs={{0,4},{4,8},{8,12},{12,0},{1,5},{5,9},{9,13},{13,1},{2,6},{6,10},{... | collective-permute-start | bytes 196616 | tf_op jit(solution)/shard_map/ppermute | solution.py:24
  43.7 1.9 %copy-start.2 = (f32[32,8,128]{2,1,0:T(8,128)S(1)}, f32[32,8,128]{2,1,0:T(8,128)}, u32[]{:S(2)}) copy-start(f32[32,8,128]{2,1,0:T(8,128)} %shard_map.140) | copy-start | bytes 393220
  62.5 7.7 %collective-permute-start.7 = (f32[32,8,128]{2,1,0:T(8,128)}, f32[32,8,128]{2,1,0:T(8,128)S(1)}, u32[]{:S(2)}, u32[]{:S(2)}) collective-permute-start(f32[32,8,128]{2,1,0:T(8,128)} %shard_map.141), channel_id=1, source_target_pairs={{0,4},{4,8},{8,12},{12,0},{1,5},{5,9},{9,13},{13,1},{2,6},{6,10},{... | collective-permute-start | bytes 393224 | tf_op jit(solution)/shard_map/ppermute | solution.py:36
  64.9 0.9 copy-start.4
  65.8 9.5 %collective-permute-start.8 = (f32[32,8,128]{2,1,0:T(8,128)S(1)}, f32[32,8,128]{2,1,0:T(8,128)S(1)}, u32[]{:S(2)}, u32[]{:S(2)}) collective-permute-start(f32[32,8,128]{2,1,0:T(8,128)S(1)} %copy-done.4), channel_id=1, source_target_pairs={{0,8},{4,12},{8,0},{12,4},{1,9},{5,13},{9,1},{13,5},{2,10},{6,14},... | collective-permute-start | bytes 393224 | tf_op jit(solution)/shard_map/ppermute | solution.py:36
  69.8 8.1 %collective-permute-start.9 = (f32[32,8,128]{2,1,0:T(8,128)S(1)}, f32[32,8,128]{2,1,0:T(8,128)S(1)}, u32[]{:S(2)}, u32[]{:S(2)}) collective-permute-start(f32[32,8,128]{2,1,0:T(8,128)S(1)} %copy-done.4), channel_id=1, source_target_pairs={{0,12},{4,0},{8,4},{12,8},{1,13},{5,1},{9,5},{13,9},{2,14},{6,2},{... | collective-permute-start | bytes 393224 | tf_op jit(solution)/shard_map/ppermute | solution.py:36
  78.0 0.8 copy-start.3
  (4 other events, 2.5 us)
where the time goes:
time: 111 us; the launch traced here: 109 us
  Pallas kernels  62.2 us (56%)
  starting transfers between devices  15.8 us (14%)
  local copies, waits for them, and re-layouts  13 us (12%)
  waiting for transfers between devices  11.5 us (10%)
  other arithmetic  5.26 us (5%)
    pallas_call x2, Pallas kernels, update(): pl.pallas_call(make_update_kernel(margin, tile_scale), out_shape=jax.Shap...  32.3 us
    pallas_call x1, Pallas kernels, grid_stage(): pl.pallas_call(kernel, out_shape=jax.ShapeDtypeStruct((n_own, solves, gpt...  29.9 us
    ppermute x6, starting transfers between devices, gather_slots(): lax.ppermute(x, axis, [(i, (i + s) % count) for i in range(count)])  11.1 us
    ppermute x6, waiting for transfers between devices, gather_slots(): lax.ppermute(x, axis, [(i, (i + s) % count) for i in range(count)])  8.06 us
    unnamed x40, local copies, waits for them, and re-layouts  6.07 us
    ppermute x2, starting transfers between devices, with_halo(): lax.ppermute(tail, axis, [(i, (i + 1) % count) for i in range(count)])  4.54 us
    ppermute x2, waiting for transfers between devices, with_halo(): lax.ppermute(head, axis, [((i + 1) % count, i) for i in range(count)])  3.33 us
  transfers between devices with their start and end apart: 10, of which 7 were waited for; matrix products, arithmetic and copies ran while one was open for 7% of the time, Pallas kernels for 0%

commit v1 on v0

--- a/solution.py
+++ b/solution.py
@@ -62,19 +62,23 @@
 
 def make_update_kernel(margin, tile_scale):
     def update_kernel(
-        cols_ref, own_ref, halo_ref, w_ref, obs_ref, diag_ref, thr_ref, live_ref, step_ref,
-        out_ref, buf0, buf1,
+        base_ref, cols_ref, own_ref, halo_ref, w_ref, obs_ref, diag_ref, thr_ref, live_ref,
+        step_ref, out_ref, buf0, buf1,
     ):
         reg_dev, _, cap = own_ref.shape
+        count = out_ref.shape[0]
         tiles = cols_ref.shape[0] // reg_dev
-
-        def fill(a, buf):
+        base = base_ref[0]
+
+        def fill(i, buf):
+            a = i + base
             own_t = own_ref[a].T
             for t in range(tiles):
                 b = cols_ref[a * tiles + t]
                 buf[:, t * cap : (t + 1) * cap] = corr_block(own_t, halo_ref[b])
 
-        def use(a, buf):
+        def use(i, buf):
+            a = i + base
             weights = jnp.concatenate(
                 [w_ref[cols_ref[a * tiles + t]] for t in range(tiles)], axis=1
             )
@@ -85,7 +89,7 @@
             applied = cov * tile_scale + diag * current
             residual = (obs_ref[a] - applied) * live_ref[a]
             factor = thr / jnp.maximum(jnp.abs(residual), thr)
-            out_ref[a] = current + step_ref[...] * factor * residual / diag
+            out_ref[i] = current + step_ref[...] * factor * residual / diag
 
         fill(0, buf0)
 
@@ -94,26 +98,27 @@
             use(a, buf0)
             fill(a + 1, buf1)
             use(a + 1, buf1)
-            fill(jnp.minimum(a + 2, reg_dev - 1), buf0)
+            fill(jnp.minimum(a + 2, count - 1), buf0)
             return carry
 
-        lax.fori_loop(0, reg_dev // 2, pair, 0)
+        lax.fori_loop(0, count // 2, pair, 0)
 
     return update_kernel
 
 
-def update(cols, own_sites, halo_sites, halo_w, observed, diagonal, threshold, live, step, margin, tile_scale):
+def update(base, count, cols, own_sites, halo_sites, halo_w, observed, diagonal, threshold, live, step, margin, tile_scale):
     reg_dev, _, cap = own_sites.shape
-    assert reg_dev % 2 == 0
+    assert count % 2 == 0
     tiles = cols.shape[0] // reg_dev
     vmem = pl.BlockSpec(memory_space=pltpu.VMEM)
+    smem = pl.BlockSpec(memory_space=pltpu.SMEM)
     return pl.pallas_call(
         make_update_kernel(margin, tile_scale),
-        out_shape=jax.ShapeDtypeStruct(diagonal.shape, jnp.float32),
-        in_specs=[pl.BlockSpec(memory_space=pltpu.SMEM)] + [vmem] * 8,
+        out_shape=jax.ShapeDtypeStruct((count,) + diagonal.shape[1:], jnp.float32),
+        in_specs=[smem, smem] + [vmem] * 8,
         out_specs=vmem,
         scratch_shapes=[pltpu.VMEM((cap, tiles * cap), jnp.float32)] * 2,
-    )(cols, own_sites, halo_sites, halo_w, observed, diagonal, threshold, live, step)
+    )(base, cols, own_sites, halo_sites, halo_w, observed, diagonal, threshold, live, step)
 
 
 def make_grid_kernel(per_slab, reg_dev, n_wide, cap, regions):
@@ -263,18 +268,40 @@
     step = jnp.broadcast_to(step_size[:, None], (solves, capacity))
     local_cols = ((tile_columns - first_row + margin) % regions).reshape(-1)
     tile_scale = 2.0 / (capacity * tile_columns.shape[1])
+    n_slab = lax.axis_size("slab")
+    assert n_slab == 2 and margin * n_slab == reg_dev
+    sidx = lax.axis_index("slab")
+    sub = reg_dev // n_slab
+    base = (sidx * sub).astype(jnp.int32).reshape(1)
+    blocks = n_wide * n_slab
+    pairs = ("wide", "slab")
+    other_pairs = [(b, b ^ 1) for b in range(blocks)]
+    q1_pairs = [(b, (b - 2) % blocks) if b % 2 == 0 else (b, (b + 2) % blocks) for b in range(blocks)]
+    q2_pairs = [(b, (b - 1) % blocks) if b % 2 == 0 else (b, (b + 1) % blocks) for b in range(blocks)]
+    first = sidx == 0
+
+    def own_rows(mine):
+        other = lax.ppermute(mine, pairs, other_pairs)
+        return jnp.where(first, jnp.concatenate([mine, other]), jnp.concatenate([other, mine]))
+
+    weights_wide = with_halo(obs_weights, "wide", margin)
     for sweep_index in range(ITERS):
-        weights_wide = with_halo(obs_weights, "wide", margin)
-        obs_weights = update(
-            local_cols, obs_sites, sites_wide, weights_wide, observed, diagonal, threshold,
-            live, step, margin, tile_scale,
+        mine = update(
+            base, sub, local_cols, obs_sites, sites_wide, weights_wide, observed, diagonal,
+            threshold, live, step, margin, tile_scale,
         )
+        obs_weights = own_rows(mine)
+        if sweep_index + 1 < ITERS:
+            q1 = lax.ppermute(mine, pairs, q1_pairs)
+            q2 = lax.ppermute(mine, pairs, q2_pairs)
+            left = jnp.where(first, q2, q1)
+            right = jnp.where(first, q1, q2)
+            weights_wide = jnp.concatenate([left, obs_weights, right])
     w_slots = jnp.concatenate(
         [gather_slots(obs_weights, "wide"), jnp.zeros((ROWS, solves, capacity), jnp.float32)], axis=0
     )
 
     slab_count = slab_order.shape[0]
-    n_slab = lax.axis_size("slab")
     n_own = slab_count // (n_wide * n_slab)
     pos0 = (me * n_slab + lax.axis_index("slab")) * n_own
     own_slabs = lax.dynamic_slice_in_dim(slab_order, pos0, n_own, 0)

time: 111 us -> 98.2 us (0.88)
  the two profiles are of different devices: /device:TPU:12 before, /device:TPU:0 now
where the time goes in v1:
time: 98.2 us; the launch traced here: 96.6 us
  Pallas kernels  45.9 us (47%)
  starting transfers between devices  19.6 us (20%)
  local copies, waits for them, and re-layouts  12.5 us (13%)
  waiting for transfers between devices  12.3 us (13%)
  other arithmetic  5.3 us (5%)
    pallas_call x1, Pallas kernels, grid_stage(): pl.pallas_call(kernel, out_shape=jax.ShapeDtypeStruct((n_own, solves, gpt...  27.5 us
    pallas_call x2, Pallas kernels, update(): pl.pallas_call(make_update_kernel(margin, tile_scale), out_shape=jax.Shap...  18.4 us
    ppermute x6, starting transfers between devices, gather_slots(): lax.ppermute(x, axis, [(i, (i + s) % count) for i in range(count)])  11.2 us
    ppermute x6, waiting for transfers between devices, gather_slots(): lax.ppermute(x, axis, [(i, (i + s) % count) for i in range(count)])  8.03 us
    unnamed x41, local copies, waits for them, and re-layouts  6.34 us
    ppermute x1, starting transfers between devices, body(): q1 = lax.ppermute(mine, pairs, q1_pairs)  3.2 us
    ppermute x1, starting transfers between devices, with_halo(): lax.ppermute(head, axis, [((i + 1) % count, i) for i in range(count)])  2.87 us
    ppermute x1, starting transfers between devices, body(): q2 = lax.ppermute(mine, pairs, q2_pairs)  2.2 us
  transfers between devices with their start and end apart: 12, of which 9 were waited for; matrix products, arithmetic and copies ran while one was open for 8% of the time, Pallas kernels for 0%

profile of v1, /device:TPU:0, one launch (start us, length us, event | category | flops | bytes accessed | tf_op | source)
XLA Modules:
  0.0 96.6 jit_solution(1932956568214692184)
XLA Ops:
  0.7 0.8 fusion.5
  3.3 5.1 %collective-permute-start.2 = (f32[32,5,128]{2,1,0:T(8,128)S(1)}, f32[32,5,128]{2,1,0:T(8,128)S(1)}, u32[]{:S(2)}, u32[]{:S(2)}) collective-permute-start(f32[32,5,128]{2,1,0:T(8,128)S(1)} %concatenate.35), channel_id=1, source_target_pairs={{0,12},{4,0},{8,4},{12,8},{1,13},{5,1},{9,5},{13,9},{2,14},{6,2},{... | collective-permute-start | bytes 245768 | tf_op jit(solution)/shard_map/ppermute | solution.py:36
  8.4 1.0 %collective-permute-start = (f32[32,5,128]{2,1,0:T(8,128)S(1)}, f32[32,5,128]{2,1,0:T(8,128)S(1)}, u32[]{:S(2)}, u32[]{:S(2)}) collective-permute-start(f32[32,5,128]{2,1,0:T(8,128)S(1)} %concatenate.35), channel_id=1, source_target_pairs={{0,4},{4,8},{8,12},{12,0},{1,5},{5,9},{9,13},{13,1},{2,6},{6,10},{... | collective-permute-start | bytes 245768 | tf_op jit(solution)/shard_map/ppermute | solution.py:36
  10.1 0.7 broadcast_add_fusion
  10.9 2.9 %collective-permute-start.4 = (f32[16,8,128]{2,1,0:T(8,128)S(1)}, f32[16,8,128]{2,1,0:T(8,128)S(1)}, u32[]{:S(2)}, u32[]{:S(2)}) collective-permute-start(f32[16,8,128]{2,1,0:T(8,128)S(1)} %get-tuple-element.11), channel_id=1, source_target_pairs={{4,0},{8,4},{12,8},{0,12},{5,1},{9,5},{13,9},{1,13},{6,2},{10,6},{... | collective-permute-start | bytes 196616 | tf_op jit(solution)/shard_map/ppermute | solution.py:26
  15.8 0.7 broadcast_multiply_fusion.thr_ref
  18.8 1.1 %collective-permute-done.4 = f32[16,8,128]{2,1,0:T(8,128)S(1)} collective-permute-done((f32[16,8,128]{2,1,0:T(8,128)S(1)}, f32[16,8,128]{2,1,0:T(8,128)S(1)}, u32[]{:S(2)}, u32[]{:S(2)}) %collective-permute-start.4) | collective-permute-done | bytes 65568 | tf_op jit(solution)/shard_map/ppermute | solution.py:26
  19.8 0.7 collective-permute-done.3
  20.6 0.7 pad_maximum_fusion.2.w_ref
  21.9 0.7 pad_maximum_fusion.1.halo_ref
  24.0 9.2 %shard_map.140 = f32[16,8,128]{2,1,0:T(8,128)} custom-call(s32[1]{0:T(128)} %bitcast.base_ref, s32[128]{0:T(128)} %reshape.139.cols_ref, f32[32,8,128]{2,1,0:T(8,128)} %copy-done.1, f32[64,8,128]{2,1,0:T(8,128)} %pad_maximum_fusion.1.halo_ref, f32[64,8,128]{2,1,0:T(8,128)} %pad_maximum_fusion.2.w_ref, f32[32,1,128]{2,1,0:T(1,128)} %bitcast.9, ...), custom_call_target="tpu_custom_call" | custom-call | tf_op jit(solution)/shard_map/pallas_call | solution.py:115
  34.0 2.2 %collective-permute-start.5 = (f32[16,8,128]{2,1,0:T(8,128)S(1)}, f32[16,8,128]{2,1,0:T(8,128)S(1)}, u32[]{:S(2)}, u32[]{:S(2)}) collective-permute-start(f32[16,8,128]{2,1,0:T(8,128)S(1)} %copy-done.5), channel_id=1, source_target_pairs={{0,13},{1,4},{4,1},{5,8},{8,5},{9,12},{12,9},{13,0},{2,15},{3,6},{... | collective-permute-start | bytes 196616 | tf_op jit(solution)/shard_map/ppermute | solution.py:296
  36.2 3.2 %collective-permute-start.6 = (f32[16,8,128]{2,1,0:T(8,128)S(1)}, f32[16,8,128]{2,1,0:T(8,128)S(1)}, u32[]{:S(2)}, u32[]{:S(2)}) collective-permute-start(f32[16,8,128]{2,1,0:T(8,128)S(1)} %copy-done.5), channel_id=1, source_target_pairs={{0,12},{1,5},{4,0},{5,9},{8,4},{9,13},{12,8},{13,1},{2,14},{3,7},{... | collective-permute-start | bytes 196616 | tf_op jit(solution)/shard_map/ppermute | solution.py:295
  39.5 1.8 %collective-permute-done.6 = f32[16,8,128]{2,1,0:T(8,128)S(1)} collective-permute-done((f32[16,8,128]{2,1,0:T(8,128)S(1)}, f32[16,8,128]{2,1,0:T(8,128)S(1)}, u32[]{:S(2)}, u32[]{:S(2)}) %collective-permute-start.6) | collective-permute-done | bytes 65568 | tf_op jit(solution)/shard_map/ppermute | solution.py:295
  41.3 0.7 pad_maximum_fusion.3.w_ref
  42.0 9.2 %shard_map.141 = f32[16,8,128]{2,1,0:T(8,128)} custom-call(s32[1]{0:T(128)} %bitcast.base_ref, s32[128]{0:T(128)} %reshape.139.cols_ref, f32[32,8,128]{2,1,0:T(8,128)} %copy-done.1, f32[64,8,128]{2,1,0:T(8,128)} %pad_maximum_fusion.1.halo_ref, f32[64,8,128]{2,1,0:T(8,128)} %pad_maximum_fusion.3.w_ref, f32[32,1,128]{2,1,0:T(1,128)} %bitcast.10, ...), custom_call_target="tpu_custom_call" | custom-call | tf_op jit(solution)/shard_map/pallas_call | solution.py:115
  52.8 0.9 collective-permute-start.9
  54.8 3.9 %collective-permute-start.10 = (f32[32,8,128]{2,1,0:T(8,128)S(1)}, f32[32,8,128]{2,1,0:T(8,128)S(1)}, u32[]{:S(2)}, u32[]{:S(2)}) collective-permute-start(f32[32,8,128]{2,1,0:T(8,128)S(1)} %get-tuple-element.5), channel_id=1, source_target_pairs={{0,8},{4,12},{8,0},{12,4},{1,9},{5,13},{9,1},{13,5},{2,10},{6,14},... | collective-permute-start | bytes 393224 | tf_op jit(solution)/shard_map/ppermute | solution.py:36
  59.7 0.8 concatenate.44.sites_ref
  60.7 0.8 collective-permute-done.9
  61.5 5.1 %collective-permute-done.10 = f32[32,8,128]{2,1,0:T(8,128)S(1)} collective-permute-done((f32[32,8,128]{2,1,0:T(8,128)S(1)}, f32[32,8,128]{2,1,0:T(8,128)S(1)}, u32[]{:S(2)}, u32[]{:S(2)}) %collective-permute-start.10) | collective-permute-done | bytes 131104 | tf_op jit(solution)/shard_map/ppermute | solution.py:36
  66.6 1.7 %collective-permute-done.11 = f32[32,8,128]{2,1,0:T(8,128)S(1)} collective-permute-done((f32[32,8,128]{2,1,0:T(8,128)S(1)}, f32[32,8,128]{2,1,0:T(8,128)S(1)}, u32[]{:S(2)}, u32[]{:S(2)}) %collective-permute-start.11) | collective-permute-done | bytes 131104 | tf_op jit(solution)/shard_map/ppermute | solution.py:36
  68.3 0.8 copy-done.2
  69.1 27.5 %shard_map.142 = f32[4,8,512]{2,1,0:T(8,128)} custom-call(s32[1]{0:T(128)} %bitcast.8.me_ref, s32[4]{0:T(128)} %copy-done.12, s32[512]{0:T(512)} %convert_element_type.40.list_ref, f32[136,8,128]{2,1,0:T(8,128)} %concatenate.44.sites_ref, f32[136,8,128]{2,1,0:T(8,128)} %copy-done.2, f32[4,8,512]{2,1,0:T(8,128)} %stack.30.gsites_ref), custom_call_target="tpu_custom_call" | custom-call | tf_op jit(solution)/shard_map/pallas_call | solution.py:204
  (89 shorter events, 13.3 us)
Async XLA Ops:
  0.6 32.6 %copy-start = (f32[32,512]{1,0:T(8,128)S(1)}, f32[32,512]{1,0:T(8,128)}, u32[]{:S(2)}) copy-start(f32[32,512]{1,0:T(8,128)} %param.21) | copy-start | bytes 196612
  2.3 0.7 copy-start.10
  3.1 6.3 %copy-start.6 = (f32[32,128]{1,0:T(8,128)S(1)}, f32[32,128]{1,0:T(8,128)}, u32[]{:S(2)}) copy-start(f32[32,128]{1,0:T(8,128)} %param.16) | copy-start | bytes 49156
  3.3 6.2 %copy-start.9 = (f32[32,128]{1,0:T(8,128)S(1)}, f32[32,128]{1,0:T(8,128)}, u32[]{:S(2)}) copy-start(f32[32,128]{1,0:T(8,128)} %param.15) | copy-start | bytes 49156
  3.3 6.2 %copy-start.11 = (s32[32]{0:T(128)S(1)}, s32[32]{0:T(128)}, u32[]{:S(2)}) copy-start(s32[32]{0:T(128)} %param.17) | copy-start | bytes 388
  3.3 18.0 %collective-permute-start.2 = (f32[32,5,128]{2,1,0:T(8,128)S(1)}, f32[32,5,128]{2,1,0:T(8,128)S(1)}, u32[]{:S(2)}, u32[]{:S(2)}) collective-permute-start(f32[32,5,128]{2,1,0:T(8,128)S(1)} %concatenate.35), channel_id=1, source_target_pairs={{0,12},{4,0},{8,4},{12,8},{1,13},{5,1},{9,5},{13,9},{2,14},{6,2},{... | collective-permute-start | bytes 245768 | tf_op jit(solution)/shard_map/ppermute | solution.py:36
  8.4 13.4 %collective-permute-start.1 = (f32[32,5,128]{2,1,0:T(8,128)S(1)}, f32[32,5,128]{2,1,0:T(8,128)S(1)}, u32[]{:S(2)}, u32[]{:S(2)}) collective-permute-start(f32[32,5,128]{2,1,0:T(8,128)S(1)} %concatenate.35), channel_id=1, source_target_pairs={{0,8},{4,12},{8,0},{12,4},{1,9},{5,13},{9,1},{13,5},{2,10},{6,14},... | collective-permute-start | bytes 245768 | tf_op jit(solution)/shard_map/ppermute | solution.py:36
  8.4 13.4 %collective-permute-start = (f32[32,5,128]{2,1,0:T(8,128)S(1)}, f32[32,5,128]{2,1,0:T(8,128)S(1)}, u32[]{:S(2)}, u32[]{:S(2)}) collective-permute-start(f32[32,5,128]{2,1,0:T(8,128)S(1)} %concatenate.35), channel_id=1, source_target_pairs={{0,4},{4,8},{8,12},{12,0},{1,5},{5,9},{9,13},{13,1},{2,6},{6,10},{... | collective-permute-start | bytes 245768 | tf_op jit(solution)/shard_map/ppermute | solution.py:36
  10.1 0.7 copy-start.3
  10.9 8.9 %collective-permute-start.4 = (f32[16,8,128]{2,1,0:T(8,128)S(1)}, f32[16,8,128]{2,1,0:T(8,128)S(1)}, u32[]{:S(2)}, u32[]{:S(2)}) collective-permute-start(f32[16,8,128]{2,1,0:T(8,128)S(1)} %get-tuple-element.11), channel_id=1, source_target_pairs={{4,0},{8,4},{12,8},{0,12},{5,1},{9,5},{13,9},{1,13},{6,2},{10,6},{... | collective-permute-start | bytes 196616 | tf_op jit(solution)/shard_map/ppermute | solution.py:26
  13.7 6.8 %collective-permute-start.3 = (f32[16,8,128]{2,1,0:T(8,128)S(1)}, f32[16,8,128]{2,1,0:T(8,128)S(1)}, u32[]{:S(2)}, u32[]{:S(2)}) collective-permute-start(f32[16,8,128]{2,1,0:T(8,128)S(1)} %get-tuple-element.10), channel_id=1, source_target_pairs={{0,4},{4,8},{8,12},{12,0},{1,5},{5,9},{9,13},{13,1},{2,6},{6,10},{... | collective-permute-start | bytes 196616 | tf_op jit(solution)/shard_map/ppermute | solution.py:24
  18.8 3.2 %copy-start.1 = (f32[32,8,128]{2,1,0:T(8,128)}, f32[32,8,128]{2,1,0:T(8,128)S(1)}, u32[]{:S(2)}) copy-start(f32[32,8,128]{2,1,0:T(8,128)S(1)} %stack.28.own_ref) | copy-start | bytes 393220
  33.2 0.8 copy-start.5
  33.2 6.2 %collective-permute-start.7 = (f32[16,8,128]{2,1,0:T(8,128)}, f32[16,8,128]{2,1,0:T(8,128)S(1)}, u32[]{:S(2)}, u32[]{:S(2)}) collective-permute-start(f32[16,8,128]{2,1,0:T(8,128)} %shard_map.140), channel_id=1, source_target_pairs={{0,1},{1,0},{4,5},{5,4},{8,9},{9,8},{12,13},{13,12},{2,3},{3,2},{6... | collective-permute-start | bytes 196616 | tf_op jit(solution)/shard_map/ppermute | solution.py:284
  34.0 5.5 %collective-permute-start.5 = (f32[16,8,128]{2,1,0:T(8,128)S(1)}, f32[16,8,128]{2,1,0:T(8,128)S(1)}, u32[]{:S(2)}, u32[]{:S(2)}) collective-permute-start(f32[16,8,128]{2,1,0:T(8,128)S(1)} %copy-done.5), channel_id=1, source_target_pairs={{0,13},{1,4},{4,1},{5,8},{8,5},{9,12},{12,9},{13,0},{2,15},{3,6},{... | collective-permute-start | bytes 196616 | tf_op jit(solution)/shard_map/ppermute | solution.py:296
  36.2 5.1 %collective-permute-start.6 = (f32[16,8,128]{2,1,0:T(8,128)S(1)}, f32[16,8,128]{2,1,0:T(8,128)S(1)}, u32[]{:S(2)}, u32[]{:S(2)}) collective-permute-start(f32[16,8,128]{2,1,0:T(8,128)S(1)} %copy-done.5), channel_id=1, source_target_pairs={{0,12},{1,5},{4,0},{5,9},{8,4},{9,13},{12,8},{13,1},{2,14},{3,7},{... | collective-permute-start | bytes 196616 | tf_op jit(solution)/shard_map/ppermute | solution.py:295
  42.0 9.5 %copy-start.8 = (f32[32,512]{1,0:T(8,128)S(1)}, f32[32,512]{1,0:T(8,128)}, u32[]{:S(2)}) copy-start(f32[32,512]{1,0:T(8,128)} %param.22) | copy-start | bytes 196612
  51.3 1.5 %copy-start.4 = (f32[16,8,128]{2,1,0:T(8,128)S(1)}, f32[16,8,128]{2,1,0:T(8,128)}, u32[]{:S(2)}) copy-start(f32[16,8,128]{2,1,0:T(8,128)} %shard_map.141) | copy-start | bytes 196612
  51.3 1.5 %collective-permute-start.8 = (f32[16,8,128]{2,1,0:T(8,128)}, f32[16,8,128]{2,1,0:T(8,128)S(1)}, u32[]{:S(2)}, u32[]{:S(2)}) collective-permute-start(f32[16,8,128]{2,1,0:T(8,128)} %shard_map.141), channel_id=1, source_target_pairs={{0,1},{1,0},{4,5},{5,4},{8,9},{9,8},{12,13},{13,12},{2,3},{3,2},{6... | collective-permute-start | bytes 196616 | tf_op jit(solution)/shard_map/ppermute | solution.py:284
  52.8 7.7 %copy-start.7 = (f32[32,8,128]{2,1,0:T(8,128)}, f32[32,8,128]{2,1,0:T(8,128)S(1)}, u32[]{:S(2)}) copy-start(f32[32,8,128]{2,1,0:T(8,128)S(1)} %get-tuple-element.5) | copy-start | bytes 393220
  52.8 8.7 %collective-permute-start.9 = (f32[32,8,128]{2,1,0:T(8,128)S(1)}, f32[32,8,128]{2,1,0:T(8,128)S(1)}, u32[]{:S(2)}, u32[]{:S(2)}) collective-permute-start(f32[32,8,128]{2,1,0:T(8,128)S(1)} %get-tuple-element.5), channel_id=1, source_target_pairs={{0,4},{4,8},{8,12},{12,0},{1,5},{5,9},{9,13},{13,1},{2,6},{6,10},{... | collective-permute-start | bytes 393224 | tf_op jit(solution)/shard_map/ppermute | solution.py:36
  54.8 11.7 %collective-permute-start.10 = (f32[32,8,128]{2,1,0:T(8,128)S(1)}, f32[32,8,128]{2,1,0:T(8,128)S(1)}, u32[]{:S(2)}, u32[]{:S(2)}) collective-permute-start(f32[32,8,128]{2,1,0:T(8,128)S(1)} %get-tuple-element.5), channel_id=1, source_target_pairs={{0,8},{4,12},{8,0},{12,4},{1,9},{5,13},{9,1},{13,5},{2,10},{6,14},... | collective-permute-start | bytes 393224 | tf_op jit(solution)/shard_map/ppermute | solution.py:36
  60.5 7.7 %collective-permute-start.11 = (f32[32,8,128]{2,1,0:T(8,128)S(1)}, f32[32,8,128]{2,1,0:T(8,128)S(1)}, u32[]{:S(2)}, u32[]{:S(2)}) collective-permute-start(f32[32,8,128]{2,1,0:T(8,128)S(1)} %get-tuple-element.5), channel_id=1, source_target_pairs={{0,12},{4,0},{8,4},{12,8},{1,13},{5,1},{9,5},{13,9},{2,14},{6,2},{... | collective-permute-start | bytes 393224 | tf_op jit(solution)/shard_map/ppermute | solution.py:36
  68.2 0.8 copy-start.2
  (7 other events, 4.6 us)

commit v2 on v1

--- a/solution.py
+++ b/solution.py
@@ -121,7 +121,7 @@
     )(base, cols, own_sites, halo_sites, halo_w, observed, diagonal, threshold, live, step)
 
 
-def make_grid_kernel(per_slab, reg_dev, n_wide, cap, regions):
+def make_grid_kernel(per_slab, reg_dev, n_wide, cap, regions, n_split):
     window = (2 * SLAB_REACH + 1) * per_slab
 
     def grid_kernel(
@@ -131,6 +131,7 @@
         n_own = out_ref.shape[0]
         gpr = list_ref.shape[0] // regions
         me = me_ref[0]
+        part = me_ref[1]
         total = jnp.int32(0)
         for j in range(n_own):
             slab = own_slabs_ref[j]
@@ -158,20 +159,28 @@
 
             lax.fori_loop(first_group, total // GROUP, mark, 0)
         n_groups = total // GROUP
-        for e in range(GROUP):
-            sel_ref[total + e] = regions
-        slab_ref[n_groups] = 0
-        n_pairs = (n_groups + 1) // 2
-        last = 2 * n_pairs - 1
+        step = 2 * n_split
+        padded = jnp.maximum((n_groups + step - 1) // step * step, step)
+
+        def pad(g, carry):
+            for e in range(GROUP):
+                sel_ref[g * GROUP + e] = regions
+            slab_ref[g] = 0
+            return carry
+
+        lax.fori_loop(n_groups, padded, pad, 0)
+        n_local = padded // n_split
         out_ref[...] = jnp.zeros(out_ref.shape, jnp.float32)
 
-        def fill(g, buf):
+        def fill(l, buf):
+            g = l * n_split + part
             g_t = gsites_ref[slab_ref[g]].T
             for e in range(GROUP):
                 slot = sel_ref[g * GROUP + e]
                 buf[:, e * cap : (e + 1) * cap] = corr_block(g_t, sites_ref[slot])
 
-        def use(g, buf):
+        def use(l, buf):
+            g = l * n_split + part
             j = slab_ref[g]
             weights = jnp.concatenate(
                 [w_ref[sel_ref[g * GROUP + e]] for e in range(GROUP)], axis=1
@@ -181,38 +190,44 @@
         fill(0, buf0)
 
         def pair(i, carry):
-            g = 2 * i
-            use(g, buf0)
-            fill(g + 1, buf1)
-            use(g + 1, buf1)
-            fill(jnp.minimum(g + 2, last), buf0)
+            l = 2 * i
+            use(l, buf0)
+            fill(l + 1, buf1)
+            use(l + 1, buf1)
+            fill(jnp.minimum(l + 2, n_local - 1), buf0)
             return carry
 
-        lax.fori_loop(0, n_pairs, pair, 0)
+        lax.fori_loop(0, n_local // 2, pair, 0)
         out_ref[...] = out_ref[...] / cap
 
     return grid_kernel, window
 
 
-def grid_stage(me, own_slabs, list_slots, site_slots, w_slots, gsites, reg_dev, n_wide, regions, slab_count):
+def grid_stage(me, own_slabs, list_slots, site_slots, w_slots, gsites, reg_dev, n_wide, regions, slab_count, n_split):
     solves, cap = w_slots.shape[1:]
     n_own, _, gpts = gsites.shape
-    kernel, window = make_grid_kernel(regions // slab_count, reg_dev, n_wide, cap, regions)
+    kernel, window = make_grid_kernel(regions // slab_count, reg_dev, n_wide, cap, regions, n_split)
     vmem = pl.BlockSpec(memory_space=pltpu.VMEM)
     smem = pl.BlockSpec(memory_space=pltpu.SMEM)
-    sel_len = n_own * (window + GROUP) + 2 * GROUP
+    max_groups = n_own * (window // GROUP + 1) + 4 * n_split
     return pl.pallas_call(
         kernel,
         out_shape=jax.ShapeDtypeStruct((n_own, solves, gpts), jnp.float32),
         in_specs=[smem, smem, smem, vmem, vmem, vmem],
         out_specs=vmem,
         scratch_shapes=[
-            pltpu.SMEM((sel_len,), jnp.int32),
-            pltpu.SMEM((sel_len // GROUP + 2,), jnp.int32),
+            pltpu.SMEM((max_groups * GROUP,), jnp.int32),
+            pltpu.SMEM((max_groups,), jnp.int32),
             pltpu.VMEM((gpts, GROUP * cap), jnp.float32),
             pltpu.VMEM((gpts, GROUP * cap), jnp.float32),
         ],
     )(me, own_slabs, list_slots, site_slots, w_slots, gsites)
+
+
+def to_canonical(slots, axis, count):
+    me = lax.axis_index(axis)
+    idx = lax.rem(me - jnp.arange(count, dtype=jnp.int32) + count, count)
+    return jnp.take(slots, idx, axis=0)
 
 
 def body(
@@ -285,20 +300,30 @@
         return jnp.where(first, jnp.concatenate([mine, other]), jnp.concatenate([other, mine]))
 
     weights_wide = with_halo(obs_weights, "wide", margin)
+    n_split = lax.axis_size("narrow")
+    solves = obs_weights.shape[1]
     for sweep_index in range(ITERS):
         mine = update(
             base, sub, local_cols, obs_sites, sites_wide, weights_wide, observed, diagonal,
             threshold, live, step, margin, tile_scale,
         )
-        obs_weights = own_rows(mine)
         if sweep_index + 1 < ITERS:
+            obs_weights = own_rows(mine)
             q1 = lax.ppermute(mine, pairs, q1_pairs)
             q2 = lax.ppermute(mine, pairs, q2_pairs)
             left = jnp.where(first, q2, q1)
             right = jnp.where(first, q1, q2)
             weights_wide = jnp.concatenate([left, obs_weights, right])
+    spread = ("narrow", "slab")
+    pieces = to_canonical(gather_slots(mine[None], spread), spread, n_split * n_slab)
+    pieces = pieces.reshape((n_split, n_slab * sub, solves, capacity))
+    obs_weights = pieces[lax.axis_index("narrow")]
+    all_solves = jnp.transpose(pieces, (1, 0, 2, 3)).reshape(
+        (reg_dev, n_split * solves, capacity)
+    )
     w_slots = jnp.concatenate(
-        [gather_slots(obs_weights, "wide"), jnp.zeros((ROWS, solves, capacity), jnp.float32)], axis=0
+        [gather_slots(all_solves, "wide"), jnp.zeros((ROWS, n_split * solves, capacity), jnp.float32)],
+        axis=0,
     )
 
     slab_count = slab_order.shape[0]
@@ -308,8 +333,9 @@
     g_lat = grid_latitude[own_slabs]
     g_lon = FULL_TURN * (own_slabs[:, None].astype(jnp.float32) + grid_offset[own_slabs]) / slab_count
     gsites = unit_rows(g_lat, g_lon)
-    grid_increment = grid_stage(
-        me.astype(jnp.int32).reshape(1),
+    nidx = lax.axis_index("narrow")
+    partial = grid_stage(
+        jnp.stack([me, nidx]).astype(jnp.int32),
         own_slabs,
         list_slots,
         site_slots,
@@ -319,7 +345,15 @@
         n_wide,
         regions,
         slab_count,
-    )
+        n_split,
+    )
+    chunks = partial.reshape((n_own, n_split, solves, -1))
+    grid_increment = lax.dynamic_index_in_dim(chunks, nidx, axis=1, keepdims=False)
+    for s in range(1, n_split):
+        send = lax.dynamic_index_in_dim(chunks, lax.rem(nidx + s, n_split), axis=1, keepdims=False)
+        grid_increment = grid_increment + lax.ppermute(
+            send, "narrow", [(i, (i + s) % n_split) for i in range(n_split)]
+        )
     return (obs_weights, grid_increment)
 
 

time: 98.2 us -> 108 us (1.100)
  the two profiles are of different devices: /device:TPU:0 before, /device:TPU:8 now
where the time goes in v2:
time: 108 us
  Pallas kernels  36.9 us (34%)
  waiting for transfers between devices  28.6 us (26%)
  starting transfers between devices  18.5 us (17%)
  other arithmetic  13.5 us (12%)
  local copies, waits for them, and re-layouts  9.41 us (9%)
    ppermute x9, waiting for transfers between devices, gather_slots(): lax.ppermute(x, axis, [(i, (i + s) % count) for i in range(count)])  20.8 us
    pallas_call x1, Pallas kernels, grid_stage(): pl.pallas_call(kernel, out_shape=jax.ShapeDtypeStruct((n_own, solves, gpt...  18.5 us
    pallas_call x2, Pallas kernels, update(): pl.pallas_call(make_update_kernel(margin, tile_scale), out_shape=jax.Shap...  18.4 us
    ppermute x9, starting transfers between devices, gather_slots(): lax.ppermute(x, axis, [(i, (i + s) % count) for i in range(count)])  12.7 us
    ppermute x1, waiting for transfers between devices, body(): q1 = lax.ppermute(mine, pairs, q1_pairs)  3.1 us
    ppermute x1, waiting for transfers between devices, body(): lax.ppermute(send, 'narrow', [(i, (i + s) % n_split) for i in range(n_spl...  2.53 us
  transfers between devices with their start and end apart: 15, of which 11 were waited for; matrix products, arithmetic and copies ran while one was open for 12% of the time, Pallas kernels for 0%

profile of v2, /device:TPU:8, one launch (start us, length us, event | category | flops | bytes accessed | tf_op | source)
XLA Modules:
  0.0 107.8 jit_solution(3797607204371089512)
XLA Ops:
  3.4 3.0 %collective-permute-start.1 = (f32[32,5,128]{2,1,0:T(8,128)S(1)}, f32[32,5,128]{2,1,0:T(8,128)S(1)}, u32[]{:S(2)}, u32[]{:S(2)}) collective-permute-start(f32[32,5,128]{2,1,0:T(8,128)S(1)} %concatenate.32), channel_id=1, source_target_pairs={{0,8},{4,12},{8,0},{12,4},{1,9},{5,13},{9,1},{13,5},{2,10},{6,14},... | collective-permute-start | bytes 245768 | tf_op jit(solution)/shard_map/ppermute | solution.py:36
  6.4 2.5 %collective-permute-start = (f32[32,5,128]{2,1,0:T(8,128)S(1)}, f32[32,5,128]{2,1,0:T(8,128)S(1)}, u32[]{:S(2)}, u32[]{:S(2)}) collective-permute-start(f32[32,5,128]{2,1,0:T(8,128)S(1)} %concatenate.32), channel_id=1, source_target_pairs={{0,4},{4,8},{8,12},{12,0},{1,5},{5,9},{9,13},{13,1},{2,6},{6,10},{... | collective-permute-start | bytes 245768 | tf_op jit(solution)/shard_map/ppermute | solution.py:36
  10.5 1.4 %broadcast_add_fusion = (f32[32,8,128]{2,1,0:T(8,128)}, f32[32,8,128]{2,1,0:T(8,128)S(1)}) fusion(f32[8]{0:T(128)} %param.23, f32[32,128]{1,0:T(8,128)S(1)} %mul.70, f32[32,128]{1,0:T(8,128)S(1)} %fusion.1), kind=kLoop, calls=%fused_computation.18 | loop fusion | flops 65536 | bytes 294944 | tf_op jit(solution)/shard_map/add | solution.py:278
  12.0 2.0 %collective-permute-start.3 = (f32[16,8,128]{2,1,0:T(8,128)S(1)}, f32[16,8,128]{2,1,0:T(8,128)S(1)}, u32[]{:S(2)}, u32[]{:S(2)}) collective-permute-start(f32[16,8,128]{2,1,0:T(8,128)S(1)} %get-tuple-element.10), channel_id=1, source_target_pairs={{0,4},{4,8},{8,12},{12,0},{1,5},{5,9},{9,13},{13,1},{2,6},{6,10},{... | collective-permute-start | bytes 196616 | tf_op jit(solution)/shard_map/ppermute | solution.py:24
  14.0 1.4 %compare_convert_fusion.live_ref = f32[32,1,128]{2,1,0:T(1,128)} fusion(s32[32]{0:T(128)} %param.17), kind=kLoop, calls=%fused_computation.20 | loop fusion | flops 8192 | bytes 16512 | tf_op jit(solution)/shard_map/convert_element_type | solution.py:274
  18.4 1.6 %collective-permute-done.4 = f32[16,8,128]{2,1,0:T(8,128)S(1)} collective-permute-done((f32[16,8,128]{2,1,0:T(8,128)S(1)}, f32[16,8,128]{2,1,0:T(8,128)S(1)}, u32[]{:S(2)}, u32[]{:S(2)}) %collective-permute-start.4) | collective-permute-done | bytes 65568 | tf_op jit(solution)/shard_map/ppermute | solution.py:26
  22.4 9.2 %shard_map.140 = f32[16,8,128]{2,1,0:T(8,128)} custom-call(s32[1]{0:T(128)} %bitcast.1.base_ref, s32[128]{0:T(128)} %reshape.190.cols_ref, f32[32,8,128]{2,1,0:T(8,128)} %copy-done.1, f32[64,8,128]{2,1,0:T(8,128)} %pad_maximum_fusion.1.halo_ref, f32[64,8,128]{2,1,0:T(8,128)} %pad_maximum_fusion.2.w_ref, f32[32,1,128]{2,1,0:T(1,128)} %bitcast.36, ...), custom_call_target="tpu_custom_call" | custom-call | tf_op jit(solution)/shard_map/pallas_call | solution.py:115
  32.4 1.8 %collective-permute-start.6 = (f32[16,8,128]{2,1,0:T(8,128)}, f32[16,8,128]{2,1,0:T(8,128)S(1)}, u32[]{:S(2)}, u32[]{:S(2)}) collective-permute-start(f32[16,8,128]{2,1,0:T(8,128)} %shard_map.140), channel_id=1, source_target_pairs={{0,12},{1,5},{4,0},{5,9},{8,4},{9,13},{12,8},{13,1},{2,14},{3,7},{... | collective-permute-start | bytes 196616 | tf_op jit(solution)/shard_map/ppermute | solution.py:312
  34.3 0.9 maximum_select_fusion
  35.6 3.1 %collective-permute-done.6 = f32[16,8,128]{2,1,0:T(8,128)S(1)} collective-permute-done((f32[16,8,128]{2,1,0:T(8,128)}, f32[16,8,128]{2,1,0:T(8,128)S(1)}, u32[]{:S(2)}, u32[]{:S(2)}) %collective-permute-start.6) | collective-permute-done | bytes 65568 | tf_op jit(solution)/shard_map/ppermute | solution.py:312
  39.4 9.2 %shard_map.141 = f32[16,8,128]{2,1,0:T(8,128)} custom-call(s32[1]{0:T(128)} %bitcast.1.base_ref, s32[128]{0:T(128)} %reshape.190.cols_ref, f32[32,8,128]{2,1,0:T(8,128)} %copy-done.1, f32[64,8,128]{2,1,0:T(8,128)} %pad_maximum_fusion.1.halo_ref, f32[64,8,128]{2,1,0:T(8,128)} %pad_maximum_fusion.3.w_ref, f32[32,1,128]{2,1,0:T(1,128)} %bitcast.37, ...), custom_call_target="tpu_custom_call" | custom-call | tf_op jit(solution)/shard_map/pallas_call | solution.py:115
  48.8 1.3 %collective-permute-start.9 = (f32[1,16,8,128]{3,2,1,0:T(8,128)}, f32[1,16,8,128]{3,2,1,0:T(8,128)S(1)}, u32[]{:S(2)}, u32[]{:S(2)}) collective-permute-start(f32[1,16,8,128]{3,2,1,0:T(8,128)} %bitcast.39), channel_id=1, source_target_pairs={{0,2},{1,3},{2,0},{3,1},{4,6},{5,7},{6,4},{7,5},{8,10},{9,11},{10,... | collective-permute-start | bytes 196616 | tf_op jit(solution)/shard_map/ppermute | solution.py:36
  51.0 3.5 %collective-permute-done.9 = f32[1,16,8,128]{3,2,1,0:T(8,128)S(1)} collective-permute-done((f32[1,16,8,128]{3,2,1,0:T(8,128)}, f32[1,16,8,128]{3,2,1,0:T(8,128)S(1)}, u32[]{:S(2)}, u32[]{:S(2)}) %collective-permute-start.9) | collective-permute-done | bytes 65568 | tf_op jit(solution)/shard_map/ppermute | solution.py:36
  56.2 1.1 %collective-permute-start.11 = (f32[32,16,128]{2,1,0:T(8,128)S(1)}, f32[32,16,128]{2,1,0:T(8,128)S(1)}, u32[]{:S(2)}, u32[]{:S(2)}) collective-permute-start(f32[32,16,128]{2,1,0:T(8,128)S(1)} %bitcast.31), channel_id=1, source_target_pairs={{0,4},{4,8},{8,12},{12,0},{1,5},{5,9},{9,13},{13,1},{2,6},{6,10},{... | collective-permute-start | bytes 786440 | tf_op jit(solution)/shard_map/ppermute | solution.py:36
  57.4 2.3 %collective-permute-start.12 = (f32[32,16,128]{2,1,0:T(8,128)S(1)}, f32[32,16,128]{2,1,0:T(8,128)S(1)}, u32[]{:S(2)}, u32[]{:S(2)}) collective-permute-start(f32[32,16,128]{2,1,0:T(8,128)S(1)} %bitcast.32), channel_id=1, source_target_pairs={{0,8},{4,12},{8,0},{12,4},{1,9},{5,13},{9,1},{13,5},{2,10},{6,14},... | collective-permute-start | bytes 786440 | tf_op jit(solution)/shard_map/ppermute | solution.py:36
  61.4 2.0 %collective-permute-start.13 = (f32[32,16,128]{2,1,0:T(8,128)S(1)}, f32[32,16,128]{2,1,0:T(8,128)S(1)}, u32[]{:S(2)}, u32[]{:S(2)}) collective-permute-start(f32[32,16,128]{2,1,0:T(8,128)S(1)} %bitcast.33), channel_id=1, source_target_pairs={{0,12},{4,0},{8,4},{12,8},{1,13},{5,1},{9,5},{13,9},{2,14},{6,2},{... | collective-permute-start | bytes 786440 | tf_op jit(solution)/shard_map/ppermute | solution.py:36
  65.2 10.1 %collective-permute-done.11 = f32[32,16,128]{2,1,0:T(8,128)S(1)} collective-permute-done((f32[32,16,128]{2,1,0:T(8,128)S(1)}, f32[32,16,128]{2,1,0:T(8,128)S(1)}, u32[]{:S(2)}, u32[]{:S(2)}) %collective-permute-start.11) | collective-permute-done | bytes 262176 | tf_op jit(solution)/shard_map/ppermute | solution.py:36
  75.3 3.8 %collective-permute-done.12 = f32[32,16,128]{2,1,0:T(8,128)S(1)} collective-permute-done((f32[32,16,128]{2,1,0:T(8,128)S(1)}, f32[32,16,128]{2,1,0:T(8,128)S(1)}, u32[]{:S(2)}, u32[]{:S(2)}) %collective-permute-start.12) | collective-permute-done | bytes 262176 | tf_op jit(solution)/shard_map/ppermute | solution.py:36
  79.2 2.5 %collective-permute-done.13 = f32[32,16,128]{2,1,0:T(8,128)S(1)} collective-permute-done((f32[32,16,128]{2,1,0:T(8,128)S(1)}, f32[32,16,128]{2,1,0:T(8,128)S(1)}, u32[]{:S(2)}, u32[]{:S(2)}) %collective-permute-start.13) | collective-permute-done | bytes 262176 | tf_op jit(solution)/shard_map/ppermute | solution.py:36
  81.8 1.0 copy-done.2
  82.8 18.5 %shard_map.142 = f32[4,16,512]{2,1,0:T(8,128)} custom-call(s32[2]{0:T(128)} %pad_add_fusion.me_ref, s32[4]{0:T(128)} %copy-done.7, s32[512]{0:T(512)} %convert_element_type.40.list_ref, f32[136,8,128]{2,1,0:T(8,128)} %concatenate.40.sites_ref, f32[136,16,128]{2,1,0:T(8,128)} %copy-done.2, f32[4,8,512]{2,1,0:T(8,128)} %stack.42.gsites_ref), custom_call_target="tpu_custom_call" | custom-call | tf_op jit(solution)/shard_map/pallas_call | solution.py:213
  102.1 1.1 collective-permute-start.14
  103.8 2.5 %collective-permute-done.14 = f32[4,8,512]{2,1,0:T(8,128)S(1)} collective-permute-done((f32[4,8,512]{2,1,0:T(8,128)S(1)}, f32[4,8,512]{2,1,0:T(8,128)S(1)}, u32[]{:S(2)}, u32[]{:S(2)}) %collective-permute-start.14) | collective-permute-done | bytes 65568 | tf_op jit(solution)/shard_map/ppermute | solution.py:354
  106.4 1.5 %bitcast_add_fusion = f32[4,8,512]{2,1,0:T(8,128)} fusion(f32[4,8,512]{2,1,0:T(8,128)S(1)} %collective-permute-done.14, f32[4,2,8,512]{3,2,1,0:T(8,128)} %bitcast.35, s32[]{:T(128)S(6)} %select_n.73), kind=kLoop, calls=%fused_computation.15 | loop fusion | flops 16384 | bytes 196612 | tf_op jit(solution)/shard_map/add | solution.py:354
  (90 shorter events, 19.5 us)
Async XLA Ops:
  0.6 15.6 %copy-start = (f32[32,512]{1,0:T(8,128)S(1)}, f32[32,512]{1,0:T(8,128)}, u32[]{:S(2)}) copy-start(f32[32,512]{1,0:T(8,128)} %param.21) | copy-start | bytes 196612
  0.6 14.7 %copy-start.4 = (f32[32,128]{1,0:T(8,128)S(1)}, f32[32,128]{1,0:T(8,128)}, u32[]{:S(2)}) copy-start(f32[32,128]{1,0:T(8,128)} %param.16) | copy-start | bytes 49156
  0.7 14.7 %copy-start.6 = (s32[32,4]{0,1:T(4,128)S(1)}, s32[32,4]{0,1:T(4,128)}, u32[]{:S(2)}) copy-start(s32[32,4]{0,1:T(4,128)} %param.18) | copy-start | bytes 1540
  0.7 14.7 %copy-start.8 = (f32[8]{0:T(128)S(1)}, f32[8]{0:T(128)}, u32[]{:S(2)}) copy-start(f32[8]{0:T(128)} %param.24) | copy-start | bytes 100
  0.7 15.4 %copy-start.10 = (s32[32]{0:T(128)S(1)}, s32[32]{0:T(128)}, u32[]{:S(2)}) copy-start(s32[32]{0:T(128)} %param.20) | copy-start | bytes 388
  0.7 17.2 %copy-start.5 = (f32[32,512]{1,0:T(8,128)S(1)}, f32[32,512]{1,0:T(8,128)}, u32[]{:S(2)}) copy-start(f32[32,512]{1,0:T(8,128)} %param.22) | copy-start | bytes 196612
  3.3 17.5 %collective-permute-start.2 = (f32[32,5,128]{2,1,0:T(8,128)S(1)}, f32[32,5,128]{2,1,0:T(8,128)S(1)}, u32[]{:S(2)}, u32[]{:S(2)}) collective-permute-start(f32[32,5,128]{2,1,0:T(8,128)S(1)} %concatenate.32), channel_id=1, source_target_pairs={{0,12},{4,0},{8,4},{12,8},{1,13},{5,1},{9,5},{13,9},{2,14},{6,2},{... | collective-permute-start | bytes 245768 | tf_op jit(solution)/shard_map/ppermute | solution.py:36
  3.4 17.5 %collective-permute-start.1 = (f32[32,5,128]{2,1,0:T(8,128)S(1)}, f32[32,5,128]{2,1,0:T(8,128)S(1)}, u32[]{:S(2)}, u32[]{:S(2)}) collective-permute-start(f32[32,5,128]{2,1,0:T(8,128)S(1)} %concatenate.32), channel_id=1, source_target_pairs={{0,8},{4,12},{8,0},{12,4},{1,9},{5,13},{9,1},{13,5},{2,10},{6,14},... | collective-permute-start | bytes 245768 | tf_op jit(solution)/shard_map/ppermute | solution.py:36
  6.4 14.4 %collective-permute-start = (f32[32,5,128]{2,1,0:T(8,128)S(1)}, f32[32,5,128]{2,1,0:T(8,128)S(1)}, u32[]{:S(2)}, u32[]{:S(2)}) collective-permute-start(f32[32,5,128]{2,1,0:T(8,128)S(1)} %concatenate.32), channel_id=1, source_target_pairs={{0,4},{4,8},{8,12},{12,0},{1,5},{5,9},{9,13},{13,1},{2,6},{6,10},{... | collective-permute-start | bytes 245768 | tf_op jit(solution)/shard_map/ppermute | solution.py:36
  10.5 10.5 %copy-start.3 = (f32[32,128]{1,0:T(8,128)}, f32[32,128]{1,0:T(8,128)S(1)}, u32[]{:S(2)}) copy-start(f32[32,128]{1,0:T(8,128)S(1)} %fusion.1) | copy-start | bytes 49156
  11.9 8.2 %collective-permute-start.4 = (f32[16,8,128]{2,1,0:T(8,128)S(1)}, f32[16,8,128]{2,1,0:T(8,128)S(1)}, u32[]{:S(2)}, u32[]{:S(2)}) collective-permute-start(f32[16,8,128]{2,1,0:T(8,128)S(1)} %get-tuple-element.11), channel_id=1, source_target_pairs={{4,0},{8,4},{12,8},{0,12},{5,1},{9,5},{13,9},{1,13},{6,2},{10,6},{... | collective-permute-start | bytes 196616 | tf_op jit(solution)/shard_map/ppermute | solution.py:26
  12.0 8.2 %collective-permute-start.3 = (f32[16,8,128]{2,1,0:T(8,128)S(1)}, f32[16,8,128]{2,1,0:T(8,128)S(1)}, u32[]{:S(2)}, u32[]{:S(2)}) collective-permute-start(f32[16,8,128]{2,1,0:T(8,128)S(1)} %get-tuple-element.10), channel_id=1, source_target_pairs={{0,4},{4,8},{8,12},{12,0},{1,5},{5,9},{9,13},{13,1},{2,6},{6,10},{... | collective-permute-start | bytes 196616 | tf_op jit(solution)/shard_map/ppermute | solution.py:24
  16.2 4.8 %copy-start.7 = (s32[4]{0:T(128)}, s32[4]{0:T(128)S(1)}, u32[]{:S(2)}) copy-start(s32[4]{0:T(128)S(1)} %get-tuple-element.3.own_slabs_ref) | copy-start | bytes 52
  17.9 3.2 %copy-start.1 = (f32[32,8,128]{2,1,0:T(8,128)}, f32[32,8,128]{2,1,0:T(8,128)S(1)}, u32[]{:S(2)}) copy-start(f32[32,8,128]{2,1,0:T(8,128)S(1)} %stack.37.own_ref) | copy-start | bytes 393220
  31.6 2.7 %collective-permute-start.7 = (f32[16,8,128]{2,1,0:T(8,128)}, f32[16,8,128]{2,1,0:T(8,128)S(1)}, u32[]{:S(2)}, u32[]{:S(2)}) collective-permute-start(f32[16,8,128]{2,1,0:T(8,128)} %shard_map.140), channel_id=1, source_target_pairs={{0,1},{1,0},{4,5},{5,4},{8,9},{9,8},{12,13},{13,12},{2,3},{3,2},{6... | collective-permute-start | bytes 196616 | tf_op jit(solution)/shard_map/ppermute | solution.py:299
  31.6 4.0 %collective-permute-start.5 = (f32[16,8,128]{2,1,0:T(8,128)}, f32[16,8,128]{2,1,0:T(8,128)S(1)}, u32[]{:S(2)}, u32[]{:S(2)}) collective-permute-start(f32[16,8,128]{2,1,0:T(8,128)} %shard_map.140), channel_id=1, source_target_pairs={{0,13},{1,4},{4,1},{5,8},{8,5},{9,12},{12,9},{13,0},{2,15},{3,6},{... | collective-permute-start | bytes 196616 | tf_op jit(solution)/shard_map/ppermute | solution.py:313
  32.4 6.2 %collective-permute-start.6 = (f32[16,8,128]{2,1,0:T(8,128)}, f32[16,8,128]{2,1,0:T(8,128)S(1)}, u32[]{:S(2)}, u32[]{:S(2)}) collective-permute-start(f32[16,8,128]{2,1,0:T(8,128)} %shard_map.140), channel_id=1, source_target_pairs={{0,12},{1,5},{4,0},{5,9},{8,4},{9,13},{12,8},{13,1},{2,14},{3,7},{... | collective-permute-start | bytes 196616 | tf_op jit(solution)/shard_map/ppermute | solution.py:312
  48.6 2.4 %collective-permute-start.10 = (f32[1,16,8,128]{3,2,1,0:T(8,128)}, f32[1,16,8,128]{3,2,1,0:T(8,128)S(1)}, u32[]{:S(2)}, u32[]{:S(2)}) collective-permute-start(f32[1,16,8,128]{3,2,1,0:T(8,128)} %bitcast.38), channel_id=1, source_target_pairs={{0,3},{1,0},{2,1},{3,2},{4,7},{5,4},{6,5},{7,6},{8,11},{9,8},{10,9... | collective-permute-start | bytes 196616 | tf_op jit(solution)/shard_map/ppermute | solution.py:36
  48.8 5.8 %collective-permute-start.9 = (f32[1,16,8,128]{3,2,1,0:T(8,128)}, f32[1,16,8,128]{3,2,1,0:T(8,128)S(1)}, u32[]{:S(2)}, u32[]{:S(2)}) collective-permute-start(f32[1,16,8,128]{3,2,1,0:T(8,128)} %bitcast.39), channel_id=1, source_target_pairs={{0,2},{1,3},{2,0},{3,1},{4,6},{5,7},{6,4},{7,5},{8,10},{9,11},{10,... | collective-permute-start | bytes 196616 | tf_op jit(solution)/shard_map/ppermute | solution.py:36
  50.1 4.6 %collective-permute-start.8 = (f32[1,16,8,128]{3,2,1,0:T(8,128)}, f32[1,16,8,128]{3,2,1,0:T(8,128)S(1)}, u32[]{:S(2)}, u32[]{:S(2)}) collective-permute-start(f32[1,16,8,128]{3,2,1,0:T(8,128)} %bitcast.40), channel_id=1, source_target_pairs={{0,1},{1,2},{2,3},{3,0},{4,5},{5,6},{6,7},{7,4},{8,9},{9,10},{10,1... | collective-permute-start | bytes 196616 | tf_op jit(solution)/shard_map/ppermute | solution.py:36
  56.2 19.1 %collective-permute-start.11 = (f32[32,16,128]{2,1,0:T(8,128)S(1)}, f32[32,16,128]{2,1,0:T(8,128)S(1)}, u32[]{:S(2)}, u32[]{:S(2)}) collective-permute-start(f32[32,16,128]{2,1,0:T(8,128)S(1)} %bitcast.31), channel_id=1, source_target_pairs={{0,4},{4,8},{8,12},{12,0},{1,5},{5,9},{9,13},{13,1},{2,6},{6,10},{... | collective-permute-start | bytes 786440 | tf_op jit(solution)/shard_map/ppermute | solution.py:36
  57.4 21.8 %collective-permute-start.12 = (f32[32,16,128]{2,1,0:T(8,128)S(1)}, f32[32,16,128]{2,1,0:T(8,128)S(1)}, u32[]{:S(2)}, u32[]{:S(2)}) collective-permute-start(f32[32,16,128]{2,1,0:T(8,128)S(1)} %bitcast.32), channel_id=1, source_target_pairs={{0,8},{4,12},{8,0},{12,4},{1,9},{5,13},{9,1},{13,5},{2,10},{6,14},... | collective-permute-start | bytes 786440 | tf_op jit(solution)/shard_map/ppermute | solution.py:36
  61.4 20.3 %collective-permute-start.13 = (f32[32,16,128]{2,1,0:T(8,128)S(1)}, f32[32,16,128]{2,1,0:T(8,128)S(1)}, u32[]{:S(2)}, u32[]{:S(2)}) collective-permute-start(f32[32,16,128]{2,1,0:T(8,128)S(1)} %bitcast.33), channel_id=1, source_target_pairs={{0,12},{4,0},{8,4},{12,8},{1,13},{5,1},{9,5},{13,9},{2,14},{6,2},{... | collective-permute-start | bytes 786440 | tf_op jit(solution)/shard_map/ppermute | solution.py:36
  102.1 4.3 %collective-permute-start.14 = (f32[4,8,512]{2,1,0:T(8,128)S(1)}, f32[4,8,512]{2,1,0:T(8,128)S(1)}, u32[]{:S(2)}, u32[]{:S(2)}) collective-permute-start(f32[4,8,512]{2,1,0:T(8,128)S(1)} %dynamic-slice_bitcast_fusion.1), channel_id=1, source_target_pairs={{0,2},{2,0},{1,3},{3,1},{4,6},{6,4},{5,7},{7,5},{8,10},{10,8},{9,1... | collective-permute-start | bytes 196616 | tf_op jit(solution)/shard_map/ppermute | solution.py:354
  (2 other events, 1.9 us)

commit v3 on v1

--- a/solution.py
+++ b/solution.py
@@ -240,34 +240,6 @@
     obs_lon = FULL_TURN * (row_ids[:, None].astype(jnp.float32) + obs_offset) / regions
     obs_sites = unit_rows(obs_latitude, obs_lon)
     gpr = slab_list.shape[1]
-    packed = jnp.concatenate(
-        [
-            obs_sites[:, :4, :],
-            jnp.pad(slab_list.astype(jnp.float32), ((0, 0), (0, capacity - gpr)))[:, None, :],
-        ],
-        axis=1,
-    )
-    slots = gather_slots(packed, "wide")
-    spare = jnp.zeros((ROWS, ROWS, capacity), jnp.float32)
-    site_slots = jnp.concatenate(
-        [jnp.pad(slots[:, :3, :], ((0, 0), (0, ROWS - 3), (0, 0))), spare], axis=0
-    )
-    list_slots = slots[:, 4, :gpr].astype(jnp.int32).reshape(-1)
-    left = site_slots[2 * reg_dev - margin : 2 * reg_dev]
-    right = site_slots[(n_wide - 1) * reg_dev : (n_wide - 1) * reg_dev + margin]
-    sites_wide = jnp.concatenate([left, obs_sites, right], axis=0)
-    live_mask = (jnp.arange(capacity, dtype=jnp.int32)[None, :] < region_sizes[:, None]).astype(
-        jnp.float32
-    )
-    solves = ridge_weight.shape[0]
-    diagonal = (obs_error * obs_error)[:, None, :] + ridge_weight[None, :, None]
-    observed = (innovation * live_mask)[:, None, :]
-    threshold = huber_cut[None, :, None] * obs_error[:, None, :]
-    obs_weights = observed / diagonal
-    live = live_mask[:, None, :]
-    step = jnp.broadcast_to(step_size[:, None], (solves, capacity))
-    local_cols = ((tile_columns - first_row + margin) % regions).reshape(-1)
-    tile_scale = 2.0 / (capacity * tile_columns.shape[1])
     n_slab = lax.axis_size("slab")
     assert n_slab == 2 and margin * n_slab == reg_dev
     sidx = lax.axis_index("slab")
@@ -275,30 +247,89 @@
     base = (sidx * sub).astype(jnp.int32).reshape(1)
     blocks = n_wide * n_slab
     pairs = ("wide", "slab")
-    other_pairs = [(b, b ^ 1) for b in range(blocks)]
+    first = sidx == 0
+    bid = me * n_slab + sidx
+
+    live_mask = (jnp.arange(capacity, dtype=jnp.int32)[None, :] < region_sizes[:, None]).astype(
+        jnp.float32
+    )
+    masked = innovation * live_mask
+    packed = jnp.concatenate(
+        [
+            obs_sites[:, :4, :],
+            jnp.pad(slab_list.astype(jnp.float32), ((0, 0), (0, capacity - gpr)))[:, None, :],
+            masked[:, None, :],
+            obs_error[:, None, :],
+        ],
+        axis=1,
+    )
+    slots = gather_slots(lax.dynamic_slice_in_dim(packed, sidx * sub, sub, 0), pairs)
+
+    left_rows = jnp.where(
+        first, slots[1 * sub : 2 * sub], slots[2 * sub : 3 * sub]
+    )
+    right_rows = jnp.where(
+        first,
+        slots[(blocks - 2) * sub : (blocks - 1) * sub],
+        slots[(blocks - 1) * sub : blocks * sub],
+    )
+    spare = jnp.zeros((ROWS, ROWS, capacity), jnp.float32)
+    site_slots = jnp.concatenate(
+        [jnp.pad(slots[:, :3, :], ((0, 0), (0, ROWS - 3), (0, 0))), spare], axis=0
+    )
+    list_slots = slots[:, 4, :gpr].astype(jnp.int32).reshape(-1)
+
+    def sites_of(rows):
+        return jnp.pad(rows[:, :3, :], ((0, 0), (0, ROWS - 3), (0, 0)))
+
+    sites_wide = jnp.concatenate([sites_of(left_rows), obs_sites, sites_of(right_rows)], axis=0)
+    solves = ridge_weight.shape[0]
+
+    def start_weights(masked_rows, error_rows):
+        return masked_rows[:, None, :] / ((error_rows * error_rows)[:, None, :] + ridge_weight[None, :, None])
+
+    diagonal = (obs_error * obs_error)[:, None, :] + ridge_weight[None, :, None]
+    observed = masked[:, None, :]
+    threshold = huber_cut[None, :, None] * obs_error[:, None, :]
+    obs_weights = observed / diagonal
+    live = live_mask[:, None, :]
+    step = jnp.broadcast_to(step_size[:, None], (solves, capacity))
+    local_cols = ((tile_columns - first_row + margin) % regions).reshape(-1)
+    tile_scale = 2.0 / (capacity * tile_columns.shape[1])
     q1_pairs = [(b, (b - 2) % blocks) if b % 2 == 0 else (b, (b + 2) % blocks) for b in range(blocks)]
     q2_pairs = [(b, (b - 1) % blocks) if b % 2 == 0 else (b, (b + 1) % blocks) for b in range(blocks)]
-    first = sidx == 0
-
-    def own_rows(mine):
-        other = lax.ppermute(mine, pairs, other_pairs)
-        return jnp.where(first, jnp.concatenate([mine, other]), jnp.concatenate([other, mine]))
-
-    weights_wide = with_halo(obs_weights, "wide", margin)
+    other_pairs = [(b, b ^ 1) for b in range(blocks)]
+
+    weights_wide = jnp.concatenate(
+        [
+            start_weights(left_rows[:, 5, :], left_rows[:, 6, :]),
+            obs_weights,
+            start_weights(right_rows[:, 5, :], right_rows[:, 6, :]),
+        ]
+    )
     for sweep_index in range(ITERS):
         mine = update(
             base, sub, local_cols, obs_sites, sites_wide, weights_wide, observed, diagonal,
             threshold, live, step, margin, tile_scale,
         )
-        obs_weights = own_rows(mine)
         if sweep_index + 1 < ITERS:
+            other = lax.ppermute(mine, pairs, other_pairs)
+            obs_weights = jnp.where(
+                first, jnp.concatenate([mine, other]), jnp.concatenate([other, mine])
+            )
             q1 = lax.ppermute(mine, pairs, q1_pairs)
             q2 = lax.ppermute(mine, pairs, q2_pairs)
             left = jnp.where(first, q2, q1)
             right = jnp.where(first, q1, q2)
             weights_wide = jnp.concatenate([left, obs_weights, right])
+    w_gathered = gather_slots(mine, pairs)
+    obs_weights = jnp.where(
+        first,
+        jnp.concatenate([w_gathered[:sub], w_gathered[(blocks - 1) * sub :]]),
+        jnp.concatenate([w_gathered[sub : 2 * sub], w_gathered[:sub]]),
+    )
     w_slots = jnp.concatenate(
-        [gather_slots(obs_weights, "wide"), jnp.zeros((ROWS, solves, capacity), jnp.float32)], axis=0
+        [w_gathered, jnp.zeros((ROWS, solves, capacity), jnp.float32)], axis=0
     )
 
     slab_count = slab_order.shape[0]
@@ -309,14 +340,14 @@
     g_lon = FULL_TURN * (own_slabs[:, None].astype(jnp.float32) + grid_offset[own_slabs]) / slab_count
     gsites = unit_rows(g_lat, g_lon)
     grid_increment = grid_stage(
-        me.astype(jnp.int32).reshape(1),
+        bid.astype(jnp.int32).reshape(1),
         own_slabs,
         list_slots,
         site_slots,
         w_slots,
         gsites,
-        reg_dev,
-        n_wide,
+        sub,
+        blocks,
         regions,
         slab_count,
     )

time: 98.2 us -> 101 us (1.029)
    ppermute x6 -> x14, starting transfers between devices: 11.2 us -> 16.7 us  [gather_slots(): lax.ppermute(x, axis, [(i, (i + s) % count) for i in range(count)])]
    ppermute x1, starting transfers between devices: 3.2 us -> 0.01 us  [body(): q1 = lax.ppermute(mine, pairs, q1_pairs)]
    ppermute x4 -> x1, starting transfers between devices: 3.06 us -> 0.01 us  [body(): other = lax.ppermute(mine, pairs, other_pairs)]
    ppermute x4 -> x1, waiting for transfers between devices: 2.43 us -> 0.01 us  [body(): other = lax.ppermute(mine, pairs, other_pairs)]
    ppermute x6 -> x14, waiting for transfers between devices: 8.03 us -> 10.4 us  [gather_slots(): lax.ppermute(x, axis, [(i, (i + s) % count) for i in range(count)])]
    ppermute x1, starting transfers between devices: 2.2 us -> 3.58 us  [body(): q2 = lax.ppermute(mine, pairs, q2_pairs)]
    unnamed x41 -> x50, local copies, waits for them, and re-layouts: 6.34 us -> 6.86 us
  transfers between devices with their start and end apart: 12 -> 17, of which waited for: 9 -> 9; matrix products, arithmetic and copies ran while one was open for 8% -> 8% of each run, Pallas kernels for 0% -> 0%
where the time goes in v3:
time: 101 us; the launch traced here: 99 us
  Pallas kernels  45.9 us (45%)
  starting transfers between devices  20.3 us (20%)
  waiting for transfers between devices  13.3 us (13%)
  local copies, waits for them, and re-layouts  13.1 us (13%)
  other arithmetic  5.45 us (5%)
    pallas_call x1, Pallas kernels, grid_stage(): pl.pallas_call(kernel, out_shape=jax.ShapeDtypeStruct((n_own, solves, gpt...  27.5 us
    pallas_call x2, Pallas kernels, update(): pl.pallas_call(make_update_kernel(margin, tile_scale), out_shape=jax.Shap...  18.4 us
    ppermute x14, starting transfers between devices, gather_slots(): lax.ppermute(x, axis, [(i, (i + s) % count) for i in range(count)])  16.7 us
    ppermute x14, waiting for transfers between devices, gather_slots(): lax.ppermute(x, axis, [(i, (i + s) % count) for i in range(count)])  10.4 us
    unnamed x50, local copies, waits for them, and re-layouts  6.86 us
    ppermute x1, starting transfers between devices, body(): q2 = lax.ppermute(mine, pairs, q2_pairs)  3.58 us
  transfers between devices with their start and end apart: 17, of which 9 were waited for; matrix products, arithmetic and copies ran while one was open for 8% of the time, Pallas kernels for 0%

profile of v3, /device:TPU:0, one launch (start us, length us, event | category | flops | bytes accessed | tf_op | source)
XLA Modules:
  0.0 99.0 jit_solution(8795288932729572666)
XLA Ops:
  5.3 2.6 %collective-permute-start.1 = (f32[16,7,128]{2,1,0:T(8,128)S(1)}, f32[16,7,128]{2,1,0:T(8,128)S(1)}, u32[]{:S(2)}, u32[]{:S(2)}) collective-permute-start(f32[16,7,128]{2,1,0:T(8,128)S(1)} %get-tuple-element.5), channel_id=1, source_target_pairs={{0,4},{1,5},{4,8},{5,9},{8,12},{9,13},{12,0},{13,1},{2,6},{3,7},{6... | collective-permute-start | bytes 172040 | tf_op jit(solution)/shard_map/ppermute | solution.py:36
  7.9 2.5 %collective-permute-start.9 = (f32[16,7,128]{2,1,0:T(8,128)S(1)}, f32[16,7,128]{2,1,0:T(8,128)S(1)}, u32[]{:S(2)}, u32[]{:S(2)}) collective-permute-start(f32[16,7,128]{2,1,0:T(8,128)S(1)} %get-tuple-element.5), channel_id=1, source_target_pairs={{0,5},{1,8},{4,9},{5,12},{8,13},{9,0},{12,1},{13,4},{2,7},{3,10},{... | collective-permute-start | bytes 172040 | tf_op jit(solution)/shard_map/ppermute | solution.py:36
  10.5 1.2 %collective-permute-start.10 = (f32[16,7,128]{2,1,0:T(8,128)S(1)}, f32[16,7,128]{2,1,0:T(8,128)S(1)}, u32[]{:S(2)}, u32[]{:S(2)}) collective-permute-start(f32[16,7,128]{2,1,0:T(8,128)S(1)} %get-tuple-element.5), channel_id=1, source_target_pairs={{0,8},{1,9},{4,12},{5,13},{8,0},{9,1},{12,4},{13,5},{2,10},{3,11},... | collective-permute-start | bytes 172040 | tf_op jit(solution)/shard_map/ppermute | solution.py:36
  11.7 1.2 %collective-permute-start.11 = (f32[16,7,128]{2,1,0:T(8,128)S(1)}, f32[16,7,128]{2,1,0:T(8,128)S(1)}, u32[]{:S(2)}, u32[]{:S(2)}) collective-permute-start(f32[16,7,128]{2,1,0:T(8,128)S(1)} %get-tuple-element.5), channel_id=1, source_target_pairs={{0,9},{1,12},{4,13},{5,0},{8,1},{9,4},{12,5},{13,8},{2,11},{3,14},... | collective-permute-start | bytes 172040 | tf_op jit(solution)/shard_map/ppermute | solution.py:36
  20.1 1.3 %collective-permute-start.2 = (f32[16,7,128]{2,1,0:T(8,128)S(1)}, f32[16,7,128]{2,1,0:T(8,128)S(1)}, u32[]{:S(2)}, u32[]{:S(2)}) collective-permute-start(f32[16,7,128]{2,1,0:T(8,128)S(1)} %get-tuple-element.5), channel_id=1, source_target_pairs={{0,12},{1,13},{4,0},{5,1},{8,4},{9,5},{12,8},{13,9},{2,14},{3,15},... | collective-permute-start | bytes 172040 | tf_op jit(solution)/shard_map/ppermute | solution.py:36
  21.4 1.5 %collective-permute-start.3 = (f32[16,7,128]{2,1,0:T(8,128)S(1)}, f32[16,7,128]{2,1,0:T(8,128)S(1)}, u32[]{:S(2)}, u32[]{:S(2)}) collective-permute-start(f32[16,7,128]{2,1,0:T(8,128)S(1)} %get-tuple-element.5), channel_id=1, source_target_pairs={{0,13},{1,0},{4,1},{5,4},{8,5},{9,8},{12,9},{13,12},{2,15},{3,2},{... | collective-permute-start | bytes 172040 | tf_op jit(solution)/shard_map/ppermute | solution.py:36
  23.0 1.4 %collective-permute-done.2 = f32[16,7,128]{2,1,0:T(8,128)S(1)} collective-permute-done((f32[16,7,128]{2,1,0:T(8,128)S(1)}, f32[16,7,128]{2,1,0:T(8,128)S(1)}, u32[]{:S(2)}, u32[]{:S(2)}) %collective-permute-start.2) | collective-permute-done | bytes 57376 | tf_op jit(solution)/shard_map/ppermute | solution.py:36
  24.9 0.9 select_maximum_fusion
  27.1 9.2 %shard_map.140 = f32[16,8,128]{2,1,0:T(8,128)} custom-call(s32[1]{0:T(128)} %bitcast.base_ref, s32[128]{0:T(128)} %reshape.139.cols_ref, f32[32,8,128]{2,1,0:T(8,128)} %copy-done.1, f32[64,8,128]{2,1,0:T(8,128)} %get-tuple-element.28.halo_ref, f32[64,8,128]{2,1,0:T(8,128)} %get-tuple-element.29.w_ref, f32[32,1,128]{2,1,0:T(1,128)} %bitcast.15, ...), custom_call_target="tpu_custom_call" | custom-call | tf_op jit(solution)/shard_map/pallas_call | solution.py:115
  36.3 3.6 %collective-permute-start.4 = (f32[16,8,128]{2,1,0:T(8,128)}, f32[16,8,128]{2,1,0:T(8,128)S(1)}, u32[]{:S(2)}, u32[]{:S(2)}) collective-permute-start(f32[16,8,128]{2,1,0:T(8,128)} %shard_map.140), channel_id=1, source_target_pairs={{0,13},{1,4},{4,1},{5,8},{8,5},{9,12},{12,9},{13,0},{2,15},{3,6},{... | collective-permute-start | bytes 196616 | tf_op jit(solution)/shard_map/ppermute | solution.py:321
  40.9 0.8 pad.41.sites_ref
  41.7 1.0 collective-permute-done.4
  42.7 1.9 %collective-permute-done.5 = f32[16,8,128]{2,1,0:T(8,128)S(1)} collective-permute-done((f32[16,8,128]{2,1,0:T(8,128)}, f32[16,8,128]{2,1,0:T(8,128)S(1)}, u32[]{:S(2)}, u32[]{:S(2)}) %collective-permute-start.5) | collective-permute-done | bytes 65568 | tf_op jit(solution)/shard_map/ppermute | solution.py:320
  45.3 9.2 %shard_map.141 = f32[16,8,128]{2,1,0:T(8,128)} custom-call(s32[1]{0:T(128)} %bitcast.base_ref, s32[128]{0:T(128)} %reshape.139.cols_ref, f32[32,8,128]{2,1,0:T(8,128)} %copy-done.1, f32[64,8,128]{2,1,0:T(8,128)} %get-tuple-element.28.halo_ref, f32[64,8,128]{2,1,0:T(8,128)} %pad_maximum_fusion.1.w_ref, f32[32,1,128]{2,1,0:T(1,128)} %bitcast.16, ...), custom_call_target="tpu_custom_call" | custom-call | tf_op jit(solution)/shard_map/pallas_call | solution.py:115
  54.5 1.0 collective-permute-start.7
  55.5 1.9 %collective-permute-start.13 = (f32[16,8,128]{2,1,0:T(8,128)}, f32[16,8,128]{2,1,0:T(8,128)S(1)}, u32[]{:S(2)}, u32[]{:S(2)}) collective-permute-start(f32[16,8,128]{2,1,0:T(8,128)} %shard_map.141), channel_id=1, source_target_pairs={{0,5},{1,8},{4,9},{5,12},{8,13},{9,0},{12,1},{13,4},{2,7},{3,10},{... | collective-permute-start | bytes 196616 | tf_op jit(solution)/shard_map/ppermute | solution.py:36
  57.4 2.2 %collective-permute-start.14 = (f32[16,8,128]{2,1,0:T(8,128)}, f32[16,8,128]{2,1,0:T(8,128)S(1)}, u32[]{:S(2)}, u32[]{:S(2)}) collective-permute-start(f32[16,8,128]{2,1,0:T(8,128)} %shard_map.141), channel_id=1, source_target_pairs={{0,8},{1,9},{4,12},{5,13},{8,0},{9,1},{12,4},{13,5},{2,10},{3,11},... | collective-permute-start | bytes 196616 | tf_op jit(solution)/shard_map/ppermute | solution.py:36
  59.6 0.9 constant_dynamic-update-slice_fusion.16
  60.5 0.9 collective-permute-done.8
  61.4 1.2 %collective-permute-done.12 = f32[16,8,128]{2,1,0:T(8,128)S(1)} collective-permute-done((f32[16,8,128]{2,1,0:T(8,128)}, f32[16,8,128]{2,1,0:T(8,128)S(1)}, u32[]{:S(2)}, u32[]{:S(2)}) %collective-permute-start.12) | collective-permute-done | bytes 65568 | tf_op jit(solution)/shard_map/ppermute | solution.py:36
  63.3 4.2 %collective-permute-done.13 = f32[16,8,128]{2,1,0:T(8,128)S(1)} collective-permute-done((f32[16,8,128]{2,1,0:T(8,128)}, f32[16,8,128]{2,1,0:T(8,128)S(1)}, u32[]{:S(2)}, u32[]{:S(2)}) %collective-permute-start.13) | collective-permute-done | bytes 65568 | tf_op jit(solution)/shard_map/ppermute | solution.py:36
  67.7 2.2 %collective-permute-done.16 = f32[16,8,128]{2,1,0:T(8,128)S(1)} collective-permute-done((f32[16,8,128]{2,1,0:T(8,128)S(1)}, f32[16,8,128]{2,1,0:T(8,128)S(1)}, u32[]{:S(2)}, u32[]{:S(2)}) %collective-permute-start.16) | collective-permute-done | bytes 65568 | tf_op jit(solution)/shard_map/ppermute | solution.py:36
  70.0 0.8 copy-done.2
  70.8 27.5 %shard_map.142 = f32[4,8,512]{2,1,0:T(8,128)} custom-call(s32[1]{0:T(128)} %bitcast.13.me_ref, s32[4]{0:T(128)} %copy-done.12, s32[512]{0:T(512)} %convert_element_type.43.list_ref, f32[136,8,128]{2,1,0:T(8,128)} %pad.41.sites_ref, f32[136,8,128]{2,1,0:T(8,128)} %copy-done.2, f32[4,8,512]{2,1,0:T(8,128)} %stack.30.gsites_ref), custom_call_target="tpu_custom_call" | custom-call | tf_op jit(solution)/shard_map/pallas_call | solution.py:204
  (110 shorter events, 16.9 us)
Async XLA Ops:
  0.6 15.0 %copy-start = (f32[32,512]{1,0:T(8,128)S(1)}, f32[32,512]{1,0:T(8,128)}, u32[]{:S(2)}) copy-start(f32[32,512]{1,0:T(8,128)} %param.21) | copy-start | bytes 196612
  3.0 13.8 %copy-start.4 = (f32[32,128]{1,0:T(8,128)}, f32[32,128]{1,0:T(8,128)S(1)}, u32[]{:S(2)}) copy-start(f32[32,128]{1,0:T(8,128)S(1)} %fusion.1) | copy-start | bytes 49156
  4.8 15.3 %collective-permute-start = (f32[16,7,128]{2,1,0:T(8,128)S(1)}, f32[16,7,128]{2,1,0:T(8,128)S(1)}, u32[]{:S(2)}, u32[]{:S(2)}) collective-permute-start(f32[16,7,128]{2,1,0:T(8,128)S(1)} %get-tuple-element.5), channel_id=1, source_target_pairs={{0,1},{1,4},{4,5},{5,8},{8,9},{9,12},{12,13},{13,0},{2,3},{3,6},{6... | collective-permute-start | bytes 172040 | tf_op jit(solution)/shard_map/ppermute | solution.py:36
  5.3 16.1 %collective-permute-start.1 = (f32[16,7,128]{2,1,0:T(8,128)S(1)}, f32[16,7,128]{2,1,0:T(8,128)S(1)}, u32[]{:S(2)}, u32[]{:S(2)}) collective-permute-start(f32[16,7,128]{2,1,0:T(8,128)S(1)} %get-tuple-element.5), channel_id=1, source_target_pairs={{0,4},{1,5},{4,8},{5,9},{8,12},{9,13},{12,0},{13,1},{2,6},{3,7},{6... | collective-permute-start | bytes 172040 | tf_op jit(solution)/shard_map/ppermute | solution.py:36
  7.9 15.0 %collective-permute-start.9 = (f32[16,7,128]{2,1,0:T(8,128)S(1)}, f32[16,7,128]{2,1,0:T(8,128)S(1)}, u32[]{:S(2)}, u32[]{:S(2)}) collective-permute-start(f32[16,7,128]{2,1,0:T(8,128)S(1)} %get-tuple-element.5), channel_id=1, source_target_pairs={{0,5},{1,8},{4,9},{5,12},{8,13},{9,0},{12,1},{13,4},{2,7},{3,10},{... | collective-permute-start | bytes 172040 | tf_op jit(solution)/shard_map/ppermute | solution.py:36
  10.5 12.5 %collective-permute-start.10 = (f32[16,7,128]{2,1,0:T(8,128)S(1)}, f32[16,7,128]{2,1,0:T(8,128)S(1)}, u32[]{:S(2)}, u32[]{:S(2)}) collective-permute-start(f32[16,7,128]{2,1,0:T(8,128)S(1)} %get-tuple-element.5), channel_id=1, source_target_pairs={{0,8},{1,9},{4,12},{5,13},{8,0},{9,1},{12,4},{13,5},{2,10},{3,11},... | collective-permute-start | bytes 172040 | tf_op jit(solution)/shard_map/ppermute | solution.py:36
  11.7 11.3 %collective-permute-start.11 = (f32[16,7,128]{2,1,0:T(8,128)S(1)}, f32[16,7,128]{2,1,0:T(8,128)S(1)}, u32[]{:S(2)}, u32[]{:S(2)}) collective-permute-start(f32[16,7,128]{2,1,0:T(8,128)S(1)} %get-tuple-element.5), channel_id=1, source_target_pairs={{0,9},{1,12},{4,13},{5,0},{8,1},{9,4},{12,5},{13,8},{2,11},{3,14},... | collective-permute-start | bytes 172040 | tf_op jit(solution)/shard_map/ppermute | solution.py:36
  15.0 1.3 %copy-start.7 = (f32[32,512]{1,0:T(8,128)S(1)}, f32[32,512]{1,0:T(8,128)}, u32[]{:S(2)}) copy-start(f32[32,512]{1,0:T(8,128)} %param.22) | copy-start | bytes 196612
  19.3 5.6 %copy-start.1 = (f32[32,8,128]{2,1,0:T(8,128)}, f32[32,8,128]{2,1,0:T(8,128)S(1)}, u32[]{:S(2)}) copy-start(f32[32,8,128]{2,1,0:T(8,128)S(1)} %stack.28.own_ref) | copy-start | bytes 393220
  20.1 4.3 %collective-permute-start.2 = (f32[16,7,128]{2,1,0:T(8,128)S(1)}, f32[16,7,128]{2,1,0:T(8,128)S(1)}, u32[]{:S(2)}, u32[]{:S(2)}) collective-permute-start(f32[16,7,128]{2,1,0:T(8,128)S(1)} %get-tuple-element.5), channel_id=1, source_target_pairs={{0,12},{1,13},{4,0},{5,1},{8,4},{9,5},{12,8},{13,9},{2,14},{3,15},... | collective-permute-start | bytes 172040 | tf_op jit(solution)/shard_map/ppermute | solution.py:36
  21.4 3.4 %collective-permute-start.3 = (f32[16,7,128]{2,1,0:T(8,128)S(1)}, f32[16,7,128]{2,1,0:T(8,128)S(1)}, u32[]{:S(2)}, u32[]{:S(2)}) collective-permute-start(f32[16,7,128]{2,1,0:T(8,128)S(1)} %get-tuple-element.5), channel_id=1, source_target_pairs={{0,13},{1,0},{4,1},{5,4},{8,5},{9,8},{12,9},{13,12},{2,15},{3,2},{... | collective-permute-start | bytes 172040 | tf_op jit(solution)/shard_map/ppermute | solution.py:36
  36.3 6.4 %collective-permute-start.4 = (f32[16,8,128]{2,1,0:T(8,128)}, f32[16,8,128]{2,1,0:T(8,128)S(1)}, u32[]{:S(2)}, u32[]{:S(2)}) collective-permute-start(f32[16,8,128]{2,1,0:T(8,128)} %shard_map.140), channel_id=1, source_target_pairs={{0,13},{1,4},{4,1},{5,8},{8,5},{9,12},{12,9},{13,0},{2,15},{3,6},{... | collective-permute-start | bytes 196616 | tf_op jit(solution)/shard_map/ppermute | solution.py:321
  39.9 4.7 %collective-permute-start.5 = (f32[16,8,128]{2,1,0:T(8,128)}, f32[16,8,128]{2,1,0:T(8,128)S(1)}, u32[]{:S(2)}, u32[]{:S(2)}) collective-permute-start(f32[16,8,128]{2,1,0:T(8,128)} %shard_map.140), channel_id=1, source_target_pairs={{0,12},{1,5},{4,0},{5,9},{8,4},{9,13},{12,8},{13,1},{2,14},{3,7},{... | collective-permute-start | bytes 196616 | tf_op jit(solution)/shard_map/ppermute | solution.py:320
  39.9 1.8 %collective-permute-start.6 = (f32[16,8,128]{2,1,0:T(8,128)}, f32[16,8,128]{2,1,0:T(8,128)S(1)}, u32[]{:S(2)}, u32[]{:S(2)}) collective-permute-start(f32[16,8,128]{2,1,0:T(8,128)} %shard_map.140), channel_id=1, source_target_pairs={{0,1},{1,0},{4,5},{5,4},{8,9},{9,8},{12,13},{13,12},{2,3},{3,2},{6... | collective-permute-start | bytes 196616 | tf_op jit(solution)/shard_map/ppermute | solution.py:316
  40.9 0.9 copy-start.5
  54.5 6.9 %copy-start.3 = (f32[16,8,128]{2,1,0:T(8,128)S(1)}, f32[16,8,128]{2,1,0:T(8,128)}, u32[]{:S(2)}) copy-start(f32[16,8,128]{2,1,0:T(8,128)} %shard_map.141) | copy-start | bytes 196612
  54.5 15.4 %collective-permute-start.7 = (f32[16,8,128]{2,1,0:T(8,128)}, f32[16,8,128]{2,1,0:T(8,128)S(1)}, u32[]{:S(2)}, u32[]{:S(2)}) collective-permute-start(f32[16,8,128]{2,1,0:T(8,128)} %shard_map.141), channel_id=1, source_target_pairs={{0,13},{1,0},{4,1},{5,4},{8,5},{9,8},{12,9},{13,12},{2,15},{3,2},{... | collective-permute-start | bytes 196616 | tf_op jit(solution)/shard_map/ppermute | solution.py:36
  55.5 5.9 %collective-permute-start.8 = (f32[16,8,128]{2,1,0:T(8,128)}, f32[16,8,128]{2,1,0:T(8,128)S(1)}, u32[]{:S(2)}, u32[]{:S(2)}) collective-permute-start(f32[16,8,128]{2,1,0:T(8,128)} %shard_map.141), channel_id=1, source_target_pairs={{0,1},{1,4},{4,5},{5,8},{8,9},{9,12},{12,13},{13,0},{2,3},{3,6},{6... | collective-permute-start | bytes 196616 | tf_op jit(solution)/shard_map/ppermute | solution.py:36
  55.5 7.1 %collective-permute-start.12 = (f32[16,8,128]{2,1,0:T(8,128)}, f32[16,8,128]{2,1,0:T(8,128)S(1)}, u32[]{:S(2)}, u32[]{:S(2)}) collective-permute-start(f32[16,8,128]{2,1,0:T(8,128)} %shard_map.141), channel_id=1, source_target_pairs={{0,4},{1,5},{4,8},{5,9},{8,12},{9,13},{12,0},{13,1},{2,6},{3,7},{6... | collective-permute-start | bytes 196616 | tf_op jit(solution)/shard_map/ppermute | solution.py:36
  55.5 12.0 %collective-permute-start.13 = (f32[16,8,128]{2,1,0:T(8,128)}, f32[16,8,128]{2,1,0:T(8,128)S(1)}, u32[]{:S(2)}, u32[]{:S(2)}) collective-permute-start(f32[16,8,128]{2,1,0:T(8,128)} %shard_map.141), channel_id=1, source_target_pairs={{0,5},{1,8},{4,9},{5,12},{8,13},{9,0},{12,1},{13,4},{2,7},{3,10},{... | collective-permute-start | bytes 196616 | tf_op jit(solution)/shard_map/ppermute | solution.py:36
  57.4 10.3 %collective-permute-start.14 = (f32[16,8,128]{2,1,0:T(8,128)}, f32[16,8,128]{2,1,0:T(8,128)S(1)}, u32[]{:S(2)}, u32[]{:S(2)}) collective-permute-start(f32[16,8,128]{2,1,0:T(8,128)} %shard_map.141), channel_id=1, source_target_pairs={{0,8},{1,9},{4,12},{5,13},{8,0},{9,1},{12,4},{13,5},{2,10},{3,11},... | collective-permute-start | bytes 196616 | tf_op jit(solution)/shard_map/ppermute | solution.py:36
  61.4 6.3 %collective-permute-start.15 = (f32[16,8,128]{2,1,0:T(8,128)S(1)}, f32[16,8,128]{2,1,0:T(8,128)S(1)}, u32[]{:S(2)}, u32[]{:S(2)}) collective-permute-start(f32[16,8,128]{2,1,0:T(8,128)S(1)} %copy-done.3), channel_id=1, source_target_pairs={{0,9},{1,12},{4,13},{5,0},{8,1},{9,4},{12,5},{13,8},{2,11},{3,14},... | collective-permute-start | bytes 196616 | tf_op jit(solution)/shard_map/ppermute | solution.py:36
  62.6 7.3 %collective-permute-start.16 = (f32[16,8,128]{2,1,0:T(8,128)S(1)}, f32[16,8,128]{2,1,0:T(8,128)S(1)}, u32[]{:S(2)}, u32[]{:S(2)}) collective-permute-start(f32[16,8,128]{2,1,0:T(8,128)S(1)} %copy-done.3), channel_id=1, source_target_pairs={{0,12},{1,13},{4,0},{5,1},{8,4},{9,5},{12,8},{13,9},{2,14},{3,15},... | collective-permute-start | bytes 196616 | tf_op jit(solution)/shard_map/ppermute | solution.py:36
  69.9 0.8 copy-start.2
  (11 other events, 7.5 us)

commit v4 on v1

--- a/solution.py
+++ b/solution.py
@@ -44,6 +44,14 @@
         [c * jnp.cos(longitude), c * jnp.sin(longitude), jnp.sin(latitude)] + [zero] * (ROWS - 3),
         axis=-2,
     )
+
+
+def corr_cols(cx, cy, cz, row):
+    dx = cx - row[0:1, :]
+    dy = cy - row[1:2, :]
+    dz = cz - row[2:3, :]
+    d2 = dx * dx + dy * dy + dz * dz
+    return jnp.exp(jnp.sqrt(d2) * (-DECAY_RATE))
 
 
 def corr_block(col_t, row):
@@ -126,7 +134,7 @@
 
     def grid_kernel(
         me_ref, own_slabs_ref, list_ref, sites_ref, w_ref, gsites_ref, out_ref,
-        sel_ref, slab_ref, buf0, buf1,
+        sel_ref, slab_ref, buf0, buf1, cols_ref,
     ):
         n_own = out_ref.shape[0]
         gpr = list_ref.shape[0] // regions
@@ -164,12 +172,20 @@
         n_pairs = (n_groups + 1) // 2
         last = 2 * n_pairs - 1
         out_ref[...] = jnp.zeros(out_ref.shape, jnp.float32)
+        gpts = out_ref.shape[2]
+        for j in range(n_own):
+            g_t = gsites_ref[j].T
+            for c in range(3):
+                cols_ref[3 * j + c] = jnp.broadcast_to(g_t[:, c : c + 1], (gpts, cap))
 
         def fill(g, buf):
-            g_t = gsites_ref[slab_ref[g]].T
+            j = slab_ref[g]
+            cx = cols_ref[3 * j]
+            cy = cols_ref[3 * j + 1]
+            cz = cols_ref[3 * j + 2]
             for e in range(GROUP):
                 slot = sel_ref[g * GROUP + e]
-                buf[:, e * cap : (e + 1) * cap] = corr_block(g_t, sites_ref[slot])
+                buf[:, e * cap : (e + 1) * cap] = corr_cols(cx, cy, cz, sites_ref[slot])
 
         def use(g, buf):
             j = slab_ref[g]
@@ -211,6 +227,7 @@
             pltpu.SMEM((sel_len // GROUP + 2,), jnp.int32),
             pltpu.VMEM((gpts, GROUP * cap), jnp.float32),
             pltpu.VMEM((gpts, GROUP * cap), jnp.float32),
+            pltpu.VMEM((3 * n_own, gpts, cap), jnp.float32),
         ],
     )(me, own_slabs, list_slots, site_slots, w_slots, gsites)
 

time: 98.2 us -> 102 us (1.039)
  Pallas kernels: 45.9 us -> 49.9 us
    pallas_call x1, Pallas kernels: 27.5 us -> 31.5 us  [grid_stage(): pl.pallas_call(kernel, out_shape=jax.ShapeDtypeStruct((n_own, solves, gpt...]
where the time goes in v4:
time: 102 us; the launch traced here: 101 us
  Pallas kernels  49.9 us (49%)
  starting transfers between devices  19.6 us (19%)
  local copies, waits for them, and re-layouts  12.5 us (12%)
  waiting for transfers between devices  12.4 us (12%)
  other arithmetic  5.3 us (5%)
    pallas_call x1, Pallas kernels, grid_stage(): pl.pallas_call(kernel, out_shape=jax.ShapeDtypeStruct((n_own, solves, gpt...  31.5 us
    pallas_call x2, Pallas kernels, update(): pl.pallas_call(make_update_kernel(margin, tile_scale), out_shape=jax.Shap...  18.4 us
    ppermute x6, starting transfers between devices, gather_slots(): lax.ppermute(x, axis, [(i, (i + s) % count) for i in range(count)])  11.2 us
    ppermute x6, waiting for transfers between devices, gather_slots(): lax.ppermute(x, axis, [(i, (i + s) % count) for i in range(count)])  8.03 us
    unnamed x41, local copies, waits for them, and re-layouts  6.34 us
    ppermute x1, starting transfers between devices, body(): q1 = lax.ppermute(mine, pairs, q1_pairs)  3.2 us
    ppermute x1, starting transfers between devices, with_halo(): lax.ppermute(head, axis, [((i + 1) % count, i) for i in range(count)])  2.87 us
    ppermute x1, starting transfers between devices, body(): q2 = lax.ppermute(mine, pairs, q2_pairs)  2.2 us
  transfers between devices with their start and end apart: 12, of which 9 were waited for; matrix products, arithmetic and copies ran while one was open for 8% of the time, Pallas kernels for 0%

profile of v4, /device:TPU:0, one launch (start us, length us, event | category | flops | bytes accessed | tf_op | source)
XLA Modules:
  0.0 100.6 jit_solution(3642279724522848880)
XLA Ops:
  0.7 0.8 fusion.5
  3.3 5.1 %collective-permute-start.2 = (f32[32,5,128]{2,1,0:T(8,128)S(1)}, f32[32,5,128]{2,1,0:T(8,128)S(1)}, u32[]{:S(2)}, u32[]{:S(2)}) collective-permute-start(f32[32,5,128]{2,1,0:T(8,128)S(1)} %concatenate.35), channel_id=1, source_target_pairs={{0,12},{4,0},{8,4},{12,8},{1,13},{5,1},{9,5},{13,9},{2,14},{6,2},{... | collective-permute-start | bytes 245768 | tf_op jit(solution)/shard_map/ppermute | solution.py:36
  8.4 1.0 %collective-permute-start = (f32[32,5,128]{2,1,0:T(8,128)S(1)}, f32[32,5,128]{2,1,0:T(8,128)S(1)}, u32[]{:S(2)}, u32[]{:S(2)}) collective-permute-start(f32[32,5,128]{2,1,0:T(8,128)S(1)} %concatenate.35), channel_id=1, source_target_pairs={{0,4},{4,8},{8,12},{12,0},{1,5},{5,9},{9,13},{13,1},{2,6},{6,10},{... | collective-permute-start | bytes 245768 | tf_op jit(solution)/shard_map/ppermute | solution.py:36
  10.1 0.7 broadcast_add_fusion
  10.9 2.9 %collective-permute-start.4 = (f32[16,8,128]{2,1,0:T(8,128)S(1)}, f32[16,8,128]{2,1,0:T(8,128)S(1)}, u32[]{:S(2)}, u32[]{:S(2)}) collective-permute-start(f32[16,8,128]{2,1,0:T(8,128)S(1)} %get-tuple-element.11), channel_id=1, source_target_pairs={{4,0},{8,4},{12,8},{0,12},{5,1},{9,5},{13,9},{1,13},{6,2},{10,6},{... | collective-permute-start | bytes 196616 | tf_op jit(solution)/shard_map/ppermute | solution.py:26
  15.8 0.7 broadcast_multiply_fusion.thr_ref
  18.8 1.1 %collective-permute-done.4 = f32[16,8,128]{2,1,0:T(8,128)S(1)} collective-permute-done((f32[16,8,128]{2,1,0:T(8,128)S(1)}, f32[16,8,128]{2,1,0:T(8,128)S(1)}, u32[]{:S(2)}, u32[]{:S(2)}) %collective-permute-start.4) | collective-permute-done | bytes 65568 | tf_op jit(solution)/shard_map/ppermute | solution.py:26
  19.8 0.7 collective-permute-done.3
  20.6 0.7 pad_maximum_fusion.2.w_ref
  21.9 0.7 pad_maximum_fusion.1.halo_ref
  24.0 9.2 %shard_map.140 = f32[16,8,128]{2,1,0:T(8,128)} custom-call(s32[1]{0:T(128)} %bitcast.base_ref, s32[128]{0:T(128)} %reshape.139.cols_ref, f32[32,8,128]{2,1,0:T(8,128)} %copy-done.1, f32[64,8,128]{2,1,0:T(8,128)} %pad_maximum_fusion.1.halo_ref, f32[64,8,128]{2,1,0:T(8,128)} %pad_maximum_fusion.2.w_ref, f32[32,1,128]{2,1,0:T(1,128)} %bitcast.9, ...), custom_call_target="tpu_custom_call" | custom-call | tf_op jit(solution)/shard_map/pallas_call | solution.py:123
  34.0 2.2 %collective-permute-start.5 = (f32[16,8,128]{2,1,0:T(8,128)S(1)}, f32[16,8,128]{2,1,0:T(8,128)S(1)}, u32[]{:S(2)}, u32[]{:S(2)}) collective-permute-start(f32[16,8,128]{2,1,0:T(8,128)S(1)} %copy-done.5), channel_id=1, source_target_pairs={{0,13},{1,4},{4,1},{5,8},{8,5},{9,12},{12,9},{13,0},{2,15},{3,6},{... | collective-permute-start | bytes 196616 | tf_op jit(solution)/shard_map/ppermute | solution.py:313
  36.2 3.2 %collective-permute-start.6 = (f32[16,8,128]{2,1,0:T(8,128)S(1)}, f32[16,8,128]{2,1,0:T(8,128)S(1)}, u32[]{:S(2)}, u32[]{:S(2)}) collective-permute-start(f32[16,8,128]{2,1,0:T(8,128)S(1)} %copy-done.5), channel_id=1, source_target_pairs={{0,12},{1,5},{4,0},{5,9},{8,4},{9,13},{12,8},{13,1},{2,14},{3,7},{... | collective-permute-start | bytes 196616 | tf_op jit(solution)/shard_map/ppermute | solution.py:312
  39.5 1.8 %collective-permute-done.6 = f32[16,8,128]{2,1,0:T(8,128)S(1)} collective-permute-done((f32[16,8,128]{2,1,0:T(8,128)S(1)}, f32[16,8,128]{2,1,0:T(8,128)S(1)}, u32[]{:S(2)}, u32[]{:S(2)}) %collective-permute-start.6) | collective-permute-done | bytes 65568 | tf_op jit(solution)/shard_map/ppermute | solution.py:312
  41.3 0.7 pad_maximum_fusion.3.w_ref
  42.0 9.2 %shard_map.141 = f32[16,8,128]{2,1,0:T(8,128)} custom-call(s32[1]{0:T(128)} %bitcast.base_ref, s32[128]{0:T(128)} %reshape.139.cols_ref, f32[32,8,128]{2,1,0:T(8,128)} %copy-done.1, f32[64,8,128]{2,1,0:T(8,128)} %pad_maximum_fusion.1.halo_ref, f32[64,8,128]{2,1,0:T(8,128)} %pad_maximum_fusion.3.w_ref, f32[32,1,128]{2,1,0:T(1,128)} %bitcast.10, ...), custom_call_target="tpu_custom_call" | custom-call | tf_op jit(solution)/shard_map/pallas_call | solution.py:123
  52.8 1.0 collective-permute-start.9
  54.8 3.9 %collective-permute-start.10 = (f32[32,8,128]{2,1,0:T(8,128)S(1)}, f32[32,8,128]{2,1,0:T(8,128)S(1)}, u32[]{:S(2)}, u32[]{:S(2)}) collective-permute-start(f32[32,8,128]{2,1,0:T(8,128)S(1)} %get-tuple-element.5), channel_id=1, source_target_pairs={{0,8},{4,12},{8,0},{12,4},{1,9},{5,13},{9,1},{13,5},{2,10},{6,14},... | collective-permute-start | bytes 393224 | tf_op jit(solution)/shard_map/ppermute | solution.py:36
  59.7 0.8 concatenate.44.sites_ref
  60.7 0.8 collective-permute-done.9
  61.4 5.1 %collective-permute-done.10 = f32[32,8,128]{2,1,0:T(8,128)S(1)} collective-permute-done((f32[32,8,128]{2,1,0:T(8,128)S(1)}, f32[32,8,128]{2,1,0:T(8,128)S(1)}, u32[]{:S(2)}, u32[]{:S(2)}) %collective-permute-start.10) | collective-permute-done | bytes 131104 | tf_op jit(solution)/shard_map/ppermute | solution.py:36
  66.6 1.7 %collective-permute-done.11 = f32[32,8,128]{2,1,0:T(8,128)S(1)} collective-permute-done((f32[32,8,128]{2,1,0:T(8,128)S(1)}, f32[32,8,128]{2,1,0:T(8,128)S(1)}, u32[]{:S(2)}, u32[]{:S(2)}) %collective-permute-start.11) | collective-permute-done | bytes 131104 | tf_op jit(solution)/shard_map/ppermute | solution.py:36
  68.3 0.8 copy-done.2
  69.1 31.5 %shard_map.142 = f32[4,8,512]{2,1,0:T(8,128)} custom-call(s32[1]{0:T(128)} %bitcast.8.me_ref, s32[4]{0:T(128)} %copy-done.12, s32[512]{0:T(512)} %convert_element_type.40.list_ref, f32[136,8,128]{2,1,0:T(8,128)} %concatenate.44.sites_ref, f32[136,8,128]{2,1,0:T(8,128)} %copy-done.2, f32[4,8,512]{2,1,0:T(8,128)} %stack.30.gsites_ref), custom_call_target="tpu_custom_call" | custom-call | tf_op jit(solution)/shard_map/pallas_call | solution.py:220
  (89 shorter events, 13.3 us)
Async XLA Ops:
  0.6 32.6 %copy-start = (f32[32,512]{1,0:T(8,128)S(1)}, f32[32,512]{1,0:T(8,128)}, u32[]{:S(2)}) copy-start(f32[32,512]{1,0:T(8,128)} %param.21) | copy-start | bytes 196612
  2.3 0.7 copy-start.10
  3.1 6.3 %copy-start.6 = (f32[32,128]{1,0:T(8,128)S(1)}, f32[32,128]{1,0:T(8,128)}, u32[]{:S(2)}) copy-start(f32[32,128]{1,0:T(8,128)} %param.16) | copy-start | bytes 49156
  3.3 6.2 %copy-start.9 = (f32[32,128]{1,0:T(8,128)S(1)}, f32[32,128]{1,0:T(8,128)}, u32[]{:S(2)}) copy-start(f32[32,128]{1,0:T(8,128)} %param.15) | copy-start | bytes 49156
  3.3 6.2 %copy-start.11 = (s32[32]{0:T(128)S(1)}, s32[32]{0:T(128)}, u32[]{:S(2)}) copy-start(s32[32]{0:T(128)} %param.17) | copy-start | bytes 388
  3.3 18.0 %collective-permute-start.2 = (f32[32,5,128]{2,1,0:T(8,128)S(1)}, f32[32,5,128]{2,1,0:T(8,128)S(1)}, u32[]{:S(2)}, u32[]{:S(2)}) collective-permute-start(f32[32,5,128]{2,1,0:T(8,128)S(1)} %concatenate.35), channel_id=1, source_target_pairs={{0,12},{4,0},{8,4},{12,8},{1,13},{5,1},{9,5},{13,9},{2,14},{6,2},{... | collective-permute-start | bytes 245768 | tf_op jit(solution)/shard_map/ppermute | solution.py:36
  8.4 13.4 %collective-permute-start.1 = (f32[32,5,128]{2,1,0:T(8,128)S(1)}, f32[32,5,128]{2,1,0:T(8,128)S(1)}, u32[]{:S(2)}, u32[]{:S(2)}) collective-permute-start(f32[32,5,128]{2,1,0:T(8,128)S(1)} %concatenate.35), channel_id=1, source_target_pairs={{0,8},{4,12},{8,0},{12,4},{1,9},{5,13},{9,1},{13,5},{2,10},{6,14},... | collective-permute-start | bytes 245768 | tf_op jit(solution)/shard_map/ppermute | solution.py:36
  8.4 13.4 %collective-permute-start = (f32[32,5,128]{2,1,0:T(8,128)S(1)}, f32[32,5,128]{2,1,0:T(8,128)S(1)}, u32[]{:S(2)}, u32[]{:S(2)}) collective-permute-start(f32[32,5,128]{2,1,0:T(8,128)S(1)} %concatenate.35), channel_id=1, source_target_pairs={{0,4},{4,8},{8,12},{12,0},{1,5},{5,9},{9,13},{13,1},{2,6},{6,10},{... | collective-permute-start | bytes 245768 | tf_op jit(solution)/shard_map/ppermute | solution.py:36
  10.1 0.7 copy-start.3
  10.9 8.9 %collective-permute-start.4 = (f32[16,8,128]{2,1,0:T(8,128)S(1)}, f32[16,8,128]{2,1,0:T(8,128)S(1)}, u32[]{:S(2)}, u32[]{:S(2)}) collective-permute-start(f32[16,8,128]{2,1,0:T(8,128)S(1)} %get-tuple-element.11), channel_id=1, source_target_pairs={{4,0},{8,4},{12,8},{0,12},{5,1},{9,5},{13,9},{1,13},{6,2},{10,6},{... | collective-permute-start | bytes 196616 | tf_op jit(solution)/shard_map/ppermute | solution.py:26
  13.7 6.8 %collective-permute-start.3 = (f32[16,8,128]{2,1,0:T(8,128)S(1)}, f32[16,8,128]{2,1,0:T(8,128)S(1)}, u32[]{:S(2)}, u32[]{:S(2)}) collective-permute-start(f32[16,8,128]{2,1,0:T(8,128)S(1)} %get-tuple-element.10), channel_id=1, source_target_pairs={{0,4},{4,8},{8,12},{12,0},{1,5},{5,9},{9,13},{13,1},{2,6},{6,10},{... | collective-permute-start | bytes 196616 | tf_op jit(solution)/shard_map/ppermute | solution.py:24
  18.8 3.2 %copy-start.1 = (f32[32,8,128]{2,1,0:T(8,128)}, f32[32,8,128]{2,1,0:T(8,128)S(1)}, u32[]{:S(2)}) copy-start(f32[32,8,128]{2,1,0:T(8,128)S(1)} %stack.28.own_ref) | copy-start | bytes 393220
  33.2 0.8 copy-start.5
  33.2 6.2 %collective-permute-start.7 = (f32[16,8,128]{2,1,0:T(8,128)}, f32[16,8,128]{2,1,0:T(8,128)S(1)}, u32[]{:S(2)}, u32[]{:S(2)}) collective-permute-start(f32[16,8,128]{2,1,0:T(8,128)} %shard_map.140), channel_id=1, source_target_pairs={{0,1},{1,0},{4,5},{5,4},{8,9},{9,8},{12,13},{13,12},{2,3},{3,2},{6... | collective-permute-start | bytes 196616 | tf_op jit(solution)/shard_map/ppermute | solution.py:301
  34.0 5.5 %collective-permute-start.5 = (f32[16,8,128]{2,1,0:T(8,128)S(1)}, f32[16,8,128]{2,1,0:T(8,128)S(1)}, u32[]{:S(2)}, u32[]{:S(2)}) collective-permute-start(f32[16,8,128]{2,1,0:T(8,128)S(1)} %copy-done.5), channel_id=1, source_target_pairs={{0,13},{1,4},{4,1},{5,8},{8,5},{9,12},{12,9},{13,0},{2,15},{3,6},{... | collective-permute-start | bytes 196616 | tf_op jit(solution)/shard_map/ppermute | solution.py:313
  36.2 5.1 %collective-permute-start.6 = (f32[16,8,128]{2,1,0:T(8,128)S(1)}, f32[16,8,128]{2,1,0:T(8,128)S(1)}, u32[]{:S(2)}, u32[]{:S(2)}) collective-permute-start(f32[16,8,128]{2,1,0:T(8,128)S(1)} %copy-done.5), channel_id=1, source_target_pairs={{0,12},{1,5},{4,0},{5,9},{8,4},{9,13},{12,8},{13,1},{2,14},{3,7},{... | collective-permute-start | bytes 196616 | tf_op jit(solution)/shard_map/ppermute | solution.py:312
  42.0 9.5 %copy-start.8 = (f32[32,512]{1,0:T(8,128)S(1)}, f32[32,512]{1,0:T(8,128)}, u32[]{:S(2)}) copy-start(f32[32,512]{1,0:T(8,128)} %param.22) | copy-start | bytes 196612
  51.3 1.5 %copy-start.4 = (f32[16,8,128]{2,1,0:T(8,128)S(1)}, f32[16,8,128]{2,1,0:T(8,128)}, u32[]{:S(2)}) copy-start(f32[16,8,128]{2,1,0:T(8,128)} %shard_map.141) | copy-start | bytes 196612
  51.3 1.5 %collective-permute-start.8 = (f32[16,8,128]{2,1,0:T(8,128)}, f32[16,8,128]{2,1,0:T(8,128)S(1)}, u32[]{:S(2)}, u32[]{:S(2)}) collective-permute-start(f32[16,8,128]{2,1,0:T(8,128)} %shard_map.141), channel_id=1, source_target_pairs={{0,1},{1,0},{4,5},{5,4},{8,9},{9,8},{12,13},{13,12},{2,3},{3,2},{6... | collective-permute-start | bytes 196616 | tf_op jit(solution)/shard_map/ppermute | solution.py:301
  52.8 7.7 %copy-start.7 = (f32[32,8,128]{2,1,0:T(8,128)}, f32[32,8,128]{2,1,0:T(8,128)S(1)}, u32[]{:S(2)}) copy-start(f32[32,8,128]{2,1,0:T(8,128)S(1)} %get-tuple-element.5) | copy-start | bytes 393220
  52.8 8.7 %collective-permute-start.9 = (f32[32,8,128]{2,1,0:T(8,128)S(1)}, f32[32,8,128]{2,1,0:T(8,128)S(1)}, u32[]{:S(2)}, u32[]{:S(2)}) collective-permute-start(f32[32,8,128]{2,1,0:T(8,128)S(1)} %get-tuple-element.5), channel_id=1, source_target_pairs={{0,4},{4,8},{8,12},{12,0},{1,5},{5,9},{9,13},{13,1},{2,6},{6,10},{... | collective-permute-start | bytes 393224 | tf_op jit(solution)/shard_map/ppermute | solution.py:36
  54.8 11.7 %collective-permute-start.10 = (f32[32,8,128]{2,1,0:T(8,128)S(1)}, f32[32,8,128]{2,1,0:T(8,128)S(1)}, u32[]{:S(2)}, u32[]{:S(2)}) collective-permute-start(f32[32,8,128]{2,1,0:T(8,128)S(1)} %get-tuple-element.5), channel_id=1, source_target_pairs={{0,8},{4,12},{8,0},{12,4},{1,9},{5,13},{9,1},{13,5},{2,10},{6,14},... | collective-permute-start | bytes 393224 | tf_op jit(solution)/shard_map/ppermute | solution.py:36
  60.5 7.7 %collective-permute-start.11 = (f32[32,8,128]{2,1,0:T(8,128)S(1)}, f32[32,8,128]{2,1,0:T(8,128)S(1)}, u32[]{:S(2)}, u32[]{:S(2)}) collective-permute-start(f32[32,8,128]{2,1,0:T(8,128)S(1)} %get-tuple-element.5), channel_id=1, source_target_pairs={{0,12},{4,0},{8,4},{12,8},{1,13},{5,1},{9,5},{13,9},{2,14},{6,2},{... | collective-permute-start | bytes 393224 | tf_op jit(solution)/shard_map/ppermute | solution.py:36
  68.2 0.8 copy-start.2
  (7 other events, 4.6 us)

commit v5 on v1

--- a/solution.py
+++ b/solution.py
@@ -12,7 +12,7 @@
 FULL_TURN = 6.283185307179586
 HIGHEST = lax.Precision.HIGHEST
 ROWS = 8
-GROUP = 4
+GROUP = 2
 
 
 def with_halo(cells, axis, width):

time: 98.2 us -> 98.3 us (level)
  the two profiles are of different devices: /device:TPU:0 before, /device:TPU:9 now
where the time goes in v5:
time: 98.3 us; the launch traced here: 98.5 us
  Pallas kernels  49.1 us (50%)
  starting transfers between devices  15.5 us (16%)
  waiting for transfers between devices  15.4 us (16%)
  local copies, waits for them, and re-layouts  12.3 us (13%)
  other arithmetic  5.3 us (5%)
    pallas_call x1, Pallas kernels, grid_stage(): pl.pallas_call(kernel, out_shape=jax.ShapeDtypeStruct((n_own, solves, gpt...  30.7 us
    pallas_call x2, Pallas kernels, update(): pl.pallas_call(make_update_kernel(margin, tile_scale), out_shape=jax.Shap...  18.4 us
    ppermute x6, starting transfers between devices, gather_slots(): lax.ppermute(x, axis, [(i, (i + s) % count) for i in range(count)])  9.84 us
    ppermute x6, waiting for transfers between devices, gather_slots(): lax.ppermute(x, axis, [(i, (i + s) % count) for i in range(count)])  8.01 us
    unnamed x41, local copies, waits for them, and re-layouts  6.1 us
    ppermute x1, waiting for transfers between devices, with_halo(): lax.ppermute(head, axis, [((i + 1) % count, i) for i in range(count)])  3.38 us
    ppermute x1, starting transfers between devices, body(): q2 = lax.ppermute(mine, pairs, q2_pairs)  2.34 us
  transfers between devices with their start and end apart: 12, of which 7 were waited for; matrix products, arithmetic and copies ran while one was open for 8% of the time, Pallas kernels for 0%

profile of v5, /device:TPU:9, one launch (start us, length us, event | category | flops | bytes accessed | tf_op | source)
XLA Modules:
  0.0 98.5 jit_solution(12207605516939173666)
XLA Ops:
  0.7 0.8 fusion.5
  3.4 2.5 %collective-permute-start.1 = (f32[32,5,128]{2,1,0:T(8,128)S(1)}, f32[32,5,128]{2,1,0:T(8,128)S(1)}, u32[]{:S(2)}, u32[]{:S(2)}) collective-permute-start(f32[32,5,128]{2,1,0:T(8,128)S(1)} %concatenate.35), channel_id=1, source_target_pairs={{0,8},{4,12},{8,0},{12,4},{1,9},{5,13},{9,1},{13,5},{2,10},{6,14},... | collective-permute-start | bytes 245768 | tf_op jit(solution)/shard_map/ppermute | solution.py:36
  5.8 2.2 %collective-permute-start = (f32[32,5,128]{2,1,0:T(8,128)S(1)}, f32[32,5,128]{2,1,0:T(8,128)S(1)}, u32[]{:S(2)}, u32[]{:S(2)}) collective-permute-start(f32[32,5,128]{2,1,0:T(8,128)S(1)} %concatenate.35), channel_id=1, source_target_pairs={{0,4},{4,8},{8,12},{12,0},{1,5},{5,9},{9,13},{13,1},{2,6},{6,10},{... | collective-permute-start | bytes 245768 | tf_op jit(solution)/shard_map/ppermute | solution.py:36
  8.7 0.7 broadcast_add_fusion
  9.5 1.5 %collective-permute-start.3 = (f32[16,8,128]{2,1,0:T(8,128)S(1)}, f32[16,8,128]{2,1,0:T(8,128)S(1)}, u32[]{:S(2)}, u32[]{:S(2)}) collective-permute-start(f32[16,8,128]{2,1,0:T(8,128)S(1)} %get-tuple-element.10), channel_id=1, source_target_pairs={{0,4},{4,8},{8,12},{12,0},{1,5},{5,9},{9,13},{13,1},{2,6},{6,10},{... | collective-permute-start | bytes 196616 | tf_op jit(solution)/shard_map/ppermute | solution.py:24
  13.0 0.7 broadcast_multiply_fusion.thr_ref
  16.0 3.4 %collective-permute-done.4 = f32[16,8,128]{2,1,0:T(8,128)S(1)} collective-permute-done((f32[16,8,128]{2,1,0:T(8,128)S(1)}, f32[16,8,128]{2,1,0:T(8,128)S(1)}, u32[]{:S(2)}, u32[]{:S(2)}) %collective-permute-start.4) | collective-permute-done | bytes 65568 | tf_op jit(solution)/shard_map/ppermute | solution.py:26
  19.6 0.7 pad_maximum_fusion.2.w_ref
  20.4 0.7 pad_maximum_fusion.1.halo_ref
  22.5 9.2 %shard_map.140 = f32[16,8,128]{2,1,0:T(8,128)} custom-call(s32[1]{0:T(128)} %bitcast.base_ref, s32[128]{0:T(128)} %reshape.139.cols_ref, f32[32,8,128]{2,1,0:T(8,128)} %copy-done.1, f32[64,8,128]{2,1,0:T(8,128)} %pad_maximum_fusion.1.halo_ref, f32[64,8,128]{2,1,0:T(8,128)} %pad_maximum_fusion.2.w_ref, f32[32,1,128]{2,1,0:T(1,128)} %bitcast.9, ...), custom_call_target="tpu_custom_call" | custom-call | tf_op jit(solution)/shard_map/pallas_call | solution.py:115
  31.7 1.2 %collective-permute-start.7 = (f32[16,8,128]{2,1,0:T(8,128)}, f32[16,8,128]{2,1,0:T(8,128)S(1)}, u32[]{:S(2)}, u32[]{:S(2)}) collective-permute-start(f32[16,8,128]{2,1,0:T(8,128)} %shard_map.140), channel_id=1, source_target_pairs={{0,1},{1,0},{4,5},{5,4},{8,9},{9,8},{12,13},{13,12},{2,3},{3,2},{6... | collective-permute-start | bytes 196616 | tf_op jit(solution)/shard_map/ppermute | solution.py:284
  33.5 2.3 %collective-permute-start.5 = (f32[16,8,128]{2,1,0:T(8,128)S(1)}, f32[16,8,128]{2,1,0:T(8,128)S(1)}, u32[]{:S(2)}, u32[]{:S(2)}) collective-permute-start(f32[16,8,128]{2,1,0:T(8,128)S(1)} %copy-done.5), channel_id=1, source_target_pairs={{0,13},{1,4},{4,1},{5,8},{8,5},{9,12},{12,9},{13,0},{2,15},{3,6},{... | collective-permute-start | bytes 196616 | tf_op jit(solution)/shard_map/ppermute | solution.py:296
  35.8 1.9 %collective-permute-done.5 = f32[16,8,128]{2,1,0:T(8,128)S(1)} collective-permute-done((f32[16,8,128]{2,1,0:T(8,128)S(1)}, f32[16,8,128]{2,1,0:T(8,128)S(1)}, u32[]{:S(2)}, u32[]{:S(2)}) %collective-permute-start.5) | collective-permute-done | bytes 65568 | tf_op jit(solution)/shard_map/ppermute | solution.py:296
  37.8 1.5 %collective-permute-done.6 = f32[16,8,128]{2,1,0:T(8,128)S(1)} collective-permute-done((f32[16,8,128]{2,1,0:T(8,128)S(1)}, f32[16,8,128]{2,1,0:T(8,128)S(1)}, u32[]{:S(2)}, u32[]{:S(2)}) %collective-permute-start.6) | collective-permute-done | bytes 65568 | tf_op jit(solution)/shard_map/ppermute | solution.py:295
  39.2 0.7 pad_maximum_fusion.3.w_ref
  40.0 9.2 %shard_map.141 = f32[16,8,128]{2,1,0:T(8,128)} custom-call(s32[1]{0:T(128)} %bitcast.base_ref, s32[128]{0:T(128)} %reshape.139.cols_ref, f32[32,8,128]{2,1,0:T(8,128)} %copy-done.1, f32[64,8,128]{2,1,0:T(8,128)} %pad_maximum_fusion.1.halo_ref, f32[64,8,128]{2,1,0:T(8,128)} %pad_maximum_fusion.3.w_ref, f32[32,1,128]{2,1,0:T(1,128)} %bitcast.10, ...), custom_call_target="tpu_custom_call" | custom-call | tf_op jit(solution)/shard_map/pallas_call | solution.py:115
  50.9 1.4 %collective-permute-start.9 = (f32[32,8,128]{2,1,0:T(8,128)S(1)}, f32[32,8,128]{2,1,0:T(8,128)S(1)}, u32[]{:S(2)}, u32[]{:S(2)}) collective-permute-start(f32[32,8,128]{2,1,0:T(8,128)S(1)} %get-tuple-element.5), channel_id=1, source_target_pairs={{0,4},{4,8},{8,12},{12,0},{1,5},{5,9},{9,13},{13,1},{2,6},{6,10},{... | collective-permute-start | bytes 393224 | tf_op jit(solution)/shard_map/ppermute | solution.py:36
  53.4 2.3 %collective-permute-start.10 = (f32[32,8,128]{2,1,0:T(8,128)S(1)}, f32[32,8,128]{2,1,0:T(8,128)S(1)}, u32[]{:S(2)}, u32[]{:S(2)}) collective-permute-start(f32[32,8,128]{2,1,0:T(8,128)S(1)} %get-tuple-element.5), channel_id=1, source_target_pairs={{0,8},{4,12},{8,0},{12,4},{1,9},{5,13},{9,1},{13,5},{2,10},{6,14},... | collective-permute-start | bytes 393224 | tf_op jit(solution)/shard_map/ppermute | solution.py:36
  56.7 0.8 concatenate.44.sites_ref
  57.5 1.5 %collective-permute-start.11 = (f32[32,8,128]{2,1,0:T(8,128)S(1)}, f32[32,8,128]{2,1,0:T(8,128)S(1)}, u32[]{:S(2)}, u32[]{:S(2)}) collective-permute-start(f32[32,8,128]{2,1,0:T(8,128)S(1)} %get-tuple-element.5), channel_id=1, source_target_pairs={{0,12},{4,0},{8,4},{12,8},{1,13},{5,1},{9,5},{13,9},{2,14},{6,2},{... | collective-permute-start | bytes 393224 | tf_op jit(solution)/shard_map/ppermute | solution.py:36
  59.0 4.8 %collective-permute-done.10 = f32[32,8,128]{2,1,0:T(8,128)S(1)} collective-permute-done((f32[32,8,128]{2,1,0:T(8,128)S(1)}, f32[32,8,128]{2,1,0:T(8,128)S(1)}, u32[]{:S(2)}, u32[]{:S(2)}) %collective-permute-start.10) | collective-permute-done | bytes 131104 | tf_op jit(solution)/shard_map/ppermute | solution.py:36
  63.7 3.2 %collective-permute-done.11 = f32[32,8,128]{2,1,0:T(8,128)S(1)} collective-permute-done((f32[32,8,128]{2,1,0:T(8,128)S(1)}, f32[32,8,128]{2,1,0:T(8,128)S(1)}, u32[]{:S(2)}, u32[]{:S(2)}) %collective-permute-start.11) | collective-permute-done | bytes 131104 | tf_op jit(solution)/shard_map/ppermute | solution.py:36
  67.0 0.8 copy-done.2
  67.9 30.7 %shard_map.142 = f32[4,8,512]{2,1,0:T(8,128)} custom-call(s32[1]{0:T(128)} %bitcast.8.me_ref, s32[4]{0:T(128)} %copy-done.12, s32[512]{0:T(512)} %convert_element_type.40.list_ref, f32[136,8,128]{2,1,0:T(8,128)} %concatenate.44.sites_ref, f32[136,8,128]{2,1,0:T(8,128)} %copy-done.2, f32[4,8,512]{2,1,0:T(8,128)} %stack.30.gsites_ref), custom_call_target="tpu_custom_call" | custom-call | tf_op jit(solution)/shard_map/pallas_call | solution.py:204
  (89 shorter events, 12.9 us)
Async XLA Ops:
  0.6 32.3 %copy-start = (f32[32,512]{1,0:T(8,128)S(1)}, f32[32,512]{1,0:T(8,128)}, u32[]{:S(2)}) copy-start(f32[32,512]{1,0:T(8,128)} %param.21) | copy-start | bytes 196612
  2.3 0.7 copy-start.10
  3.1 4.9 %copy-start.6 = (f32[32,128]{1,0:T(8,128)S(1)}, f32[32,128]{1,0:T(8,128)}, u32[]{:S(2)}) copy-start(f32[32,128]{1,0:T(8,128)} %param.16) | copy-start | bytes 49156
  3.3 4.8 %copy-start.9 = (f32[32,128]{1,0:T(8,128)S(1)}, f32[32,128]{1,0:T(8,128)}, u32[]{:S(2)}) copy-start(f32[32,128]{1,0:T(8,128)} %param.15) | copy-start | bytes 49156
  3.3 4.8 %copy-start.11 = (s32[32]{0:T(128)S(1)}, s32[32]{0:T(128)}, u32[]{:S(2)}) copy-start(s32[32]{0:T(128)} %param.17) | copy-start | bytes 388
  3.3 17.0 %collective-permute-start.2 = (f32[32,5,128]{2,1,0:T(8,128)S(1)}, f32[32,5,128]{2,1,0:T(8,128)S(1)}, u32[]{:S(2)}, u32[]{:S(2)}) collective-permute-start(f32[32,5,128]{2,1,0:T(8,128)S(1)} %concatenate.35), channel_id=1, source_target_pairs={{0,12},{4,0},{8,4},{12,8},{1,13},{5,1},{9,5},{13,9},{2,14},{6,2},{... | collective-permute-start | bytes 245768 | tf_op jit(solution)/shard_map/ppermute | solution.py:36
  3.4 16.9 %collective-permute-start.1 = (f32[32,5,128]{2,1,0:T(8,128)S(1)}, f32[32,5,128]{2,1,0:T(8,128)S(1)}, u32[]{:S(2)}, u32[]{:S(2)}) collective-permute-start(f32[32,5,128]{2,1,0:T(8,128)S(1)} %concatenate.35), channel_id=1, source_target_pairs={{0,8},{4,12},{8,0},{12,4},{1,9},{5,13},{9,1},{13,5},{2,10},{6,14},... | collective-permute-start | bytes 245768 | tf_op jit(solution)/shard_map/ppermute | solution.py:36
  5.8 14.5 %collective-permute-start = (f32[32,5,128]{2,1,0:T(8,128)S(1)}, f32[32,5,128]{2,1,0:T(8,128)S(1)}, u32[]{:S(2)}, u32[]{:S(2)}) collective-permute-start(f32[32,5,128]{2,1,0:T(8,128)S(1)} %concatenate.35), channel_id=1, source_target_pairs={{0,4},{4,8},{8,12},{12,0},{1,5},{5,9},{9,13},{13,1},{2,6},{6,10},{... | collective-permute-start | bytes 245768 | tf_op jit(solution)/shard_map/ppermute | solution.py:36
  8.7 0.7 copy-start.3
  9.5 9.9 %collective-permute-start.4 = (f32[16,8,128]{2,1,0:T(8,128)S(1)}, f32[16,8,128]{2,1,0:T(8,128)S(1)}, u32[]{:S(2)}, u32[]{:S(2)}) collective-permute-start(f32[16,8,128]{2,1,0:T(8,128)S(1)} %get-tuple-element.11), channel_id=1, source_target_pairs={{4,0},{8,4},{12,8},{0,12},{5,1},{9,5},{13,9},{1,13},{6,2},{10,6},{... | collective-permute-start | bytes 196616 | tf_op jit(solution)/shard_map/ppermute | solution.py:26
  9.5 10.0 %collective-permute-start.3 = (f32[16,8,128]{2,1,0:T(8,128)S(1)}, f32[16,8,128]{2,1,0:T(8,128)S(1)}, u32[]{:S(2)}, u32[]{:S(2)}) collective-permute-start(f32[16,8,128]{2,1,0:T(8,128)S(1)} %get-tuple-element.10), channel_id=1, source_target_pairs={{0,4},{4,8},{8,12},{12,0},{1,5},{5,9},{9,13},{13,1},{2,6},{6,10},{... | collective-permute-start | bytes 196616 | tf_op jit(solution)/shard_map/ppermute | solution.py:24
  16.0 4.4 %copy-start.1 = (f32[32,8,128]{2,1,0:T(8,128)}, f32[32,8,128]{2,1,0:T(8,128)S(1)}, u32[]{:S(2)}) copy-start(f32[32,8,128]{2,1,0:T(8,128)S(1)} %stack.28.own_ref) | copy-start | bytes 393220
  31.7 1.8 %copy-start.5 = (f32[16,8,128]{2,1,0:T(8,128)S(1)}, f32[16,8,128]{2,1,0:T(8,128)}, u32[]{:S(2)}) copy-start(f32[16,8,128]{2,1,0:T(8,128)} %shard_map.140) | copy-start | bytes 196612
  31.7 4.2 %collective-permute-start.7 = (f32[16,8,128]{2,1,0:T(8,128)}, f32[16,8,128]{2,1,0:T(8,128)S(1)}, u32[]{:S(2)}, u32[]{:S(2)}) collective-permute-start(f32[16,8,128]{2,1,0:T(8,128)} %shard_map.140), channel_id=1, source_target_pairs={{0,1},{1,0},{4,5},{5,4},{8,9},{9,8},{12,13},{13,12},{2,3},{3,2},{6... | collective-permute-start | bytes 196616 | tf_op jit(solution)/shard_map/ppermute | solution.py:284
  33.5 4.3 %collective-permute-start.5 = (f32[16,8,128]{2,1,0:T(8,128)S(1)}, f32[16,8,128]{2,1,0:T(8,128)S(1)}, u32[]{:S(2)}, u32[]{:S(2)}) collective-permute-start(f32[16,8,128]{2,1,0:T(8,128)S(1)} %copy-done.5), channel_id=1, source_target_pairs={{0,13},{1,4},{4,1},{5,8},{8,5},{9,12},{12,9},{13,0},{2,15},{3,6},{... | collective-permute-start | bytes 196616 | tf_op jit(solution)/shard_map/ppermute | solution.py:296
  35.8 3.4 %collective-permute-start.6 = (f32[16,8,128]{2,1,0:T(8,128)S(1)}, f32[16,8,128]{2,1,0:T(8,128)S(1)}, u32[]{:S(2)}, u32[]{:S(2)}) collective-permute-start(f32[16,8,128]{2,1,0:T(8,128)S(1)} %copy-done.5), channel_id=1, source_target_pairs={{0,12},{1,5},{4,0},{5,9},{8,4},{9,13},{12,8},{13,1},{2,14},{3,7},{... | collective-permute-start | bytes 196616 | tf_op jit(solution)/shard_map/ppermute | solution.py:295
  40.0 9.9 %copy-start.8 = (f32[32,512]{1,0:T(8,128)S(1)}, f32[32,512]{1,0:T(8,128)}, u32[]{:S(2)}) copy-start(f32[32,512]{1,0:T(8,128)} %param.22) | copy-start | bytes 196612
  49.2 1.7 %copy-start.4 = (f32[16,8,128]{2,1,0:T(8,128)S(1)}, f32[16,8,128]{2,1,0:T(8,128)}, u32[]{:S(2)}) copy-start(f32[16,8,128]{2,1,0:T(8,128)} %shard_map.141) | copy-start | bytes 196612
  49.2 1.7 %collective-permute-start.8 = (f32[16,8,128]{2,1,0:T(8,128)}, f32[16,8,128]{2,1,0:T(8,128)S(1)}, u32[]{:S(2)}, u32[]{:S(2)}) collective-permute-start(f32[16,8,128]{2,1,0:T(8,128)} %shard_map.141), channel_id=1, source_target_pairs={{0,1},{1,0},{4,5},{5,4},{8,9},{9,8},{12,13},{13,12},{2,3},{3,2},{6... | collective-permute-start | bytes 196616 | tf_op jit(solution)/shard_map/ppermute | solution.py:284
  50.9 6.6 %copy-start.7 = (f32[32,8,128]{2,1,0:T(8,128)}, f32[32,8,128]{2,1,0:T(8,128)S(1)}, u32[]{:S(2)}) copy-start(f32[32,8,128]{2,1,0:T(8,128)S(1)} %get-tuple-element.5) | copy-start | bytes 393220
  50.9 8.0 %collective-permute-start.9 = (f32[32,8,128]{2,1,0:T(8,128)S(1)}, f32[32,8,128]{2,1,0:T(8,128)S(1)}, u32[]{:S(2)}, u32[]{:S(2)}) collective-permute-start(f32[32,8,128]{2,1,0:T(8,128)S(1)} %get-tuple-element.5), channel_id=1, source_target_pairs={{0,4},{4,8},{8,12},{12,0},{1,5},{5,9},{9,13},{13,1},{2,6},{6,10},{... | collective-permute-start | bytes 393224 | tf_op jit(solution)/shard_map/ppermute | solution.py:36
  53.4 10.3 %collective-permute-start.10 = (f32[32,8,128]{2,1,0:T(8,128)S(1)}, f32[32,8,128]{2,1,0:T(8,128)S(1)}, u32[]{:S(2)}, u32[]{:S(2)}) collective-permute-start(f32[32,8,128]{2,1,0:T(8,128)S(1)} %get-tuple-element.5), channel_id=1, source_target_pairs={{0,8},{4,12},{8,0},{12,4},{1,9},{5,13},{9,1},{13,5},{2,10},{6,14},... | collective-permute-start | bytes 393224 | tf_op jit(solution)/shard_map/ppermute | solution.py:36
  57.5 9.5 %collective-permute-start.11 = (f32[32,8,128]{2,1,0:T(8,128)S(1)}, f32[32,8,128]{2,1,0:T(8,128)S(1)}, u32[]{:S(2)}, u32[]{:S(2)}) collective-permute-start(f32[32,8,128]{2,1,0:T(8,128)S(1)} %get-tuple-element.5), channel_id=1, source_target_pairs={{0,12},{4,0},{8,4},{12,8},{1,13},{5,1},{9,5},{13,9},{2,14},{6,2},{... | collective-permute-start | bytes 393224 | tf_op jit(solution)/shard_map/ppermute | solution.py:36
  67.0 0.8 copy-start.2
  (7 other events, 4.6 us)

commit v6 on v1

--- a/solution.py
+++ b/solution.py
@@ -11,6 +11,7 @@
 DECAY_RATE = 1.0 / 0.15
 FULL_TURN = 6.283185307179586
 HIGHEST = lax.Precision.HIGHEST
+MATMUL_PRECISION = lax.Precision.HIGH
 ROWS = 8
 GROUP = 4
 
@@ -56,7 +57,7 @@
 
 def contract_lanes(w, c):
     return lax.dot_general(
-        w, c, (((1,), (1,)), ((), ())), precision=HIGHEST, preferred_element_type=jnp.float32
+        w, c, (((1,), (1,)), ((), ())), precision=MATMUL_PRECISION, preferred_element_type=jnp.float32
     )
 
 

time: 98.2 us -> 90 us (0.916)
  Pallas kernels: 45.9 us -> 38.3 us
    pallas_call x1, Pallas kernels: 27.5 us -> 23.6 us  [grid_stage(): pl.pallas_call(kernel, out_shape=jax.ShapeDtypeStruct((n_own, solves, gpt...]
    pallas_call x2, Pallas kernels: 18.4 us -> 14.7 us  [update(): pl.pallas_call(make_update_kernel(margin, tile_scale), out_shape=jax.Shap...]
  transfers between devices with their start and end apart: 12 -> 12, of which waited for: 9 -> 9; matrix products, arithmetic and copies ran while one was open for 8% -> 9% of each run, Pallas kernels for 0% -> 0%
where the time goes in v6:
time: 90 us; the launch traced here: 89 us
  Pallas kernels  38.3 us (43%)
  starting transfers between devices  19.6 us (22%)
  local copies, waits for them, and re-layouts  12.5 us (14%)
  waiting for transfers between devices  12.4 us (14%)
  other arithmetic  5.3 us (6%)
  between operations  0.91 us (1%)
    pallas_call x1, Pallas kernels, grid_stage(): pl.pallas_call(kernel, out_shape=jax.ShapeDtypeStruct((n_own, solves, gpt...  23.6 us
    pallas_call x2, Pallas kernels, update(): pl.pallas_call(make_update_kernel(margin, tile_scale), out_shape=jax.Shap...  14.7 us
    ppermute x6, starting transfers between devices, gather_slots(): lax.ppermute(x, axis, [(i, (i + s) % count) for i in range(count)])  11.1 us
    ppermute x6, waiting for transfers between devices, gather_slots(): lax.ppermute(x, axis, [(i, (i + s) % count) for i in range(count)])  8.03 us
    unnamed x41, local copies, waits for them, and re-layouts  6.34 us
    ppermute x1, starting transfers between devices, body(): q1 = lax.ppermute(mine, pairs, q1_pairs)  3.19 us
    ppermute x1, starting transfers between devices, with_halo(): lax.ppermute(head, axis, [((i + 1) % count, i) for i in range(count)])  2.87 us
    ppermute x1, starting transfers between devices, body(): q2 = lax.ppermute(mine, pairs, q2_pairs)  2.2 us
  transfers between devices with their start and end apart: 12, of which 9 were waited for; matrix products, arithmetic and copies ran while one was open for 9% of the time, Pallas kernels for 0%

profile of v6, /device:TPU:0, one launch (start us, length us, event | category | flops | bytes accessed | tf_op | source)
XLA Modules:
  0.0 89.0 jit_solution(2167564168852307016)
XLA Ops:
  0.7 0.8 fusion.5
  3.3 5.1 %collective-permute-start.2 = (f32[32,5,128]{2,1,0:T(8,128)S(1)}, f32[32,5,128]{2,1,0:T(8,128)S(1)}, u32[]{:S(2)}, u32[]{:S(2)}) collective-permute-start(f32[32,5,128]{2,1,0:T(8,128)S(1)} %concatenate.35), channel_id=1, source_target_pairs={{0,12},{4,0},{8,4},{12,8},{1,13},{5,1},{9,5},{13,9},{2,14},{6,2},{... | collective-permute-start | bytes 245768 | tf_op jit(solution)/shard_map/ppermute | solution.py:37
  8.4 1.0 %collective-permute-start = (f32[32,5,128]{2,1,0:T(8,128)S(1)}, f32[32,5,128]{2,1,0:T(8,128)S(1)}, u32[]{:S(2)}, u32[]{:S(2)}) collective-permute-start(f32[32,5,128]{2,1,0:T(8,128)S(1)} %concatenate.35), channel_id=1, source_target_pairs={{0,4},{4,8},{8,12},{12,0},{1,5},{5,9},{9,13},{13,1},{2,6},{6,10},{... | collective-permute-start | bytes 245768 | tf_op jit(solution)/shard_map/ppermute | solution.py:37
  10.1 0.7 broadcast_add_fusion
  10.9 2.9 %collective-permute-start.4 = (f32[16,8,128]{2,1,0:T(8,128)S(1)}, f32[16,8,128]{2,1,0:T(8,128)S(1)}, u32[]{:S(2)}, u32[]{:S(2)}) collective-permute-start(f32[16,8,128]{2,1,0:T(8,128)S(1)} %get-tuple-element.11), channel_id=1, source_target_pairs={{4,0},{8,4},{12,8},{0,12},{5,1},{9,5},{13,9},{1,13},{6,2},{10,6},{... | collective-permute-start | bytes 196616 | tf_op jit(solution)/shard_map/ppermute | solution.py:27
  15.8 0.7 broadcast_multiply_fusion.thr_ref
  18.8 1.1 %collective-permute-done.4 = f32[16,8,128]{2,1,0:T(8,128)S(1)} collective-permute-done((f32[16,8,128]{2,1,0:T(8,128)S(1)}, f32[16,8,128]{2,1,0:T(8,128)S(1)}, u32[]{:S(2)}, u32[]{:S(2)}) %collective-permute-start.4) | collective-permute-done | bytes 65568 | tf_op jit(solution)/shard_map/ppermute | solution.py:27
  19.8 0.7 collective-permute-done.3
  20.6 0.7 pad_maximum_fusion.2.w_ref
  21.9 0.7 pad_maximum_fusion.1.halo_ref
  24.0 7.3 %shard_map.140 = f32[16,8,128]{2,1,0:T(8,128)} custom-call(s32[1]{0:T(128)} %bitcast.base_ref, s32[128]{0:T(128)} %reshape.139.cols_ref, f32[32,8,128]{2,1,0:T(8,128)} %copy-done.1, f32[64,8,128]{2,1,0:T(8,128)} %pad_maximum_fusion.1.halo_ref, f32[64,8,128]{2,1,0:T(8,128)} %pad_maximum_fusion.2.w_ref, f32[32,1,128]{2,1,0:T(1,128)} %bitcast.9, ...), custom_call_target="tpu_custom_call" | custom-call | tf_op jit(solution)/shard_map/pallas_call | solution.py:116
  32.2 2.2 %collective-permute-start.5 = (f32[16,8,128]{2,1,0:T(8,128)S(1)}, f32[16,8,128]{2,1,0:T(8,128)S(1)}, u32[]{:S(2)}, u32[]{:S(2)}) collective-permute-start(f32[16,8,128]{2,1,0:T(8,128)S(1)} %copy-done.5), channel_id=1, source_target_pairs={{0,13},{1,4},{4,1},{5,8},{8,5},{9,12},{12,9},{13,0},{2,15},{3,6},{... | collective-permute-start | bytes 196616 | tf_op jit(solution)/shard_map/ppermute | solution.py:297
  34.4 3.2 %collective-permute-start.6 = (f32[16,8,128]{2,1,0:T(8,128)S(1)}, f32[16,8,128]{2,1,0:T(8,128)S(1)}, u32[]{:S(2)}, u32[]{:S(2)}) collective-permute-start(f32[16,8,128]{2,1,0:T(8,128)S(1)} %copy-done.5), channel_id=1, source_target_pairs={{0,12},{1,5},{4,0},{5,9},{8,4},{9,13},{12,8},{13,1},{2,14},{3,7},{... | collective-permute-start | bytes 196616 | tf_op jit(solution)/shard_map/ppermute | solution.py:296
  37.6 1.8 %collective-permute-done.6 = f32[16,8,128]{2,1,0:T(8,128)S(1)} collective-permute-done((f32[16,8,128]{2,1,0:T(8,128)S(1)}, f32[16,8,128]{2,1,0:T(8,128)S(1)}, u32[]{:S(2)}, u32[]{:S(2)}) %collective-permute-start.6) | collective-permute-done | bytes 65568 | tf_op jit(solution)/shard_map/ppermute | solution.py:296
  39.5 0.7 pad_maximum_fusion.3.w_ref
  40.2 7.4 %shard_map.141 = f32[16,8,128]{2,1,0:T(8,128)} custom-call(s32[1]{0:T(128)} %bitcast.base_ref, s32[128]{0:T(128)} %reshape.139.cols_ref, f32[32,8,128]{2,1,0:T(8,128)} %copy-done.1, f32[64,8,128]{2,1,0:T(8,128)} %pad_maximum_fusion.1.halo_ref, f32[64,8,128]{2,1,0:T(8,128)} %pad_maximum_fusion.3.w_ref, f32[32,1,128]{2,1,0:T(1,128)} %bitcast.10, ...), custom_call_target="tpu_custom_call" | custom-call | tf_op jit(solution)/shard_map/pallas_call | solution.py:116
  49.1 0.9 %collective-permute-start.9 = (f32[32,8,128]{2,1,0:T(8,128)S(1)}, f32[32,8,128]{2,1,0:T(8,128)S(1)}, u32[]{:S(2)}, u32[]{:S(2)}) collective-permute-start(f32[32,8,128]{2,1,0:T(8,128)S(1)} %get-tuple-element.5), channel_id=1, source_target_pairs={{0,4},{4,8},{8,12},{12,0},{1,5},{5,9},{9,13},{13,1},{2,6},{6,10},{... | collective-permute-start | bytes 393224 | tf_op jit(solution)/shard_map/ppermute | solution.py:37
  51.1 3.9 %collective-permute-start.10 = (f32[32,8,128]{2,1,0:T(8,128)S(1)}, f32[32,8,128]{2,1,0:T(8,128)S(1)}, u32[]{:S(2)}, u32[]{:S(2)}) collective-permute-start(f32[32,8,128]{2,1,0:T(8,128)S(1)} %get-tuple-element.5), channel_id=1, source_target_pairs={{0,8},{4,12},{8,0},{12,4},{1,9},{5,13},{9,1},{13,5},{2,10},{6,14},... | collective-permute-start | bytes 393224 | tf_op jit(solution)/shard_map/ppermute | solution.py:37
  56.0 0.8 concatenate.44.sites_ref
  57.0 0.8 collective-permute-done.9
  57.7 5.1 %collective-permute-done.10 = f32[32,8,128]{2,1,0:T(8,128)S(1)} collective-permute-done((f32[32,8,128]{2,1,0:T(8,128)S(1)}, f32[32,8,128]{2,1,0:T(8,128)S(1)}, u32[]{:S(2)}, u32[]{:S(2)}) %collective-permute-start.10) | collective-permute-done | bytes 131104 | tf_op jit(solution)/shard_map/ppermute | solution.py:37
  62.8 1.7 %collective-permute-done.11 = f32[32,8,128]{2,1,0:T(8,128)S(1)} collective-permute-done((f32[32,8,128]{2,1,0:T(8,128)S(1)}, f32[32,8,128]{2,1,0:T(8,128)S(1)}, u32[]{:S(2)}, u32[]{:S(2)}) %collective-permute-start.11) | collective-permute-done | bytes 131104 | tf_op jit(solution)/shard_map/ppermute | solution.py:37
  64.5 0.8 copy-done.2
  65.4 23.6 %shard_map.142 = f32[4,8,512]{2,1,0:T(8,128)} custom-call(s32[1]{0:T(128)} %bitcast.8.me_ref, s32[4]{0:T(128)} %copy-done.12, s32[512]{0:T(512)} %convert_element_type.40.list_ref, f32[136,8,128]{2,1,0:T(8,128)} %concatenate.44.sites_ref, f32[136,8,128]{2,1,0:T(8,128)} %copy-done.2, f32[4,8,512]{2,1,0:T(8,128)} %stack.30.gsites_ref), custom_call_target="tpu_custom_call" | custom-call | tf_op jit(solution)/shard_map/pallas_call | solution.py:205
  (89 shorter events, 13.3 us)
Async XLA Ops:
  0.6 30.7 %copy-start = (f32[32,512]{1,0:T(8,128)S(1)}, f32[32,512]{1,0:T(8,128)}, u32[]{:S(2)}) copy-start(f32[32,512]{1,0:T(8,128)} %param.21) | copy-start | bytes 196612
  2.3 0.7 copy-start.10
  3.1 6.3 %copy-start.6 = (f32[32,128]{1,0:T(8,128)S(1)}, f32[32,128]{1,0:T(8,128)}, u32[]{:S(2)}) copy-start(f32[32,128]{1,0:T(8,128)} %param.16) | copy-start | bytes 49156
  3.3 6.2 %copy-start.9 = (f32[32,128]{1,0:T(8,128)S(1)}, f32[32,128]{1,0:T(8,128)}, u32[]{:S(2)}) copy-start(f32[32,128]{1,0:T(8,128)} %param.15) | copy-start | bytes 49156
  3.3 6.2 %copy-start.11 = (s32[32]{0:T(128)S(1)}, s32[32]{0:T(128)}, u32[]{:S(2)}) copy-start(s32[32]{0:T(128)} %param.17) | copy-start | bytes 388
  3.3 18.0 %collective-permute-start.2 = (f32[32,5,128]{2,1,0:T(8,128)S(1)}, f32[32,5,128]{2,1,0:T(8,128)S(1)}, u32[]{:S(2)}, u32[]{:S(2)}) collective-permute-start(f32[32,5,128]{2,1,0:T(8,128)S(1)} %concatenate.35), channel_id=1, source_target_pairs={{0,12},{4,0},{8,4},{12,8},{1,13},{5,1},{9,5},{13,9},{2,14},{6,2},{... | collective-permute-start | bytes 245768 | tf_op jit(solution)/shard_map/ppermute | solution.py:37
  8.4 13.4 %collective-permute-start.1 = (f32[32,5,128]{2,1,0:T(8,128)S(1)}, f32[32,5,128]{2,1,0:T(8,128)S(1)}, u32[]{:S(2)}, u32[]{:S(2)}) collective-permute-start(f32[32,5,128]{2,1,0:T(8,128)S(1)} %concatenate.35), channel_id=1, source_target_pairs={{0,8},{4,12},{8,0},{12,4},{1,9},{5,13},{9,1},{13,5},{2,10},{6,14},... | collective-permute-start | bytes 245768 | tf_op jit(solution)/shard_map/ppermute | solution.py:37
  8.4 13.4 %collective-permute-start = (f32[32,5,128]{2,1,0:T(8,128)S(1)}, f32[32,5,128]{2,1,0:T(8,128)S(1)}, u32[]{:S(2)}, u32[]{:S(2)}) collective-permute-start(f32[32,5,128]{2,1,0:T(8,128)S(1)} %concatenate.35), channel_id=1, source_target_pairs={{0,4},{4,8},{8,12},{12,0},{1,5},{5,9},{9,13},{13,1},{2,6},{6,10},{... | collective-permute-start | bytes 245768 | tf_op jit(solution)/shard_map/ppermute | solution.py:37
  10.1 0.7 copy-start.3
  10.9 8.9 %collective-permute-start.4 = (f32[16,8,128]{2,1,0:T(8,128)S(1)}, f32[16,8,128]{2,1,0:T(8,128)S(1)}, u32[]{:S(2)}, u32[]{:S(2)}) collective-permute-start(f32[16,8,128]{2,1,0:T(8,128)S(1)} %get-tuple-element.11), channel_id=1, source_target_pairs={{4,0},{8,4},{12,8},{0,12},{5,1},{9,5},{13,9},{1,13},{6,2},{10,6},{... | collective-permute-start | bytes 196616 | tf_op jit(solution)/shard_map/ppermute | solution.py:27
  13.7 6.8 %collective-permute-start.3 = (f32[16,8,128]{2,1,0:T(8,128)S(1)}, f32[16,8,128]{2,1,0:T(8,128)S(1)}, u32[]{:S(2)}, u32[]{:S(2)}) collective-permute-start(f32[16,8,128]{2,1,0:T(8,128)S(1)} %get-tuple-element.10), channel_id=1, source_target_pairs={{0,4},{4,8},{8,12},{12,0},{1,5},{5,9},{9,13},{13,1},{2,6},{6,10},{... | collective-permute-start | bytes 196616 | tf_op jit(solution)/shard_map/ppermute | solution.py:25
  18.8 3.2 %copy-start.1 = (f32[32,8,128]{2,1,0:T(8,128)}, f32[32,8,128]{2,1,0:T(8,128)S(1)}, u32[]{:S(2)}) copy-start(f32[32,8,128]{2,1,0:T(8,128)S(1)} %stack.28.own_ref) | copy-start | bytes 393220
  31.3 0.8 copy-start.5
  31.3 6.2 %collective-permute-start.7 = (f32[16,8,128]{2,1,0:T(8,128)}, f32[16,8,128]{2,1,0:T(8,128)S(1)}, u32[]{:S(2)}, u32[]{:S(2)}) collective-permute-start(f32[16,8,128]{2,1,0:T(8,128)} %shard_map.140), channel_id=1, source_target_pairs={{0,1},{1,0},{4,5},{5,4},{8,9},{9,8},{12,13},{13,12},{2,3},{3,2},{6... | collective-permute-start | bytes 196616 | tf_op jit(solution)/shard_map/ppermute | solution.py:285
  32.2 5.5 %collective-permute-start.5 = (f32[16,8,128]{2,1,0:T(8,128)S(1)}, f32[16,8,128]{2,1,0:T(8,128)S(1)}, u32[]{:S(2)}, u32[]{:S(2)}) collective-permute-start(f32[16,8,128]{2,1,0:T(8,128)S(1)} %copy-done.5), channel_id=1, source_target_pairs={{0,13},{1,4},{4,1},{5,8},{8,5},{9,12},{12,9},{13,0},{2,15},{3,6},{... | collective-permute-start | bytes 196616 | tf_op jit(solution)/shard_map/ppermute | solution.py:297
  34.4 5.1 %collective-permute-start.6 = (f32[16,8,128]{2,1,0:T(8,128)S(1)}, f32[16,8,128]{2,1,0:T(8,128)S(1)}, u32[]{:S(2)}, u32[]{:S(2)}) collective-permute-start(f32[16,8,128]{2,1,0:T(8,128)S(1)} %copy-done.5), channel_id=1, source_target_pairs={{0,12},{1,5},{4,0},{5,9},{8,4},{9,13},{12,8},{13,1},{2,14},{3,7},{... | collective-permute-start | bytes 196616 | tf_op jit(solution)/shard_map/ppermute | solution.py:296
  40.2 7.6 %copy-start.8 = (f32[32,512]{1,0:T(8,128)S(1)}, f32[32,512]{1,0:T(8,128)}, u32[]{:S(2)}) copy-start(f32[32,512]{1,0:T(8,128)} %param.22) | copy-start | bytes 196612
  47.6 1.5 %copy-start.4 = (f32[16,8,128]{2,1,0:T(8,128)S(1)}, f32[16,8,128]{2,1,0:T(8,128)}, u32[]{:S(2)}) copy-start(f32[16,8,128]{2,1,0:T(8,128)} %shard_map.141) | copy-start | bytes 196612
  47.6 1.5 %collective-permute-start.8 = (f32[16,8,128]{2,1,0:T(8,128)}, f32[16,8,128]{2,1,0:T(8,128)S(1)}, u32[]{:S(2)}, u32[]{:S(2)}) collective-permute-start(f32[16,8,128]{2,1,0:T(8,128)} %shard_map.141), channel_id=1, source_target_pairs={{0,1},{1,0},{4,5},{5,4},{8,9},{9,8},{12,13},{13,12},{2,3},{3,2},{6... | collective-permute-start | bytes 196616 | tf_op jit(solution)/shard_map/ppermute | solution.py:285
  49.0 7.7 %copy-start.7 = (f32[32,8,128]{2,1,0:T(8,128)}, f32[32,8,128]{2,1,0:T(8,128)S(1)}, u32[]{:S(2)}) copy-start(f32[32,8,128]{2,1,0:T(8,128)S(1)} %get-tuple-element.5) | copy-start | bytes 393220
  49.1 8.7 %collective-permute-start.9 = (f32[32,8,128]{2,1,0:T(8,128)S(1)}, f32[32,8,128]{2,1,0:T(8,128)S(1)}, u32[]{:S(2)}, u32[]{:S(2)}) collective-permute-start(f32[32,8,128]{2,1,0:T(8,128)S(1)} %get-tuple-element.5), channel_id=1, source_target_pairs={{0,4},{4,8},{8,12},{12,0},{1,5},{5,9},{9,13},{13,1},{2,6},{6,10},{... | collective-permute-start | bytes 393224 | tf_op jit(solution)/shard_map/ppermute | solution.py:37
  51.1 11.7 %collective-permute-start.10 = (f32[32,8,128]{2,1,0:T(8,128)S(1)}, f32[32,8,128]{2,1,0:T(8,128)S(1)}, u32[]{:S(2)}, u32[]{:S(2)}) collective-permute-start(f32[32,8,128]{2,1,0:T(8,128)S(1)} %get-tuple-element.5), channel_id=1, source_target_pairs={{0,8},{4,12},{8,0},{12,4},{1,9},{5,13},{9,1},{13,5},{2,10},{6,14},... | collective-permute-start | bytes 393224 | tf_op jit(solution)/shard_map/ppermute | solution.py:37
  56.8 7.7 %collective-permute-start.11 = (f32[32,8,128]{2,1,0:T(8,128)S(1)}, f32[32,8,128]{2,1,0:T(8,128)S(1)}, u32[]{:S(2)}, u32[]{:S(2)}) collective-permute-start(f32[32,8,128]{2,1,0:T(8,128)S(1)} %get-tuple-element.5), channel_id=1, source_target_pairs={{0,12},{4,0},{8,4},{12,8},{1,13},{5,1},{9,5},{13,9},{2,14},{6,2},{... | collective-permute-start | bytes 393224 | tf_op jit(solution)/shard_map/ppermute | solution.py:37
  64.5 0.8 copy-start.2
  (7 other events, 4.6 us)

commit v7 on v6

--- a/solution.py
+++ b/solution.py
@@ -61,36 +61,69 @@
     )
 
 
-def make_update_kernel(margin, tile_scale):
-    def update_kernel(
-        base_ref, cols_ref, own_ref, halo_ref, w_ref, obs_ref, diag_ref, thr_ref, live_ref,
-        step_ref, out_ref, buf0, buf1,
-    ):
+def make_update_kernel(margin, tile_scale, regions, first_sweep):
+    def update_kernel(scal_ref, tc_ref, sizes_ref, ridge_ref, huber_ref, step_ref, *refs):
+        if first_sweep:
+            own_ref, sl_ref, sr_ref, innov_ref, err_ref, wl_ref, wo_ref, wr_ref = refs[:8]
+        else:
+            own_ref, sl_ref, sr_ref, innov_ref, err_ref, q1_ref, q2_ref, mine_ref, other_ref = refs[:9]
+        out_ref, buf0, buf1, hs_ref, hw_ref = refs[-5:]
         reg_dev, _, cap = own_ref.shape
-        count = out_ref.shape[0]
-        tiles = cols_ref.shape[0] // reg_dev
-        base = base_ref[0]
+        count, solves, _ = out_ref.shape
+        tiles = tc_ref.shape[1]
+        base = scal_ref[0]
+        first_row = scal_ref[1]
+
+        hs_ref[0:margin] = sl_ref[...]
+        hs_ref[margin : margin + reg_dev] = own_ref[...]
+        hs_ref[margin + reg_dev :] = sr_ref[...]
+        if first_sweep:
+            hw_ref[0:margin] = wl_ref[...]
+            hw_ref[margin : margin + reg_dev] = wo_ref[...]
+            hw_ref[margin + reg_dev :] = wr_ref[...]
+        else:
+            sel = scal_ref[2] == 1
+            q1 = q1_ref[...]
+            q2 = q2_ref[...]
+            mine = mine_ref[...]
+            other = other_ref[...]
+            hw_ref[0:margin] = jnp.where(sel, q2, q1)
+            hw_ref[margin : margin + count] = jnp.where(sel, mine, other)
+            hw_ref[margin + count : margin + 2 * count] = jnp.where(sel, other, mine)
+            hw_ref[margin + reg_dev :] = jnp.where(sel, q1, q2)
+
+        rows = lax.broadcasted_iota(jnp.int32, (solves, cap), 0)
+        ridge_b = jnp.zeros((solves, cap), jnp.float32)
+        huber_b = jnp.zeros((solves, cap), jnp.float32)
+        step_b = jnp.zeros((solves, cap), jnp.float32)
+        for k in range(solves):
+            ridge_b = jnp.where(rows == k, ridge_ref[k], ridge_b)
+            huber_b = jnp.where(rows == k, huber_ref[k], huber_b)
+            step_b = jnp.where(rows == k, step_ref[k], step_b)
+        lanes = lax.broadcasted_iota(jnp.int32, (1, cap), 1)
+
+        def column(a, t):
+            return lax.rem(tc_ref[a, t] - first_row + margin + regions, regions)
 
         def fill(i, buf):
             a = i + base
             own_t = own_ref[a].T
             for t in range(tiles):
-                b = cols_ref[a * tiles + t]
-                buf[:, t * cap : (t + 1) * cap] = corr_block(own_t, halo_ref[b])
+                buf[:, t * cap : (t + 1) * cap] = corr_block(own_t, hs_ref[column(a, t)])
 
         def use(i, buf):
             a = i + base
-            weights = jnp.concatenate(
-                [w_ref[cols_ref[a * tiles + t]] for t in range(tiles)], axis=1
-            )
+            weights = jnp.concatenate([hw_ref[column(a, t)] for t in range(tiles)], axis=1)
             cov = contract_lanes(weights, buf[...])
-            current = w_ref[a + margin]
-            diag = diag_ref[a]
-            thr = thr_ref[a]
+            current = hw_ref[a + margin]
+            err = err_ref[pl.ds(a, 1), :]
+            live = (lanes < sizes_ref[a]).astype(jnp.float32)
+            diag = err * err + ridge_b
+            thr = huber_b * err
             applied = cov * tile_scale + diag * current
-            residual = (obs_ref[a] - applied) * live_ref[a]
+            residual = (innov_ref[pl.ds(a, 1), :] * live - applied) * live
             factor = thr / jnp.maximum(jnp.abs(residual), thr)
-            out_ref[i] = current + step_ref[...] * factor * residual / diag
+            out_ref[i] = current + step_b * factor * residual / diag
 
         fill(0, buf0)
 
@@ -107,19 +140,27 @@
     return update_kernel
 
 
-def update(base, count, cols, own_sites, halo_sites, halo_w, observed, diagonal, threshold, live, step, margin, tile_scale):
+def update(scal, count, tc, sizes, ridge, huber, step, vectors, margin, tile_scale, regions, first_sweep):
+    own_sites = vectors[0]
     reg_dev, _, cap = own_sites.shape
+    solves = ridge.shape[0]
     assert count % 2 == 0
-    tiles = cols.shape[0] // reg_dev
+    tiles = tc.shape[1]
     vmem = pl.BlockSpec(memory_space=pltpu.VMEM)
     smem = pl.BlockSpec(memory_space=pltpu.SMEM)
+    halo_n = reg_dev + 2 * margin
     return pl.pallas_call(
-        make_update_kernel(margin, tile_scale),
-        out_shape=jax.ShapeDtypeStruct((count,) + diagonal.shape[1:], jnp.float32),
-        in_specs=[smem, smem] + [vmem] * 8,
+        make_update_kernel(margin, tile_scale, regions, first_sweep),
+        out_shape=jax.ShapeDtypeStruct((count, solves, cap), jnp.float32),
+        in_specs=[smem] * 6 + [vmem] * len(vectors),
         out_specs=vmem,
-        scratch_shapes=[pltpu.VMEM((cap, tiles * cap), jnp.float32)] * 2,
-    )(base, cols, own_sites, halo_sites, halo_w, observed, diagonal, threshold, live, step)
+        scratch_shapes=[
+            pltpu.VMEM((cap, tiles * cap), jnp.float32),
+            pltpu.VMEM((cap, tiles * cap), jnp.float32),
+            pltpu.VMEM((halo_n, ROWS, cap), jnp.float32),
+            pltpu.VMEM((halo_n, solves, cap), jnp.float32),
+        ],
+    )(scal, tc, sizes, ridge, huber, step, *vectors)
 
 
 def make_grid_kernel(per_slab, reg_dev, n_wide, cap, regions):
@@ -254,50 +295,50 @@
         [jnp.pad(slots[:, :3, :], ((0, 0), (0, ROWS - 3), (0, 0))), spare], axis=0
     )
     list_slots = slots[:, 4, :gpr].astype(jnp.int32).reshape(-1)
-    left = site_slots[2 * reg_dev - margin : 2 * reg_dev]
-    right = site_slots[(n_wide - 1) * reg_dev : (n_wide - 1) * reg_dev + margin]
-    sites_wide = jnp.concatenate([left, obs_sites, right], axis=0)
+    left_sites = site_slots[2 * reg_dev - margin : 2 * reg_dev]
+    right_sites = site_slots[(n_wide - 1) * reg_dev : (n_wide - 1) * reg_dev + margin]
     live_mask = (jnp.arange(capacity, dtype=jnp.int32)[None, :] < region_sizes[:, None]).astype(
         jnp.float32
     )
     solves = ridge_weight.shape[0]
     diagonal = (obs_error * obs_error)[:, None, :] + ridge_weight[None, :, None]
     observed = (innovation * live_mask)[:, None, :]
-    threshold = huber_cut[None, :, None] * obs_error[:, None, :]
     obs_weights = observed / diagonal
-    live = live_mask[:, None, :]
-    step = jnp.broadcast_to(step_size[:, None], (solves, capacity))
-    local_cols = ((tile_columns - first_row + margin) % regions).reshape(-1)
     tile_scale = 2.0 / (capacity * tile_columns.shape[1])
     n_slab = lax.axis_size("slab")
     assert n_slab == 2 and margin * n_slab == reg_dev
     sidx = lax.axis_index("slab")
     sub = reg_dev // n_slab
-    base = (sidx * sub).astype(jnp.int32).reshape(1)
     blocks = n_wide * n_slab
     pairs = ("wide", "slab")
     other_pairs = [(b, b ^ 1) for b in range(blocks)]
     q1_pairs = [(b, (b - 2) % blocks) if b % 2 == 0 else (b, (b + 2) % blocks) for b in range(blocks)]
     q2_pairs = [(b, (b - 1) % blocks) if b % 2 == 0 else (b, (b + 1) % blocks) for b in range(blocks)]
     first = sidx == 0
+    scal = jnp.stack([sidx * sub, first_row, first.astype(jnp.int32)]).astype(jnp.int32)
+    common = (obs_sites, left_sites, right_sites, innovation, obs_error)
 
     def own_rows(mine):
         other = lax.ppermute(mine, pairs, other_pairs)
-        return jnp.where(first, jnp.concatenate([mine, other]), jnp.concatenate([other, mine]))
-
-    weights_wide = with_halo(obs_weights, "wide", margin)
+        return other, jnp.where(first, jnp.concatenate([mine, other]), jnp.concatenate([other, mine]))
+
+    count = lax.axis_size("wide")
+    w_tail = lax.slice_in_dim(obs_weights, reg_dev - margin, reg_dev, axis=0)
+    w_head = lax.slice_in_dim(obs_weights, 0, margin, axis=0)
+    w_left = lax.ppermute(w_tail, "wide", [(i, (i + 1) % count) for i in range(count)])
+    w_right = lax.ppermute(w_head, "wide", [((i + 1) % count, i) for i in range(count)])
+    vectors = common + (w_left, obs_weights, w_right)
     for sweep_index in range(ITERS):
         mine = update(
-            base, sub, local_cols, obs_sites, sites_wide, weights_wide, observed, diagonal,
-            threshold, live, step, margin, tile_scale,
+            scal, sub, tile_columns, region_sizes, ridge_weight, huber_cut, step_size, vectors,
+            margin, tile_scale, regions, sweep_index == 0,
         )
-        obs_weights = own_rows(mine)
         if sweep_index + 1 < ITERS:
+            other = lax.ppermute(mine, pairs, other_pairs)
             q1 = lax.ppermute(mine, pairs, q1_pairs)
             q2 = lax.ppermute(mine, pairs, q2_pairs)
-            left = jnp.where(first, q2, q1)
-            right = jnp.where(first, q1, q2)
-            weights_wide = jnp.concatenate([left, obs_weights, right])
+            vectors = common + (q1, q2, mine, other)
+    other, obs_weights = own_rows(mine)
     w_slots = jnp.concatenate(
         [gather_slots(obs_weights, "wide"), jnp.zeros((ROWS, solves, capacity), jnp.float32)], axis=0
     )

time: 90 us -> 88.7 us (0.986)
  other arithmetic: 5.3 us -> 1.71 us
  starting transfers between devices: 19.6 us -> 16.1 us
  waiting for transfers between devices: 12.4 us -> 15.7 us
  Pallas kernels: 38.3 us -> 40 us
  local copies, waits for them, and re-layouts: 12.5 us -> 13.9 us
    ppermute x1, waiting for transfers between devices: 0.07 us -> 3.15 us  [body(): q2 = lax.ppermute(mine, pairs, q2_pairs)]
    concatenate x3 -> x0, other arithmetic: 2.15 us -> none  [the longest x1 0.72 us: body(): sites_wide = jnp.concatenate([left, obs_sites, right], axis=0)]
    pallas_call x1, Pallas kernels: 23.6 us -> 25.5 us  [grid_stage(): pl.pallas_call(kernel, out_shape=jax.ShapeDtypeStruct((n_own, solves, gpt...]
    ppermute x1, starting transfers between devices: 2.2 us -> 0.39 us  [body(): q2 = lax.ppermute(mine, pairs, q2_pairs)]
    ppermute x2 -> x3, waiting for transfers between devices: 1.8 us -> 0.01 us  [the longest x1 0.01 us: body(): other = lax.ppermute(mine, pairs, other_pairs)]
    ppermute x1, starting transfers between devices: 3.19 us -> 1.47 us  [body(): q1 = lax.ppermute(mine, pairs, q1_pairs)]
    ppermute x6, waiting for transfers between devices: 8.03 us -> 9.75 us  [gather_slots(): lax.ppermute(x, axis, [(i, (i + s) % count) for i in range(count)])]
    unnamed x41 -> x44, local copies, waits for them, and re-layouts: 6.34 us -> 7.89 us
  transfers between devices with their start and end apart: 12 -> 12, of which waited for: 9 -> 7; matrix products, arithmetic and copies ran while one was open for 9% -> 8% of each run, Pallas kernels for 0% -> 0%
where the time goes in v7:
time: 88.7 us; the launch traced here: 88.3 us
  Pallas kernels  40 us (45%)
  starting transfers between devices  16.1 us (18%)
  waiting for transfers between devices  15.7 us (18%)
  local copies, waits for them, and re-layouts  13.9 us (16%)
  other arithmetic  1.71 us (2%)
  between operations  0.9 us (1%)
    pallas_call x1, Pallas kernels, grid_stage(): pl.pallas_call(kernel, out_shape=jax.ShapeDtypeStruct((n_own, solves, gpt...  25.5 us
    pallas_call x2, Pallas kernels, update(): pl.pallas_call(make_update_kernel(margin, tile_scale, regions, first_swee...  14.5 us
    ppermute x6, starting transfers between devices, gather_slots(): lax.ppermute(x, axis, [(i, (i + s) % count) for i in range(count)])  10.1 us
    ppermute x6, waiting for transfers between devices, gather_slots(): lax.ppermute(x, axis, [(i, (i + s) % count) for i in range(count)])  9.75 us
    unnamed x44, local copies, waits for them, and re-layouts  7.89 us
    ppermute x1, waiting for transfers between devices, body(): q2 = lax.ppermute(mine, pairs, q2_pairs)  3.15 us
    ppermute x1, starting transfers between devices, body(): lax.ppermute(w_tail, 'wide', [(i, (i + 1) % count) for i in range(count)])  2.48 us
    ppermute x1, waiting for transfers between devices, body(): q1 = lax.ppermute(mine, pairs, q1_pairs)  1.99 us
  transfers between devices with their start and end apart: 12, of which 7 were waited for; matrix products, arithmetic and copies ran while one was open for 8% of the time, Pallas kernels for 0%

profile of v7, /device:TPU:0, one launch (start us, length us, event | category | flops | bytes accessed | tf_op | source)
XLA Modules:
  0.0 88.3 jit_solution(11923593915242614966)
XLA Ops:
  0.7 0.8 fusion.4
  2.3 0.7 copy-done.13
  3.3 5.1 %collective-permute-start.2 = (f32[32,5,128]{2,1,0:T(8,128)S(1)}, f32[32,5,128]{2,1,0:T(8,128)S(1)}, u32[]{:S(2)}, u32[]{:S(2)}) collective-permute-start(f32[32,5,128]{2,1,0:T(8,128)S(1)} %concatenate.20), channel_id=1, source_target_pairs={{0,12},{4,0},{8,4},{12,8},{1,13},{5,1},{9,5},{13,9},{2,14},{6,2},{... | collective-permute-start | bytes 245768 | tf_op jit(solution)/shard_map/ppermute | solution.py:37
  8.4 1.0 %collective-permute-start = (f32[32,5,128]{2,1,0:T(8,128)S(1)}, f32[32,5,128]{2,1,0:T(8,128)S(1)}, u32[]{:S(2)}, u32[]{:S(2)}) collective-permute-start(f32[32,5,128]{2,1,0:T(8,128)S(1)} %concatenate.20), channel_id=1, source_target_pairs={{0,4},{4,8},{8,12},{12,0},{1,5},{5,9},{9,13},{13,1},{2,6},{6,10},{... | collective-permute-start | bytes 245768 | tf_op jit(solution)/shard_map/ppermute | solution.py:37
  10.9 2.5 %collective-permute-start.3 = (f32[16,8,128]{2,1,0:T(8,128)S(1)}, f32[16,8,128]{2,1,0:T(8,128)S(1)}, u32[]{:S(2)}, u32[]{:S(2)}) collective-permute-start(f32[16,8,128]{2,1,0:T(8,128)S(1)} %get-tuple-element.9), channel_id=1, source_target_pairs={{0,4},{4,8},{8,12},{12,0},{1,5},{5,9},{9,13},{13,1},{2,6},{6,10},{... | collective-permute-start | bytes 196616 | tf_op jit(solution)/shard_map/ppermute | solution.py:328
  13.3 1.3 %collective-permute-start.4 = (f32[16,8,128]{2,1,0:T(8,128)S(1)}, f32[16,8,128]{2,1,0:T(8,128)S(1)}, u32[]{:S(2)}, u32[]{:S(2)}) collective-permute-start(f32[16,8,128]{2,1,0:T(8,128)S(1)} %get-tuple-element.8), channel_id=1, source_target_pairs={{4,0},{8,4},{12,8},{0,12},{5,1},{9,5},{13,9},{1,13},{6,2},{10,6},{... | collective-permute-start | bytes 196616 | tf_op jit(solution)/shard_map/ppermute | solution.py:329
  15.4 0.7 copy.29.tc_ref
  16.1 0.8 stack.48.refs_0_
  18.8 3.0 %collective-permute-done.1 = f32[32,5,128]{2,1,0:T(8,128)S(1)} collective-permute-done((f32[32,5,128]{2,1,0:T(8,128)S(1)}, f32[32,5,128]{2,1,0:T(8,128)S(1)}, u32[]{:S(2)}, u32[]{:S(2)}) %collective-permute-start.1) | collective-permute-done | bytes 81952 | tf_op jit(solution)/shard_map/ppermute | solution.py:37
  23.2 7.2 %shard_map.140.refs_7_ = f32[16,8,128]{2,1,0:T(8,128)} custom-call(s32[3]{0:T(128)} %pad_add_fusion.scal_ref, s32[32,4]{1,0:T(8,128)} %copy.29.tc_ref, s32[32]{0:T(128)} %sizes_ref.3, f32[8]{0:T(128)} %ridge_ref.3, f32[8]{0:T(128)} %huber_ref.3, f32[8]{0:T(128)} %step_ref.3, f32[32,8,128]{2,1,0:T(8,128)} %stack.48.refs_0_, ...), custom_call_target="tpu_custom_call" | custom-call | tf_op jit(solution)/shard_map/pallas_call | solution.py:152
  30.4 1.5 %collective-permute-start.5 = (f32[16,8,128]{2,1,0:T(8,128)}, f32[16,8,128]{2,1,0:T(8,128)S(1)}, u32[]{:S(2)}, u32[]{:S(2)}) collective-permute-start(f32[16,8,128]{2,1,0:T(8,128)} %shard_map.140.refs_7_), channel_id=1, source_target_pairs={{0,12},{1,5},{4,0},{5,9},{8,4},{9,13},{12,8},{13,1},{2,14},{3,7},{... | collective-permute-start | bytes 196616 | tf_op jit(solution)/shard_map/ppermute | solution.py:338
  33.2 2.0 %collective-permute-done.5.refs_5_ = f32[16,8,128]{2,1,0:T(8,128)S(1)} collective-permute-done((f32[16,8,128]{2,1,0:T(8,128)}, f32[16,8,128]{2,1,0:T(8,128)S(1)}, u32[]{:S(2)}, u32[]{:S(2)}) %collective-permute-start.5) | collective-permute-done | bytes 65568 | tf_op jit(solution)/shard_map/ppermute | solution.py:338
  35.1 3.1 %collective-permute-done.6.refs_6_ = f32[16,8,128]{2,1,0:T(8,128)S(1)} collective-permute-done((f32[16,8,128]{2,1,0:T(8,128)}, f32[16,8,128]{2,1,0:T(8,128)S(1)}, u32[]{:S(2)}, u32[]{:S(2)}) %collective-permute-start.6) | collective-permute-done | bytes 65568 | tf_op jit(solution)/shard_map/ppermute | solution.py:339
  39.5 7.3 %shard_map.141 = f32[16,8,128]{2,1,0:T(8,128)} custom-call(s32[3]{0:T(128)} %pad_add_fusion.scal_ref, s32[32,4]{1,0:T(8,128)} %copy.29.tc_ref, s32[32]{0:T(128)} %sizes_ref.3, f32[8]{0:T(128)} %ridge_ref.3, f32[8]{0:T(128)} %huber_ref.3, f32[8]{0:T(128)} %step_ref.3, f32[32,8,128]{2,1,0:T(8,128)} %stack.48.refs_0_, f32[16,8,128]{2,1,0:T(8,128)} %get-tuple-element.7.refs_1_, ...), custom_call_target="tpu_custom_call" | custom-call | tf_op jit(solution)/shard_map/pallas_call | solution.py:152
  47.5 0.8 collective-permute-done.8
  48.7 0.7 stack.50.gsites_ref
  49.5 2.0 %collective-permute-start.10 = (f32[32,8,128]{2,1,0:T(8,128)S(1)}, f32[32,8,128]{2,1,0:T(8,128)S(1)}, u32[]{:S(2)}, u32[]{:S(2)}) collective-permute-start(f32[32,8,128]{2,1,0:T(8,128)S(1)} %get-tuple-element.5), channel_id=1, source_target_pairs={{0,8},{4,12},{8,0},{12,4},{1,9},{5,13},{9,1},{13,5},{2,10},{6,14},... | collective-permute-start | bytes 393224 | tf_op jit(solution)/shard_map/ppermute | solution.py:37
  51.7 0.7 convert_element_type.31.list_ref
  52.4 0.8 concatenate.24.sites_ref
  53.3 1.9 %collective-permute-start.11 = (f32[32,8,128]{2,1,0:T(8,128)S(1)}, f32[32,8,128]{2,1,0:T(8,128)S(1)}, u32[]{:S(2)}, u32[]{:S(2)}) collective-permute-start(f32[32,8,128]{2,1,0:T(8,128)S(1)} %get-tuple-element.5), channel_id=1, source_target_pairs={{0,12},{4,0},{8,4},{12,8},{1,13},{5,1},{9,5},{13,9},{2,14},{6,2},{... | collective-permute-start | bytes 393224 | tf_op jit(solution)/shard_map/ppermute | solution.py:37
  55.2 1.5 %collective-permute-done.9 = f32[32,8,128]{2,1,0:T(8,128)S(1)} collective-permute-done((f32[32,8,128]{2,1,0:T(8,128)S(1)}, f32[32,8,128]{2,1,0:T(8,128)S(1)}, u32[]{:S(2)}, u32[]{:S(2)}) %collective-permute-start.9) | collective-permute-done | bytes 131104 | tf_op jit(solution)/shard_map/ppermute | solution.py:37
  56.7 4.8 %collective-permute-done.10 = f32[32,8,128]{2,1,0:T(8,128)S(1)} collective-permute-done((f32[32,8,128]{2,1,0:T(8,128)S(1)}, f32[32,8,128]{2,1,0:T(8,128)S(1)}, u32[]{:S(2)}, u32[]{:S(2)}) %collective-permute-start.10) | collective-permute-done | bytes 131104 | tf_op jit(solution)/shard_map/ppermute | solution.py:37
  62.0 0.8 copy-done.2
  62.8 25.5 %shard_map.142 = f32[4,8,512]{2,1,0:T(8,128)} custom-call(s32[1]{0:T(128)} %bitcast.9.me_ref, s32[4]{0:T(128)} %copy-done.16, s32[512]{0:T(512)} %convert_element_type.31.list_ref, f32[136,8,128]{2,1,0:T(8,128)} %concatenate.24.sites_ref, f32[136,8,128]{2,1,0:T(8,128)} %copy-done.2, f32[4,8,512]{2,1,0:T(8,128)} %stack.50.gsites_ref), custom_call_target="tpu_custom_call" | custom-call | tf_op jit(solution)/shard_map/pallas_call | solution.py:246
  (82 shorter events, 10.8 us)
Async XLA Ops:
  0.6 32.0 %copy-start = (f32[32,512]{1,0:T(8,128)S(1)}, f32[32,512]{1,0:T(8,128)}, u32[]{:S(2)}) copy-start(f32[32,512]{1,0:T(8,128)} %param.21) | copy-start | bytes 196612
  1.5 0.7 copy-start.18
  2.3 0.7 copy-start.13
  3.1 6.3 %copy-start.3 = (f32[32,128]{1,0:T(8,128)S(1)}, f32[32,128]{1,0:T(8,128)}, u32[]{:S(2)}) copy-start(f32[32,128]{1,0:T(8,128)} %refs_4_.3) | copy-start | bytes 49156
  3.3 6.2 %copy-start.5 = (f32[32,128]{1,0:T(8,128)S(1)}, f32[32,128]{1,0:T(8,128)}, u32[]{:S(2)}) copy-start(f32[32,128]{1,0:T(8,128)} %refs_3_.3) | copy-start | bytes 49156
  3.3 6.2 %copy-start.14 = (s32[32]{0:T(128)S(1)}, s32[32]{0:T(128)}, u32[]{:S(2)}) copy-start(s32[32]{0:T(128)} %sizes_ref.3) | copy-start | bytes 388
  3.3 15.5 %collective-permute-start.2 = (f32[32,5,128]{2,1,0:T(8,128)S(1)}, f32[32,5,128]{2,1,0:T(8,128)S(1)}, u32[]{:S(2)}, u32[]{:S(2)}) collective-permute-start(f32[32,5,128]{2,1,0:T(8,128)S(1)} %concatenate.20), channel_id=1, source_target_pairs={{0,12},{4,0},{8,4},{12,8},{1,13},{5,1},{9,5},{13,9},{2,14},{6,2},{... | collective-permute-start | bytes 245768 | tf_op jit(solution)/shard_map/ppermute | solution.py:37
  8.4 13.4 %collective-permute-start.1 = (f32[32,5,128]{2,1,0:T(8,128)S(1)}, f32[32,5,128]{2,1,0:T(8,128)S(1)}, u32[]{:S(2)}, u32[]{:S(2)}) collective-permute-start(f32[32,5,128]{2,1,0:T(8,128)S(1)} %concatenate.20), channel_id=1, source_target_pairs={{0,8},{4,12},{8,0},{12,4},{1,9},{5,13},{9,1},{13,5},{2,10},{6,14},... | collective-permute-start | bytes 245768 | tf_op jit(solution)/shard_map/ppermute | solution.py:37
  8.4 13.4 %collective-permute-start = (f32[32,5,128]{2,1,0:T(8,128)S(1)}, f32[32,5,128]{2,1,0:T(8,128)S(1)}, u32[]{:S(2)}, u32[]{:S(2)}) collective-permute-start(f32[32,5,128]{2,1,0:T(8,128)S(1)} %concatenate.20), channel_id=1, source_target_pairs={{0,4},{4,8},{8,12},{12,0},{1,5},{5,9},{9,13},{13,1},{2,6},{6,10},{... | collective-permute-start | bytes 245768 | tf_op jit(solution)/shard_map/ppermute | solution.py:37
  10.9 11.7 %collective-permute-start.3 = (f32[16,8,128]{2,1,0:T(8,128)S(1)}, f32[16,8,128]{2,1,0:T(8,128)S(1)}, u32[]{:S(2)}, u32[]{:S(2)}) collective-permute-start(f32[16,8,128]{2,1,0:T(8,128)S(1)} %get-tuple-element.9), channel_id=1, source_target_pairs={{0,4},{4,8},{8,12},{12,0},{1,5},{5,9},{9,13},{13,1},{2,6},{6,10},{... | collective-permute-start | bytes 196616 | tf_op jit(solution)/shard_map/ppermute | solution.py:328
  13.3 9.2 %collective-permute-start.4 = (f32[16,8,128]{2,1,0:T(8,128)S(1)}, f32[16,8,128]{2,1,0:T(8,128)S(1)}, u32[]{:S(2)}, u32[]{:S(2)}) collective-permute-start(f32[16,8,128]{2,1,0:T(8,128)S(1)} %get-tuple-element.8), channel_id=1, source_target_pairs={{4,0},{8,4},{12,8},{0,12},{5,1},{9,5},{13,9},{1,13},{6,2},{10,6},{... | collective-permute-start | bytes 196616 | tf_op jit(solution)/shard_map/ppermute | solution.py:329
  14.7 0.7 copy-start.17
  30.4 4.7 %collective-permute-start.5 = (f32[16,8,128]{2,1,0:T(8,128)}, f32[16,8,128]{2,1,0:T(8,128)S(1)}, u32[]{:S(2)}, u32[]{:S(2)}) collective-permute-start(f32[16,8,128]{2,1,0:T(8,128)} %shard_map.140.refs_7_), channel_id=1, source_target_pairs={{0,12},{1,5},{4,0},{5,9},{8,4},{9,13},{12,8},{13,1},{2,14},{3,7},{... | collective-permute-start | bytes 196616 | tf_op jit(solution)/shard_map/ppermute | solution.py:338
  31.9 6.4 %collective-permute-start.6 = (f32[16,8,128]{2,1,0:T(8,128)}, f32[16,8,128]{2,1,0:T(8,128)S(1)}, u32[]{:S(2)}, u32[]{:S(2)}) collective-permute-start(f32[16,8,128]{2,1,0:T(8,128)} %shard_map.140.refs_7_), channel_id=1, source_target_pairs={{0,13},{1,4},{4,1},{5,8},{8,5},{9,12},{12,9},{13,0},{2,15},{3,6},{... | collective-permute-start | bytes 196616 | tf_op jit(solution)/shard_map/ppermute | solution.py:339
  32.3 6.0 %collective-permute-start.7 = (f32[16,8,128]{2,1,0:T(8,128)}, f32[16,8,128]{2,1,0:T(8,128)S(1)}, u32[]{:S(2)}, u32[]{:S(2)}) collective-permute-start(f32[16,8,128]{2,1,0:T(8,128)} %shard_map.140.refs_7_), channel_id=1, source_target_pairs={{0,1},{1,0},{4,5},{5,4},{8,9},{9,8},{12,13},{13,12},{2,3},{3,2},{6... | collective-permute-start | bytes 196616 | tf_op jit(solution)/shard_map/ppermute | solution.py:337
  35.1 3.2 %copy-start.9 = (f32[16,8,128]{2,1,0:T(8,128)}, f32[16,8,128]{2,1,0:T(8,128)S(1)}, u32[]{:S(2)}) copy-start(f32[16,8,128]{2,1,0:T(8,128)S(1)} %collective-permute-done.5.refs_5_) | copy-start | bytes 196612
  39.5 7.4 %copy-start.12 = (f32[32,512]{1,0:T(8,128)S(1)}, f32[32,512]{1,0:T(8,128)}, u32[]{:S(2)}) copy-start(f32[32,512]{1,0:T(8,128)} %param.22) | copy-start | bytes 196612
  46.8 1.5 %copy-start.4 = (f32[16,8,128]{2,1,0:T(8,128)S(1)}, f32[16,8,128]{2,1,0:T(8,128)}, u32[]{:S(2)}) copy-start(f32[16,8,128]{2,1,0:T(8,128)} %shard_map.141) | copy-start | bytes 196612
  46.8 1.5 %collective-permute-start.8 = (f32[16,8,128]{2,1,0:T(8,128)}, f32[16,8,128]{2,1,0:T(8,128)S(1)}, u32[]{:S(2)}, u32[]{:S(2)}) collective-permute-start(f32[16,8,128]{2,1,0:T(8,128)} %shard_map.141), channel_id=1, source_target_pairs={{0,1},{1,0},{4,5},{5,4},{8,9},{9,8},{12,13},{13,12},{2,3},{3,2},{6... | collective-permute-start | bytes 196616 | tf_op jit(solution)/shard_map/ppermute | solution.py:322
  48.3 5.0 %copy-start.6 = (f32[32,8,128]{2,1,0:T(8,128)}, f32[32,8,128]{2,1,0:T(8,128)S(1)}, u32[]{:S(2)}) copy-start(f32[32,8,128]{2,1,0:T(8,128)S(1)} %get-tuple-element.5) | copy-start | bytes 393220
  48.3 8.3 %collective-permute-start.9 = (f32[32,8,128]{2,1,0:T(8,128)S(1)}, f32[32,8,128]{2,1,0:T(8,128)S(1)}, u32[]{:S(2)}, u32[]{:S(2)}) collective-permute-start(f32[32,8,128]{2,1,0:T(8,128)S(1)} %get-tuple-element.5), channel_id=1, source_target_pairs={{0,4},{4,8},{8,12},{12,0},{1,5},{5,9},{9,13},{13,1},{2,6},{6,10},{... | collective-permute-start | bytes 393224 | tf_op jit(solution)/shard_map/ppermute | solution.py:37
  49.5 12.0 %collective-permute-start.10 = (f32[32,8,128]{2,1,0:T(8,128)S(1)}, f32[32,8,128]{2,1,0:T(8,128)S(1)}, u32[]{:S(2)}, u32[]{:S(2)}) collective-permute-start(f32[32,8,128]{2,1,0:T(8,128)S(1)} %get-tuple-element.5), channel_id=1, source_target_pairs={{0,8},{4,12},{8,0},{12,4},{1,9},{5,13},{9,1},{13,5},{2,10},{6,14},... | collective-permute-start | bytes 393224 | tf_op jit(solution)/shard_map/ppermute | solution.py:37
  53.3 8.7 %collective-permute-start.11 = (f32[32,8,128]{2,1,0:T(8,128)S(1)}, f32[32,8,128]{2,1,0:T(8,128)S(1)}, u32[]{:S(2)}, u32[]{:S(2)}) collective-permute-start(f32[32,8,128]{2,1,0:T(8,128)S(1)} %get-tuple-element.5), channel_id=1, source_target_pairs={{0,12},{4,0},{8,4},{12,8},{1,13},{5,1},{9,5},{13,9},{2,14},{6,2},{... | collective-permute-start | bytes 393224 | tf_op jit(solution)/shard_map/ppermute | solution.py:37
  61.9 0.8 copy-start.2
  (8 other events, 5.0 us)

commit v8 on v7

--- a/solution.py
+++ b/solution.py
@@ -64,7 +64,7 @@
 def make_update_kernel(margin, tile_scale, regions, first_sweep):
     def update_kernel(scal_ref, tc_ref, sizes_ref, ridge_ref, huber_ref, step_ref, *refs):
         if first_sweep:
-            own_ref, sl_ref, sr_ref, innov_ref, err_ref, wl_ref, wo_ref, wr_ref = refs[:8]
+            own_ref, sl_ref, sr_ref, innov_ref, err_ref, wo_ref = refs[:6]
         else:
             own_ref, sl_ref, sr_ref, innov_ref, err_ref, q1_ref, q2_ref, mine_ref, other_ref = refs[:9]
         out_ref, buf0, buf1, hs_ref, hw_ref = refs[-5:]
@@ -74,13 +74,13 @@
         base = scal_ref[0]
         first_row = scal_ref[1]
 
-        hs_ref[0:margin] = sl_ref[...]
+        hs_ref[0:margin] = sl_ref[:, 0:ROWS, :]
         hs_ref[margin : margin + reg_dev] = own_ref[...]
-        hs_ref[margin + reg_dev :] = sr_ref[...]
+        hs_ref[margin + reg_dev :] = sr_ref[:, 0:ROWS, :]
         if first_sweep:
-            hw_ref[0:margin] = wl_ref[...]
+            hw_ref[0:margin] = sl_ref[:, ROWS:, :]
             hw_ref[margin : margin + reg_dev] = wo_ref[...]
-            hw_ref[margin + reg_dev :] = wr_ref[...]
+            hw_ref[margin + reg_dev :] = sr_ref[:, ROWS:, :]
         else:
             sel = scal_ref[2] == 1
             q1 = q1_ref[...]
@@ -295,8 +295,6 @@
         [jnp.pad(slots[:, :3, :], ((0, 0), (0, ROWS - 3), (0, 0))), spare], axis=0
     )
     list_slots = slots[:, 4, :gpr].astype(jnp.int32).reshape(-1)
-    left_sites = site_slots[2 * reg_dev - margin : 2 * reg_dev]
-    right_sites = site_slots[(n_wide - 1) * reg_dev : (n_wide - 1) * reg_dev + margin]
     live_mask = (jnp.arange(capacity, dtype=jnp.int32)[None, :] < region_sizes[:, None]).astype(
         jnp.float32
     )
@@ -316,18 +314,19 @@
     q2_pairs = [(b, (b - 1) % blocks) if b % 2 == 0 else (b, (b + 1) % blocks) for b in range(blocks)]
     first = sidx == 0
     scal = jnp.stack([sidx * sub, first_row, first.astype(jnp.int32)]).astype(jnp.int32)
-    common = (obs_sites, left_sites, right_sites, innovation, obs_error)
+    count = lax.axis_size("wide")
+    both = jnp.concatenate([obs_sites, obs_weights], axis=1)
+    tail = lax.slice_in_dim(both, reg_dev - margin, reg_dev, axis=0)
+    head = lax.slice_in_dim(both, 0, margin, axis=0)
+    left_pack = lax.ppermute(tail, "wide", [(i, (i + 1) % count) for i in range(count)])
+    right_pack = lax.ppermute(head, "wide", [((i + 1) % count, i) for i in range(count)])
+    common = (obs_sites, left_pack, right_pack, innovation, obs_error)
 
     def own_rows(mine):
         other = lax.ppermute(mine, pairs, other_pairs)
         return other, jnp.where(first, jnp.concatenate([mine, other]), jnp.concatenate([other, mine]))
 
-    count = lax.axis_size("wide")
-    w_tail = lax.slice_in_dim(obs_weights, reg_dev - margin, reg_dev, axis=0)
-    w_head = lax.slice_in_dim(obs_weights, 0, margin, axis=0)
-    w_left = lax.ppermute(w_tail, "wide", [(i, (i + 1) % count) for i in range(count)])
-    w_right = lax.ppermute(w_head, "wide", [((i + 1) % count, i) for i in range(count)])
-    vectors = common + (w_left, obs_weights, w_right)
+    vectors = common + (obs_weights,)
     for sweep_index in range(ITERS):
         mine = update(
             scal, sub, tile_columns, region_sizes, ridge_weight, huber_cut, step_size, vectors,

time: 88.7 us -> 87.7 us (0.989); the launches traced: 88.3 us -> 86.1 us
  starting transfers between devices: 16.1 us -> 19.1 us
  waiting for transfers between devices: 15.7 us -> 13.1 us
  Pallas kernels: 40 us -> 38.2 us
    ppermute x6, waiting for transfers between devices: 9.75 us -> 6.99 us  [gather_slots(): lax.ppermute(x, axis, [(i, (i + s) % count) for i in range(count)])]
    ppermute x2, waiting for transfers between devices: 0.01 us -> 2.4 us  [the longest x1 1.97 us: body(): lax.ppermute(head, 'wide', [((i + 1) % count, i) for i in range(count)])]
    pallas_call x1, Pallas kernels: 25.5 us -> 23.6 us  [grid_stage(): pl.pallas_call(kernel, out_shape=jax.ShapeDtypeStruct((n_own, solves, gpt...]
    ppermute x6, starting transfers between devices: 10.1 us -> 12 us  [gather_slots(): lax.ppermute(x, axis, [(i, (i + s) % count) for i in range(count)])]
    ppermute x1, starting transfers between devices: 1.47 us -> 3.25 us  [body(): q1 = lax.ppermute(mine, pairs, q1_pairs)]
    ppermute x1, waiting for transfers between devices: 3.15 us -> 1.69 us  [body(): q2 = lax.ppermute(mine, pairs, q2_pairs)]
  transfers between devices with their start and end apart: 12 -> 12, of which waited for: 7 -> 7; matrix products, arithmetic and copies ran while one was open for 8% -> 8% of each run, Pallas kernels for 0% -> 17%
where the time goes in v8:
time: 87.7 us; the launch traced here: 86.1 us
  Pallas kernels  38.2 us (44%)
  starting transfers between devices  19.1 us (22%)
  local copies, waits for them, and re-layouts  13.2 us (15%)
  waiting for transfers between devices  13.1 us (15%)
  other arithmetic  1.73 us (2%)
  between operations  0.9 us (1%)
    pallas_call x1, Pallas kernels, grid_stage(): pl.pallas_call(kernel, out_shape=jax.ShapeDtypeStruct((n_own, solves, gpt...  23.6 us
    pallas_call x2, Pallas kernels, update(): pl.pallas_call(make_update_kernel(margin, tile_scale, regions, first_swee...  14.6 us
    ppermute x6, starting transfers between devices, gather_slots(): lax.ppermute(x, axis, [(i, (i + s) % count) for i in range(count)])  12 us
    unnamed x44, local copies, waits for them, and re-layouts  7.76 us
    ppermute x6, waiting for transfers between devices, gather_slots(): lax.ppermute(x, axis, [(i, (i + s) % count) for i in range(count)])  6.99 us
    ppermute x1, starting transfers between devices, body(): q1 = lax.ppermute(mine, pairs, q1_pairs)  3.25 us
    ppermute x1, starting transfers between devices, body(): lax.ppermute(head, 'wide', [((i + 1) % count, i) for i in range(count)])  2.82 us
    ppermute x1, waiting for transfers between devices, body(): lax.ppermute(head, 'wide', [((i + 1) % count, i) for i in range(count)])  1.97 us
  transfers between devices with their start and end apart: 12, of which 7 were waited for; matrix products, arithmetic and copies ran while one was open for 8% of the time, Pallas kernels for 17%

profile of v8, /device:TPU:0, one launch (start us, length us, event | category | flops | bytes accessed | tf_op | source)
XLA Modules:
  0.0 86.1 jit_solution(9655655672304205317)
XLA Ops:
  0.7 0.8 fusion.4
  2.3 0.7 copy-done.13
  3.3 5.1 %collective-permute-start.8 = (f32[32,5,128]{2,1,0:T(8,128)S(1)}, f32[32,5,128]{2,1,0:T(8,128)S(1)}, u32[]{:S(2)}, u32[]{:S(2)}) collective-permute-start(f32[32,5,128]{2,1,0:T(8,128)S(1)} %concatenate.27), channel_id=1, source_target_pairs={{0,12},{4,0},{8,4},{12,8},{1,13},{5,1},{9,5},{13,9},{2,14},{6,2},{... | collective-permute-start | bytes 245768 | tf_op jit(solution)/shard_map/ppermute | solution.py:37
  9.9 1.1 %collective-permute-start = (f32[16,16,128]{2,1,0:T(8,128)S(1)}, f32[16,16,128]{2,1,0:T(8,128)S(1)}, u32[]{:S(2)}, u32[]{:S(2)}) collective-permute-start(f32[16,16,128]{2,1,0:T(8,128)S(1)} %get-tuple-element.7), channel_id=1, source_target_pairs={{0,4},{4,8},{8,12},{12,0},{1,5},{5,9},{9,13},{13,1},{2,6},{6,10},{... | collective-permute-start | bytes 393224 | tf_op jit(solution)/shard_map/ppermute | solution.py:321
  10.9 2.8 %collective-permute-start.1 = (f32[16,16,128]{2,1,0:T(8,128)S(1)}, f32[16,16,128]{2,1,0:T(8,128)S(1)}, u32[]{:S(2)}, u32[]{:S(2)}) collective-permute-start(f32[16,16,128]{2,1,0:T(8,128)S(1)} %get-tuple-element.6), channel_id=1, source_target_pairs={{4,0},{8,4},{12,8},{0,12},{5,1},{9,5},{13,9},{1,13},{6,2},{10,6},{... | collective-permute-start | bytes 393224 | tf_op jit(solution)/shard_map/ppermute | solution.py:322
  15.0 0.8 stack.48.refs_0_
  15.8 0.7 copy-done.17
  16.5 0.7 copy.30.tc_ref
  18.8 2.0 %collective-permute-done.1.refs_2_ = f32[16,16,128]{2,1,0:T(8,128)S(1)} collective-permute-done((f32[16,16,128]{2,1,0:T(8,128)S(1)}, f32[16,16,128]{2,1,0:T(8,128)S(1)}, u32[]{:S(2)}, u32[]{:S(2)}) %collective-permute-start.1) | collective-permute-done | bytes 131104 | tf_op jit(solution)/shard_map/ppermute | solution.py:322
  21.4 7.3 %shard_map.140.refs_7_ = f32[16,8,128]{2,1,0:T(8,128)} custom-call(s32[3]{0:T(128)} %pad_add_fusion.scal_ref, s32[32,4]{1,0:T(8,128)} %copy.30.tc_ref, s32[32]{0:T(128)} %sizes_ref.3, f32[8]{0:T(128)} %ridge_ref.3, f32[8]{0:T(128)} %huber_ref.3, f32[8]{0:T(128)} %step_ref.3, f32[32,8,128]{2,1,0:T(8,128)} %stack.48.refs_0_, f32[16,16,128]{2,1,0:T(8,128)} %copy-done.3, ...), custom_call_target="tpu_custom_call" | custom-call | tf_op jit(solution)/shard_map/pallas_call | solution.py:152
  28.7 3.3 %collective-permute-start.2 = (f32[16,8,128]{2,1,0:T(8,128)}, f32[16,8,128]{2,1,0:T(8,128)S(1)}, u32[]{:S(2)}, u32[]{:S(2)}) collective-permute-start(f32[16,8,128]{2,1,0:T(8,128)} %shard_map.140.refs_7_), channel_id=1, source_target_pairs={{0,12},{1,5},{4,0},{5,9},{8,4},{9,13},{12,8},{13,1},{2,14},{3,7},{... | collective-permute-start | bytes 196616 | tf_op jit(solution)/shard_map/ppermute | solution.py:337
  32.6 1.6 %collective-permute-done.2.refs_5_ = f32[16,8,128]{2,1,0:T(8,128)S(1)} collective-permute-done((f32[16,8,128]{2,1,0:T(8,128)}, f32[16,8,128]{2,1,0:T(8,128)S(1)}, u32[]{:S(2)}, u32[]{:S(2)}) %collective-permute-start.2) | collective-permute-done | bytes 65568 | tf_op jit(solution)/shard_map/ppermute | solution.py:337
  34.2 2.5 %collective-permute-start.6 = (f32[32,5,128]{2,1,0:T(8,128)S(1)}, f32[32,5,128]{2,1,0:T(8,128)S(1)}, u32[]{:S(2)}, u32[]{:S(2)}) collective-permute-start(f32[32,5,128]{2,1,0:T(8,128)S(1)} %concatenate.27), channel_id=1, source_target_pairs={{0,4},{4,8},{8,12},{12,0},{1,5},{5,9},{9,13},{13,1},{2,6},{6,10},{... | collective-permute-start | bytes 245768 | tf_op jit(solution)/shard_map/ppermute | solution.py:37
  36.7 1.7 %collective-permute-done.3.refs_6_ = f32[16,8,128]{2,1,0:T(8,128)S(1)} collective-permute-done((f32[16,8,128]{2,1,0:T(8,128)}, f32[16,8,128]{2,1,0:T(8,128)S(1)}, u32[]{:S(2)}, u32[]{:S(2)}) %collective-permute-start.3) | collective-permute-done | bytes 65568 | tf_op jit(solution)/shard_map/ppermute | solution.py:338
  39.6 7.3 %shard_map.141 = f32[16,8,128]{2,1,0:T(8,128)} custom-call(s32[3]{0:T(128)} %pad_add_fusion.scal_ref, s32[32,4]{1,0:T(8,128)} %copy.30.tc_ref, s32[32]{0:T(128)} %sizes_ref.3, f32[8]{0:T(128)} %ridge_ref.3, f32[8]{0:T(128)} %huber_ref.3, f32[8]{0:T(128)} %step_ref.3, f32[32,8,128]{2,1,0:T(8,128)} %stack.48.refs_0_, f32[16,16,128]{2,1,0:T(8,128)} %copy-done.3, ...), custom_call_target="tpu_custom_call" | custom-call | tf_op jit(solution)/shard_map/pallas_call | solution.py:152
  47.3 0.7 stack.50.gsites_ref
  48.4 1.0 %collective-permute-start.9 = (f32[32,8,128]{2,1,0:T(8,128)S(1)}, f32[32,8,128]{2,1,0:T(8,128)S(1)}, u32[]{:S(2)}, u32[]{:S(2)}) collective-permute-start(f32[32,8,128]{2,1,0:T(8,128)S(1)} %get-tuple-element.5), channel_id=1, source_target_pairs={{0,4},{4,8},{8,12},{12,0},{1,5},{5,9},{9,13},{13,1},{2,6},{6,10},{... | collective-permute-start | bytes 393224 | tf_op jit(solution)/shard_map/ppermute | solution.py:37
  49.5 1.0 %collective-permute-start.10 = (f32[32,8,128]{2,1,0:T(8,128)S(1)}, f32[32,8,128]{2,1,0:T(8,128)S(1)}, u32[]{:S(2)}, u32[]{:S(2)}) collective-permute-start(f32[32,8,128]{2,1,0:T(8,128)S(1)} %get-tuple-element.5), channel_id=1, source_target_pairs={{0,8},{4,12},{8,0},{12,4},{1,9},{5,13},{9,1},{13,5},{2,10},{6,14},... | collective-permute-start | bytes 393224 | tf_op jit(solution)/shard_map/ppermute | solution.py:37
  51.4 0.8 concatenate.29.sites_ref
  52.3 2.3 %collective-permute-start.11 = (f32[32,8,128]{2,1,0:T(8,128)S(1)}, f32[32,8,128]{2,1,0:T(8,128)S(1)}, u32[]{:S(2)}, u32[]{:S(2)}) collective-permute-start(f32[32,8,128]{2,1,0:T(8,128)S(1)} %get-tuple-element.5), channel_id=1, source_target_pairs={{0,12},{4,0},{8,4},{12,8},{1,13},{5,1},{9,5},{13,9},{2,14},{6,2},{... | collective-permute-start | bytes 393224 | tf_op jit(solution)/shard_map/ppermute | solution.py:37
  54.6 2.1 %collective-permute-done.9 = f32[32,8,128]{2,1,0:T(8,128)S(1)} collective-permute-done((f32[32,8,128]{2,1,0:T(8,128)S(1)}, f32[32,8,128]{2,1,0:T(8,128)S(1)}, u32[]{:S(2)}, u32[]{:S(2)}) %collective-permute-start.9) | collective-permute-done | bytes 131104 | tf_op jit(solution)/shard_map/ppermute | solution.py:37
  56.8 4.9 %collective-permute-done.10 = f32[32,8,128]{2,1,0:T(8,128)S(1)} collective-permute-done((f32[32,8,128]{2,1,0:T(8,128)S(1)}, f32[32,8,128]{2,1,0:T(8,128)S(1)}, u32[]{:S(2)}, u32[]{:S(2)}) %collective-permute-start.10) | collective-permute-done | bytes 131104 | tf_op jit(solution)/shard_map/ppermute | solution.py:37
  61.7 0.8 copy-done.2
  62.5 23.6 %shard_map.142 = f32[4,8,512]{2,1,0:T(8,128)} custom-call(s32[1]{0:T(128)} %bitcast.8.me_ref, s32[4]{0:T(128)} %copy-done.16, s32[512]{0:T(512)} %convert_element_type.31.list_ref, f32[136,8,128]{2,1,0:T(8,128)} %concatenate.29.sites_ref, f32[136,8,128]{2,1,0:T(8,128)} %copy-done.2, f32[4,8,512]{2,1,0:T(8,128)} %stack.50.gsites_ref), custom_call_target="tpu_custom_call" | custom-call | tf_op jit(solution)/shard_map/pallas_call | solution.py:246
  (80 shorter events, 9.7 us)
Async XLA Ops:
  0.6 16.5 %copy-start = (f32[32,512]{1,0:T(8,128)S(1)}, f32[32,512]{1,0:T(8,128)}, u32[]{:S(2)}) copy-start(f32[32,512]{1,0:T(8,128)} %param.21) | copy-start | bytes 196612
  1.5 0.7 copy-start.18
  2.3 0.7 copy-start.13
  3.1 5.3 %copy-start.6 = (f32[32,128]{1,0:T(8,128)S(1)}, f32[32,128]{1,0:T(8,128)}, u32[]{:S(2)}) copy-start(f32[32,128]{1,0:T(8,128)} %refs_4_.3) | copy-start | bytes 49156
  3.3 5.2 %copy-start.7 = (f32[32,128]{1,0:T(8,128)S(1)}, f32[32,128]{1,0:T(8,128)}, u32[]{:S(2)}) copy-start(f32[32,128]{1,0:T(8,128)} %refs_3_.3) | copy-start | bytes 49156
  3.3 5.2 %copy-start.14 = (s32[32]{0:T(128)S(1)}, s32[32]{0:T(128)}, u32[]{:S(2)}) copy-start(s32[32]{0:T(128)} %sizes_ref.3) | copy-start | bytes 388
  3.3 46.1 %collective-permute-start.8 = (f32[32,5,128]{2,1,0:T(8,128)S(1)}, f32[32,5,128]{2,1,0:T(8,128)S(1)}, u32[]{:S(2)}, u32[]{:S(2)}) collective-permute-start(f32[32,5,128]{2,1,0:T(8,128)S(1)} %concatenate.27), channel_id=1, source_target_pairs={{0,12},{4,0},{8,4},{12,8},{1,13},{5,1},{9,5},{13,9},{2,14},{6,2},{... | collective-permute-start | bytes 245768 | tf_op jit(solution)/shard_map/ppermute | solution.py:37
  8.4 41.0 %collective-permute-start.7 = (f32[32,5,128]{2,1,0:T(8,128)S(1)}, f32[32,5,128]{2,1,0:T(8,128)S(1)}, u32[]{:S(2)}, u32[]{:S(2)}) collective-permute-start(f32[32,5,128]{2,1,0:T(8,128)S(1)} %concatenate.27), channel_id=1, source_target_pairs={{0,8},{4,12},{8,0},{12,4},{1,9},{5,13},{9,1},{13,5},{2,10},{6,14},... | collective-permute-start | bytes 245768 | tf_op jit(solution)/shard_map/ppermute | solution.py:37
  9.9 8.9 %collective-permute-start = (f32[16,16,128]{2,1,0:T(8,128)S(1)}, f32[16,16,128]{2,1,0:T(8,128)S(1)}, u32[]{:S(2)}, u32[]{:S(2)}) collective-permute-start(f32[16,16,128]{2,1,0:T(8,128)S(1)} %get-tuple-element.7), channel_id=1, source_target_pairs={{0,4},{4,8},{8,12},{12,0},{1,5},{5,9},{9,13},{13,1},{2,6},{6,10},{... | collective-permute-start | bytes 393224 | tf_op jit(solution)/shard_map/ppermute | solution.py:321
  10.9 9.8 %collective-permute-start.1 = (f32[16,16,128]{2,1,0:T(8,128)S(1)}, f32[16,16,128]{2,1,0:T(8,128)S(1)}, u32[]{:S(2)}, u32[]{:S(2)}) collective-permute-start(f32[16,16,128]{2,1,0:T(8,128)S(1)} %get-tuple-element.6), channel_id=1, source_target_pairs={{4,0},{8,4},{12,8},{0,12},{5,1},{9,5},{13,9},{1,13},{6,2},{10,6},{... | collective-permute-start | bytes 393224 | tf_op jit(solution)/shard_map/ppermute | solution.py:322
  18.8 2.0 %copy-start.3 = (f32[16,16,128]{2,1,0:T(8,128)}, f32[16,16,128]{2,1,0:T(8,128)S(1)}, u32[]{:S(2)}) copy-start(f32[16,16,128]{2,1,0:T(8,128)S(1)} %collective-permute-done.refs_1_) | copy-start | bytes 393220
  21.4 10.6 %copy-start.9 = (f32[32,512]{1,0:T(8,128)S(1)}, f32[32,512]{1,0:T(8,128)}, u32[]{:S(2)}) copy-start(f32[32,512]{1,0:T(8,128)} %param.22) | copy-start | bytes 196612
  28.7 5.5 %collective-permute-start.2 = (f32[16,8,128]{2,1,0:T(8,128)}, f32[16,8,128]{2,1,0:T(8,128)S(1)}, u32[]{:S(2)}, u32[]{:S(2)}) collective-permute-start(f32[16,8,128]{2,1,0:T(8,128)} %shard_map.140.refs_7_), channel_id=1, source_target_pairs={{0,12},{1,5},{4,0},{5,9},{8,4},{9,13},{12,8},{13,1},{2,14},{3,7},{... | collective-permute-start | bytes 196616 | tf_op jit(solution)/shard_map/ppermute | solution.py:337
  32.0 6.4 %collective-permute-start.3 = (f32[16,8,128]{2,1,0:T(8,128)}, f32[16,8,128]{2,1,0:T(8,128)S(1)}, u32[]{:S(2)}, u32[]{:S(2)}) collective-permute-start(f32[16,8,128]{2,1,0:T(8,128)} %shard_map.140.refs_7_), channel_id=1, source_target_pairs={{0,13},{1,4},{4,1},{5,8},{8,5},{9,12},{12,9},{13,0},{2,15},{3,6},{... | collective-permute-start | bytes 196616 | tf_op jit(solution)/shard_map/ppermute | solution.py:338
  32.0 6.4 %collective-permute-start.4 = (f32[16,8,128]{2,1,0:T(8,128)}, f32[16,8,128]{2,1,0:T(8,128)S(1)}, u32[]{:S(2)}, u32[]{:S(2)}) collective-permute-start(f32[16,8,128]{2,1,0:T(8,128)} %shard_map.140.refs_7_), channel_id=1, source_target_pairs={{0,1},{1,0},{4,5},{5,4},{8,9},{9,8},{12,13},{13,12},{2,3},{3,2},{6... | collective-permute-start | bytes 196616 | tf_op jit(solution)/shard_map/ppermute | solution.py:336
  34.2 4.2 %copy-start.10 = (f32[16,8,128]{2,1,0:T(8,128)}, f32[16,8,128]{2,1,0:T(8,128)S(1)}, u32[]{:S(2)}) copy-start(f32[16,8,128]{2,1,0:T(8,128)S(1)} %collective-permute-done.2.refs_5_) | copy-start | bytes 196612
  34.2 15.2 %collective-permute-start.6 = (f32[32,5,128]{2,1,0:T(8,128)S(1)}, f32[32,5,128]{2,1,0:T(8,128)S(1)}, u32[]{:S(2)}, u32[]{:S(2)}) collective-permute-start(f32[32,5,128]{2,1,0:T(8,128)S(1)} %concatenate.27), channel_id=1, source_target_pairs={{0,4},{4,8},{8,12},{12,0},{1,5},{5,9},{9,13},{13,1},{2,6},{6,10},{... | collective-permute-start | bytes 245768 | tf_op jit(solution)/shard_map/ppermute | solution.py:37
  46.9 1.5 %collective-permute-start.5 = (f32[16,8,128]{2,1,0:T(8,128)}, f32[16,8,128]{2,1,0:T(8,128)S(1)}, u32[]{:S(2)}, u32[]{:S(2)}) collective-permute-start(f32[16,8,128]{2,1,0:T(8,128)} %shard_map.141), channel_id=1, source_target_pairs={{0,1},{1,0},{4,5},{5,4},{8,9},{9,8},{12,13},{13,12},{2,3},{3,2},{6... | collective-permute-start | bytes 196616 | tf_op jit(solution)/shard_map/ppermute | solution.py:326
  47.3 1.1 %copy-start.5 = (f32[16,8,128]{2,1,0:T(8,128)S(1)}, f32[16,8,128]{2,1,0:T(8,128)}, u32[]{:S(2)}) copy-start(f32[16,8,128]{2,1,0:T(8,128)} %shard_map.141) | copy-start | bytes 196612
  48.4 3.9 %copy-start.8 = (f32[32,8,128]{2,1,0:T(8,128)}, f32[32,8,128]{2,1,0:T(8,128)S(1)}, u32[]{:S(2)}) copy-start(f32[32,8,128]{2,1,0:T(8,128)S(1)} %get-tuple-element.5) | copy-start | bytes 393220
  48.4 8.3 %collective-permute-start.9 = (f32[32,8,128]{2,1,0:T(8,128)S(1)}, f32[32,8,128]{2,1,0:T(8,128)S(1)}, u32[]{:S(2)}, u32[]{:S(2)}) collective-permute-start(f32[32,8,128]{2,1,0:T(8,128)S(1)} %get-tuple-element.5), channel_id=1, source_target_pairs={{0,4},{4,8},{8,12},{12,0},{1,5},{5,9},{9,13},{13,1},{2,6},{6,10},{... | collective-permute-start | bytes 393224 | tf_op jit(solution)/shard_map/ppermute | solution.py:37
  49.5 12.1 %collective-permute-start.10 = (f32[32,8,128]{2,1,0:T(8,128)S(1)}, f32[32,8,128]{2,1,0:T(8,128)S(1)}, u32[]{:S(2)}, u32[]{:S(2)}) collective-permute-start(f32[32,8,128]{2,1,0:T(8,128)S(1)} %get-tuple-element.5), channel_id=1, source_target_pairs={{0,8},{4,12},{8,0},{12,4},{1,9},{5,13},{9,1},{13,5},{2,10},{6,14},... | collective-permute-start | bytes 393224 | tf_op jit(solution)/shard_map/ppermute | solution.py:37
  52.3 9.4 %collective-permute-start.11 = (f32[32,8,128]{2,1,0:T(8,128)S(1)}, f32[32,8,128]{2,1,0:T(8,128)S(1)}, u32[]{:S(2)}, u32[]{:S(2)}) collective-permute-start(f32[32,8,128]{2,1,0:T(8,128)S(1)} %get-tuple-element.5), channel_id=1, source_target_pairs={{0,12},{4,0},{8,4},{12,8},{1,13},{5,1},{9,5},{13,9},{2,14},{6,2},{... | collective-permute-start | bytes 393224 | tf_op jit(solution)/shard_map/ppermute | solution.py:37
  61.7 0.8 copy-start.2
  (8 other events, 5.1 us)

commit v9 on v8

--- a/solution.py
+++ b/solution.py
@@ -163,13 +163,14 @@
     )(scal, tc, sizes, ridge, huber, step, *vectors)
 
 
-def make_grid_kernel(per_slab, reg_dev, n_wide, cap, regions):
+def make_grid_kernel(per_slab, reg_dev, n_wide, cap, regions, local):
     window = (2 * SLAB_REACH + 1) * per_slab
 
-    def grid_kernel(
-        me_ref, own_slabs_ref, list_ref, sites_ref, w_ref, gsites_ref, out_ref,
-        sel_ref, slab_ref, buf0, buf1,
-    ):
+    def grid_kernel(me_ref, own_slabs_ref, list_ref, sites_ref, w_ref, gsites_ref, *refs):
+        if local:
+            out_ref, sel_ref, slab_ref, buf0, buf1 = refs
+        else:
+            init_ref, out_ref, sel_ref, slab_ref, buf0, buf1 = refs
         n_own = out_ref.shape[0]
         gpr = list_ref.shape[0] // regions
         me = me_ref[0]
@@ -185,6 +186,10 @@
                 listed = list_ref[slot * gpr] == slab
                 for e in range(1, gpr):
                     listed = jnp.logical_or(listed, list_ref[slot * gpr + e] == slab)
+                if local:
+                    listed = jnp.logical_and(listed, owner == me)
+                else:
+                    listed = jnp.logical_and(listed, owner != me)
                 sel_ref[count] = slot
                 return count + listed.astype(jnp.int32)
 
@@ -205,7 +210,15 @@
         slab_ref[n_groups] = 0
         n_pairs = (n_groups + 1) // 2
         last = 2 * n_pairs - 1
-        out_ref[...] = jnp.zeros(out_ref.shape, jnp.float32)
+        if local:
+            out_ref[...] = jnp.zeros(out_ref.shape, jnp.float32)
+        else:
+            out_ref[...] = init_ref[...]
+
+        def weight_row(slot):
+            if local:
+                return w_ref[jnp.where(slot == regions, reg_dev, slot)]
+            return w_ref[slot]
 
         def fill(g, buf):
             g_t = gsites_ref[slab_ref[g]].T
@@ -216,7 +229,7 @@
         def use(g, buf):
             j = slab_ref[g]
             weights = jnp.concatenate(
-                [w_ref[sel_ref[g * GROUP + e]] for e in range(GROUP)], axis=1
+                [weight_row(sel_ref[g * GROUP + e]) for e in range(GROUP)], axis=1
             )
             out_ref[j] = out_ref[j] + contract_lanes(weights, buf[...])
 
@@ -231,22 +244,25 @@
             return carry
 
         lax.fori_loop(0, n_pairs, pair, 0)
-        out_ref[...] = out_ref[...] / cap
+        if not local:
+            out_ref[...] = out_ref[...] / cap
 
     return grid_kernel, window
 
 
-def grid_stage(me, own_slabs, list_slots, site_slots, w_slots, gsites, reg_dev, n_wide, regions, slab_count):
+def grid_stage(me, own_slabs, list_slots, site_slots, w_slots, gsites, reg_dev, n_wide, regions, slab_count, init=None):
     solves, cap = w_slots.shape[1:]
     n_own, _, gpts = gsites.shape
-    kernel, window = make_grid_kernel(regions // slab_count, reg_dev, n_wide, cap, regions)
+    local = init is None
+    kernel, window = make_grid_kernel(regions // slab_count, reg_dev, n_wide, cap, regions, local)
     vmem = pl.BlockSpec(memory_space=pltpu.VMEM)
     smem = pl.BlockSpec(memory_space=pltpu.SMEM)
     sel_len = n_own * (window + GROUP) + 2 * GROUP
+    extra = () if local else (init,)
     return pl.pallas_call(
         kernel,
         out_shape=jax.ShapeDtypeStruct((n_own, solves, gpts), jnp.float32),
-        in_specs=[smem, smem, smem, vmem, vmem, vmem],
+        in_specs=[smem, smem, smem, vmem, vmem, vmem] + [vmem] * len(extra),
         out_specs=vmem,
         scratch_shapes=[
             pltpu.SMEM((sel_len,), jnp.int32),
@@ -254,7 +270,7 @@
             pltpu.VMEM((gpts, GROUP * cap), jnp.float32),
             pltpu.VMEM((gpts, GROUP * cap), jnp.float32),
         ],
-    )(me, own_slabs, list_slots, site_slots, w_slots, gsites)
+    )(me, own_slabs, list_slots, site_slots, w_slots, gsites, *extra)
 
 
 def body(
@@ -349,17 +365,15 @@
     g_lat = grid_latitude[own_slabs]
     g_lon = FULL_TURN * (own_slabs[:, None].astype(jnp.float32) + grid_offset[own_slabs]) / slab_count
     gsites = unit_rows(g_lat, g_lon)
+    me32 = me.astype(jnp.int32).reshape(1)
+    spare_w = jnp.zeros((ROWS, solves, capacity), jnp.float32)
+    near = grid_stage(
+        me32, own_slabs, list_slots, site_slots, jnp.concatenate([obs_weights, spare_w]),
+        gsites, reg_dev, n_wide, regions, slab_count,
+    )
     grid_increment = grid_stage(
-        me.astype(jnp.int32).reshape(1),
-        own_slabs,
-        list_slots,
-        site_slots,
-        w_slots,
-        gsites,
-        reg_dev,
-        n_wide,
-        regions,
-        slab_count,
+        me32, own_slabs, list_slots, site_slots, w_slots,
+        gsites, reg_dev, n_wide, regions, slab_count, near,
     )
     return (obs_weights, grid_increment)
 

time: 87.7 us -> 89.2 us (1.017)
  Pallas kernels: 38.2 us -> 46.4 us
  waiting for transfers between devices: 13.1 us -> 6.03 us
    pallas_call x1 -> x2, Pallas kernels: 23.6 us -> 31.8 us  [grid_stage(): pl.pallas_call(kernel, out_shape=jax.ShapeDtypeStruct((n_own, solves, gpt...]
    ppermute x6, waiting for transfers between devices: 6.99 us -> 0.02 us  [gather_slots(): lax.ppermute(x, axis, [(i, (i + s) % count) for i in range(count)])]
  transfers between devices with their start and end apart: 12 -> 12, of which waited for: 7 -> 5; matrix products, arithmetic and copies ran while one was open for 8% -> 8% of each run, Pallas kernels for 17% -> 35%
where the time goes in v9:
time: 89.2 us; the launch traced here: 88.1 us
  Pallas kernels  46.4 us (52%)
  starting transfers between devices  19.1 us (21%)
  local copies, waits for them, and re-layouts  13.9 us (16%)
  waiting for transfers between devices  6.03 us (7%)
  other arithmetic  1.73 us (2%)
  between operations  0.92 us (1%)
    pallas_call x2, Pallas kernels, grid_stage(): pl.pallas_call(kernel, out_shape=jax.ShapeDtypeStruct((n_own, solves, gpt...  31.8 us
    pallas_call x2, Pallas kernels, update(): pl.pallas_call(make_update_kernel(margin, tile_scale, regions, first_swee...  14.6 us
    ppermute x6, starting transfers between devices, gather_slots(): lax.ppermute(x, axis, [(i, (i + s) % count) for i in range(count)])  12 us
    unnamed x44, local copies, waits for them, and re-layouts  7.81 us
    ppermute x1, starting transfers between devices, body(): q1 = lax.ppermute(mine, pairs, q1_pairs)  3.25 us
    ppermute x1, starting transfers between devices, body(): lax.ppermute(head, 'wide', [((i + 1) % count, i) for i in range(count)])  2.82 us
    ppermute x1, waiting for transfers between devices, body(): lax.ppermute(head, 'wide', [((i + 1) % count, i) for i in range(count)])  1.97 us
  transfers between devices with their start and end apart: 12, of which 5 were waited for; matrix products, arithmetic and copies ran while one was open for 8% of the time, Pallas kernels for 35%

profile of v9, /device:TPU:0, one launch (start us, length us, event | category | flops | bytes accessed | tf_op | source)
XLA Modules:
  0.0 88.1 jit_solution(17364769198239581102)
XLA Ops:
  0.7 0.8 fusion.4
  2.3 0.7 copy-done.13
  3.3 5.1 %collective-permute-start.8 = (f32[32,5,128]{2,1,0:T(8,128)S(1)}, f32[32,5,128]{2,1,0:T(8,128)S(1)}, u32[]{:S(2)}, u32[]{:S(2)}) collective-permute-start(f32[32,5,128]{2,1,0:T(8,128)S(1)} %concatenate.30), channel_id=1, source_target_pairs={{0,12},{4,0},{8,4},{12,8},{1,13},{5,1},{9,5},{13,9},{2,14},{6,2},{... | collective-permute-start | bytes 245768 | tf_op jit(solution)/shard_map/ppermute | solution.py:37
  9.9 1.1 %collective-permute-start = (f32[16,16,128]{2,1,0:T(8,128)S(1)}, f32[16,16,128]{2,1,0:T(8,128)S(1)}, u32[]{:S(2)}, u32[]{:S(2)}) collective-permute-start(f32[16,16,128]{2,1,0:T(8,128)S(1)} %get-tuple-element.7), channel_id=1, source_target_pairs={{0,4},{4,8},{8,12},{12,0},{1,5},{5,9},{9,13},{13,1},{2,6},{6,10},{... | collective-permute-start | bytes 393224 | tf_op jit(solution)/shard_map/ppermute | solution.py:337
  10.9 2.8 %collective-permute-start.1 = (f32[16,16,128]{2,1,0:T(8,128)S(1)}, f32[16,16,128]{2,1,0:T(8,128)S(1)}, u32[]{:S(2)}, u32[]{:S(2)}) collective-permute-start(f32[16,16,128]{2,1,0:T(8,128)S(1)} %get-tuple-element.6), channel_id=1, source_target_pairs={{4,0},{8,4},{12,8},{0,12},{5,1},{9,5},{13,9},{1,13},{6,2},{10,6},{... | collective-permute-start | bytes 393224 | tf_op jit(solution)/shard_map/ppermute | solution.py:338
  15.1 0.8 stack.48.refs_0_
  16.5 0.7 copy.30.tc_ref
  18.8 2.0 %collective-permute-done.1.refs_2_ = f32[16,16,128]{2,1,0:T(8,128)S(1)} collective-permute-done((f32[16,16,128]{2,1,0:T(8,128)S(1)}, f32[16,16,128]{2,1,0:T(8,128)S(1)}, u32[]{:S(2)}, u32[]{:S(2)}) %collective-permute-start.1) | collective-permute-done | bytes 131104 | tf_op jit(solution)/shard_map/ppermute | solution.py:338
  21.4 7.3 %shard_map.140.refs_7_ = f32[16,8,128]{2,1,0:T(8,128)} custom-call(s32[3]{0:T(128)} %pad_add_fusion.scal_ref, s32[32,4]{1,0:T(8,128)} %copy.30.tc_ref, s32[32]{0:T(128)} %sizes_ref.3, f32[8]{0:T(128)} %ridge_ref.3, f32[8]{0:T(128)} %huber_ref.3, f32[8]{0:T(128)} %step_ref.3, f32[32,8,128]{2,1,0:T(8,128)} %stack.48.refs_0_, f32[16,16,128]{2,1,0:T(8,128)} %copy-done.4, ...), custom_call_target="tpu_custom_call" | custom-call | tf_op jit(solution)/shard_map/pallas_call | solution.py:152
  28.7 3.2 %collective-permute-start.2 = (f32[16,8,128]{2,1,0:T(8,128)}, f32[16,8,128]{2,1,0:T(8,128)S(1)}, u32[]{:S(2)}, u32[]{:S(2)}) collective-permute-start(f32[16,8,128]{2,1,0:T(8,128)} %shard_map.140.refs_7_), channel_id=1, source_target_pairs={{0,12},{1,5},{4,0},{5,9},{8,4},{9,13},{12,8},{13,1},{2,14},{3,7},{... | collective-permute-start | bytes 196616 | tf_op jit(solution)/shard_map/ppermute | solution.py:353
  32.6 1.6 %collective-permute-done.2.refs_5_ = f32[16,8,128]{2,1,0:T(8,128)S(1)} collective-permute-done((f32[16,8,128]{2,1,0:T(8,128)}, f32[16,8,128]{2,1,0:T(8,128)S(1)}, u32[]{:S(2)}, u32[]{:S(2)}) %collective-permute-start.2) | collective-permute-done | bytes 65568 | tf_op jit(solution)/shard_map/ppermute | solution.py:353
  34.2 2.5 %collective-permute-start.6 = (f32[32,5,128]{2,1,0:T(8,128)S(1)}, f32[32,5,128]{2,1,0:T(8,128)S(1)}, u32[]{:S(2)}, u32[]{:S(2)}) collective-permute-start(f32[32,5,128]{2,1,0:T(8,128)S(1)} %concatenate.30), channel_id=1, source_target_pairs={{0,4},{4,8},{8,12},{12,0},{1,5},{5,9},{9,13},{13,1},{2,6},{6,10},{... | collective-permute-start | bytes 245768 | tf_op jit(solution)/shard_map/ppermute | solution.py:37
  36.7 1.7 %collective-permute-done.3.refs_6_ = f32[16,8,128]{2,1,0:T(8,128)S(1)} collective-permute-done((f32[16,8,128]{2,1,0:T(8,128)}, f32[16,8,128]{2,1,0:T(8,128)S(1)}, u32[]{:S(2)}, u32[]{:S(2)}) %collective-permute-start.3) | collective-permute-done | bytes 65568 | tf_op jit(solution)/shard_map/ppermute | solution.py:354
  39.6 7.3 %shard_map.141 = f32[16,8,128]{2,1,0:T(8,128)} custom-call(s32[3]{0:T(128)} %pad_add_fusion.scal_ref, s32[32,4]{1,0:T(8,128)} %copy.30.tc_ref, s32[32]{0:T(128)} %sizes_ref.3, f32[8]{0:T(128)} %ridge_ref.3, f32[8]{0:T(128)} %huber_ref.3, f32[8]{0:T(128)} %step_ref.3, f32[32,8,128]{2,1,0:T(8,128)} %stack.48.refs_0_, f32[16,16,128]{2,1,0:T(8,128)} %copy-done.4, ...), custom_call_target="tpu_custom_call" | custom-call | tf_op jit(solution)/shard_map/pallas_call | solution.py:152
  47.3 0.7 stack.50.gsites_ref
  48.4 1.0 %collective-permute-start.9 = (f32[32,8,128]{2,1,0:T(8,128)S(1)}, f32[32,8,128]{2,1,0:T(8,128)S(1)}, u32[]{:S(2)}, u32[]{:S(2)}) collective-permute-start(f32[32,8,128]{2,1,0:T(8,128)S(1)} %get-tuple-element.5), channel_id=1, source_target_pairs={{0,4},{4,8},{8,12},{12,0},{1,5},{5,9},{9,13},{13,1},{2,6},{6,10},{... | collective-permute-start | bytes 393224 | tf_op jit(solution)/shard_map/ppermute | solution.py:37
  49.5 1.0 %collective-permute-start.10 = (f32[32,8,128]{2,1,0:T(8,128)S(1)}, f32[32,8,128]{2,1,0:T(8,128)S(1)}, u32[]{:S(2)}, u32[]{:S(2)}) collective-permute-start(f32[32,8,128]{2,1,0:T(8,128)S(1)} %get-tuple-element.5), channel_id=1, source_target_pairs={{0,8},{4,12},{8,0},{12,4},{1,9},{5,13},{9,1},{13,5},{2,10},{6,14},... | collective-permute-start | bytes 393224 | tf_op jit(solution)/shard_map/ppermute | solution.py:37
  50.8 0.7 convert_element_type.31.list_ref
  51.5 0.8 concatenate.32.sites_ref
  52.3 2.3 %collective-permute-start.11 = (f32[32,8,128]{2,1,0:T(8,128)S(1)}, f32[32,8,128]{2,1,0:T(8,128)S(1)}, u32[]{:S(2)}, u32[]{:S(2)}) collective-permute-start(f32[32,8,128]{2,1,0:T(8,128)S(1)} %get-tuple-element.5), channel_id=1, source_target_pairs={{0,12},{4,0},{8,4},{12,8},{1,13},{5,1},{9,5},{13,9},{2,14},{6,2},{... | collective-permute-start | bytes 393224 | tf_op jit(solution)/shard_map/ppermute | solution.py:37
  54.7 0.7 concatenate.34.w_ref
  55.4 15.9 %shard_map.142.refs_0_ = f32[4,8,512]{2,1,0:T(8,128)} custom-call(s32[1]{0:T(128)} %bitcast.8.me_ref, s32[4]{0:T(128)} %copy-done.14, s32[512]{0:T(512)} %convert_element_type.31.list_ref, f32[136,8,128]{2,1,0:T(8,128)} %concatenate.32.sites_ref, f32[40,8,128]{2,1,0:T(8,128)} %concatenate.34.w_ref, f32[4,8,512]{2,1,0:T(8,128)} %stack.50.gsites_ref), custom_call_target="tpu_custom_call" | custom-call | tf_op jit(solution)/shard_map/pallas_call | solution.py:262
  71.3 0.8 copy-done.2
  72.1 16.0 %shard_map.143 = f32[4,8,512]{2,1,0:T(8,128)} custom-call(s32[1]{0:T(128)} %bitcast.8.me_ref, s32[4]{0:T(128)} %copy-done.14, s32[512]{0:T(512)} %convert_element_type.31.list_ref, f32[136,8,128]{2,1,0:T(8,128)} %concatenate.32.sites_ref, f32[136,8,128]{2,1,0:T(8,128)} %copy-done.2, f32[4,8,512]{2,1,0:T(8,128)} %stack.50.gsites_ref, ...), custom_call_target="tpu_custom_call" | custom-call | tf_op jit(solution)/shard_map/pallas_call | solution.py:262
  (82 shorter events, 9.8 us)
Async XLA Ops:
  0.6 16.6 %copy-start = (f32[32,512]{1,0:T(8,128)S(1)}, f32[32,512]{1,0:T(8,128)}, u32[]{:S(2)}) copy-start(f32[32,512]{1,0:T(8,128)} %param.21) | copy-start | bytes 196612
  1.5 0.7 copy-start.18
  2.3 0.7 copy-start.13
  3.1 5.3 %copy-start.7 = (f32[32,128]{1,0:T(8,128)S(1)}, f32[32,128]{1,0:T(8,128)}, u32[]{:S(2)}) copy-start(f32[32,128]{1,0:T(8,128)} %refs_4_.3) | copy-start | bytes 49156
  3.3 5.2 %copy-start.8 = (f32[32,128]{1,0:T(8,128)S(1)}, f32[32,128]{1,0:T(8,128)}, u32[]{:S(2)}) copy-start(f32[32,128]{1,0:T(8,128)} %refs_3_.3) | copy-start | bytes 49156
  3.3 5.2 %copy-start.15 = (s32[32]{0:T(128)S(1)}, s32[32]{0:T(128)}, u32[]{:S(2)}) copy-start(s32[32]{0:T(128)} %sizes_ref.3) | copy-start | bytes 388
  3.3 46.1 %collective-permute-start.8 = (f32[32,5,128]{2,1,0:T(8,128)S(1)}, f32[32,5,128]{2,1,0:T(8,128)S(1)}, u32[]{:S(2)}, u32[]{:S(2)}) collective-permute-start(f32[32,5,128]{2,1,0:T(8,128)S(1)} %concatenate.30), channel_id=1, source_target_pairs={{0,12},{4,0},{8,4},{12,8},{1,13},{5,1},{9,5},{13,9},{2,14},{6,2},{... | collective-permute-start | bytes 245768 | tf_op jit(solution)/shard_map/ppermute | solution.py:37
  8.4 41.0 %collective-permute-start.7 = (f32[32,5,128]{2,1,0:T(8,128)S(1)}, f32[32,5,128]{2,1,0:T(8,128)S(1)}, u32[]{:S(2)}, u32[]{:S(2)}) collective-permute-start(f32[32,5,128]{2,1,0:T(8,128)S(1)} %concatenate.30), channel_id=1, source_target_pairs={{0,8},{4,12},{8,0},{12,4},{1,9},{5,13},{9,1},{13,5},{2,10},{6,14},... | collective-permute-start | bytes 245768 | tf_op jit(solution)/shard_map/ppermute | solution.py:37
  9.9 8.9 %collective-permute-start = (f32[16,16,128]{2,1,0:T(8,128)S(1)}, f32[16,16,128]{2,1,0:T(8,128)S(1)}, u32[]{:S(2)}, u32[]{:S(2)}) collective-permute-start(f32[16,16,128]{2,1,0:T(8,128)S(1)} %get-tuple-element.7), channel_id=1, source_target_pairs={{0,4},{4,8},{8,12},{12,0},{1,5},{5,9},{9,13},{13,1},{2,6},{6,10},{... | collective-permute-start | bytes 393224 | tf_op jit(solution)/shard_map/ppermute | solution.py:337
  10.9 9.8 %collective-permute-start.1 = (f32[16,16,128]{2,1,0:T(8,128)S(1)}, f32[16,16,128]{2,1,0:T(8,128)S(1)}, u32[]{:S(2)}, u32[]{:S(2)}) collective-permute-start(f32[16,16,128]{2,1,0:T(8,128)S(1)} %get-tuple-element.6), channel_id=1, source_target_pairs={{4,0},{8,4},{12,8},{0,12},{5,1},{9,5},{13,9},{1,13},{6,2},{10,6},{... | collective-permute-start | bytes 393224 | tf_op jit(solution)/shard_map/ppermute | solution.py:338
  18.8 2.0 %copy-start.4 = (f32[16,16,128]{2,1,0:T(8,128)}, f32[16,16,128]{2,1,0:T(8,128)S(1)}, u32[]{:S(2)}) copy-start(f32[16,16,128]{2,1,0:T(8,128)S(1)} %collective-permute-done.refs_1_) | copy-start | bytes 393220
  21.4 10.6 %copy-start.9 = (f32[32,512]{1,0:T(8,128)S(1)}, f32[32,512]{1,0:T(8,128)}, u32[]{:S(2)}) copy-start(f32[32,512]{1,0:T(8,128)} %param.22) | copy-start | bytes 196612
  28.7 5.5 %collective-permute-start.2 = (f32[16,8,128]{2,1,0:T(8,128)}, f32[16,8,128]{2,1,0:T(8,128)S(1)}, u32[]{:S(2)}, u32[]{:S(2)}) collective-permute-start(f32[16,8,128]{2,1,0:T(8,128)} %shard_map.140.refs_7_), channel_id=1, source_target_pairs={{0,12},{1,5},{4,0},{5,9},{8,4},{9,13},{12,8},{13,1},{2,14},{3,7},{... | collective-permute-start | bytes 196616 | tf_op jit(solution)/shard_map/ppermute | solution.py:353
  32.0 6.4 %collective-permute-start.3 = (f32[16,8,128]{2,1,0:T(8,128)}, f32[16,8,128]{2,1,0:T(8,128)S(1)}, u32[]{:S(2)}, u32[]{:S(2)}) collective-permute-start(f32[16,8,128]{2,1,0:T(8,128)} %shard_map.140.refs_7_), channel_id=1, source_target_pairs={{0,13},{1,4},{4,1},{5,8},{8,5},{9,12},{12,9},{13,0},{2,15},{3,6},{... | collective-permute-start | bytes 196616 | tf_op jit(solution)/shard_map/ppermute | solution.py:354
  32.0 6.4 %collective-permute-start.4 = (f32[16,8,128]{2,1,0:T(8,128)}, f32[16,8,128]{2,1,0:T(8,128)S(1)}, u32[]{:S(2)}, u32[]{:S(2)}) collective-permute-start(f32[16,8,128]{2,1,0:T(8,128)} %shard_map.140.refs_7_), channel_id=1, source_target_pairs={{0,1},{1,0},{4,5},{5,4},{8,9},{9,8},{12,13},{13,12},{2,3},{3,2},{6... | collective-permute-start | bytes 196616 | tf_op jit(solution)/shard_map/ppermute | solution.py:352
  34.2 4.2 %copy-start.10 = (f32[16,8,128]{2,1,0:T(8,128)}, f32[16,8,128]{2,1,0:T(8,128)S(1)}, u32[]{:S(2)}) copy-start(f32[16,8,128]{2,1,0:T(8,128)S(1)} %collective-permute-done.2.refs_5_) | copy-start | bytes 196612
  34.2 15.2 %collective-permute-start.6 = (f32[32,5,128]{2,1,0:T(8,128)S(1)}, f32[32,5,128]{2,1,0:T(8,128)S(1)}, u32[]{:S(2)}, u32[]{:S(2)}) collective-permute-start(f32[32,5,128]{2,1,0:T(8,128)S(1)} %concatenate.30), channel_id=1, source_target_pairs={{0,4},{4,8},{8,12},{12,0},{1,5},{5,9},{9,13},{13,1},{2,6},{6,10},{... | collective-permute-start | bytes 245768 | tf_op jit(solution)/shard_map/ppermute | solution.py:37
  46.9 1.5 %collective-permute-start.5 = (f32[16,8,128]{2,1,0:T(8,128)}, f32[16,8,128]{2,1,0:T(8,128)S(1)}, u32[]{:S(2)}, u32[]{:S(2)}) collective-permute-start(f32[16,8,128]{2,1,0:T(8,128)} %shard_map.141), channel_id=1, source_target_pairs={{0,1},{1,0},{4,5},{5,4},{8,9},{9,8},{12,13},{13,12},{2,3},{3,2},{6... | collective-permute-start | bytes 196616 | tf_op jit(solution)/shard_map/ppermute | solution.py:342
  47.3 1.1 %copy-start.6 = (f32[16,8,128]{2,1,0:T(8,128)S(1)}, f32[16,8,128]{2,1,0:T(8,128)}, u32[]{:S(2)}) copy-start(f32[16,8,128]{2,1,0:T(8,128)} %shard_map.141) | copy-start | bytes 196612
  48.4 6.3 %copy-start.3 = (f32[32,8,128]{2,1,0:T(8,128)}, f32[32,8,128]{2,1,0:T(8,128)S(1)}, u32[]{:S(2)}) copy-start(f32[32,8,128]{2,1,0:T(8,128)S(1)} %get-tuple-element.5) | copy-start | bytes 393220
  48.4 22.8 %collective-permute-start.9 = (f32[32,8,128]{2,1,0:T(8,128)S(1)}, f32[32,8,128]{2,1,0:T(8,128)S(1)}, u32[]{:S(2)}, u32[]{:S(2)}) collective-permute-start(f32[32,8,128]{2,1,0:T(8,128)S(1)} %get-tuple-element.5), channel_id=1, source_target_pairs={{0,4},{4,8},{8,12},{12,0},{1,5},{5,9},{9,13},{13,1},{2,6},{6,10},{... | collective-permute-start | bytes 393224 | tf_op jit(solution)/shard_map/ppermute | solution.py:37
  49.5 21.7 %collective-permute-start.10 = (f32[32,8,128]{2,1,0:T(8,128)S(1)}, f32[32,8,128]{2,1,0:T(8,128)S(1)}, u32[]{:S(2)}, u32[]{:S(2)}) collective-permute-start(f32[32,8,128]{2,1,0:T(8,128)S(1)} %get-tuple-element.5), channel_id=1, source_target_pairs={{0,8},{4,12},{8,0},{12,4},{1,9},{5,13},{9,1},{13,5},{2,10},{6,14},... | collective-permute-start | bytes 393224 | tf_op jit(solution)/shard_map/ppermute | solution.py:37
  52.3 18.9 %collective-permute-start.11 = (f32[32,8,128]{2,1,0:T(8,128)S(1)}, f32[32,8,128]{2,1,0:T(8,128)S(1)}, u32[]{:S(2)}, u32[]{:S(2)}) collective-permute-start(f32[32,8,128]{2,1,0:T(8,128)S(1)} %get-tuple-element.5), channel_id=1, source_target_pairs={{0,12},{4,0},{8,4},{12,8},{1,13},{5,1},{9,5},{13,9},{2,14},{6,2},{... | collective-permute-start | bytes 393224 | tf_op jit(solution)/shard_map/ppermute | solution.py:37
  71.3 0.8 copy-start.2
  (8 other events, 5.1 us)

commit v10 on v8

--- a/solution.py
+++ b/solution.py
@@ -168,7 +168,7 @@
 
     def grid_kernel(
         me_ref, own_slabs_ref, list_ref, sites_ref, w_ref, gsites_ref, out_ref,
-        sel_ref, slab_ref, buf0, buf1,
+        sel_ref, slab_ref, buf0, buf1, acc_ref,
     ):
         n_own = out_ref.shape[0]
         gpr = list_ref.shape[0] // regions
@@ -205,7 +205,7 @@
         slab_ref[n_groups] = 0
         n_pairs = (n_groups + 1) // 2
         last = 2 * n_pairs - 1
-        out_ref[...] = jnp.zeros(out_ref.shape, jnp.float32)
+        acc_ref[...] = jnp.zeros(acc_ref.shape, jnp.float32)
 
         def fill(g, buf):
             g_t = gsites_ref[slab_ref[g]].T
@@ -215,10 +215,12 @@
 
         def use(g, buf):
             j = slab_ref[g]
-            weights = jnp.concatenate(
-                [w_ref[sel_ref[g * GROUP + e]] for e in range(GROUP)], axis=1
+            columns = jnp.concatenate(
+                [w_ref[sel_ref[g * GROUP + e]].T for e in range(GROUP)], axis=0
             )
-            out_ref[j] = out_ref[j] + contract_lanes(weights, buf[...])
+            acc_ref[j] = acc_ref[j] + jnp.dot(
+                buf[...], columns, precision=MATMUL_PRECISION, preferred_element_type=jnp.float32
+            )
 
         fill(0, buf0)
 
@@ -231,7 +233,8 @@
             return carry
 
         lax.fori_loop(0, n_pairs, pair, 0)
-        out_ref[...] = out_ref[...] / cap
+        for j in range(n_own):
+            out_ref[j] = acc_ref[j].T / cap
 
     return grid_kernel, window
 
@@ -253,6 +256,7 @@
             pltpu.SMEM((sel_len // GROUP + 2,), jnp.int32),
             pltpu.VMEM((gpts, GROUP * cap), jnp.float32),
             pltpu.VMEM((gpts, GROUP * cap), jnp.float32),
+            pltpu.VMEM((n_own, gpts, solves), jnp.float32),
         ],
     )(me, own_slabs, list_slots, site_slots, w_slots, gsites)
 

time: 87.7 us -> 90.1 us (1.027)
  the two profiles are of different devices: /device:TPU:0 before, /device:TPU:13 now
where the time goes in v10:
time: 90.1 us; the launch traced here: 88.8 us
  Pallas kernels  40.7 us (45%)
  waiting for transfers between devices  16.1 us (18%)
  starting transfers between devices  15.5 us (17%)
  local copies, waits for them, and re-layouts  13.9 us (15%)
  other arithmetic  1.73 us (2%)
    pallas_call x1, Pallas kernels, grid_stage(): pl.pallas_call(kernel, out_shape=jax.ShapeDtypeStruct((n_own, solves, gpt...  26.1 us
    pallas_call x2, Pallas kernels, update(): pl.pallas_call(make_update_kernel(margin, tile_scale, regions, first_swee...  14.6 us
    ppermute x6, waiting for transfers between devices, gather_slots(): lax.ppermute(x, axis, [(i, (i + s) % count) for i in range(count)])  10.3 us
    unnamed x44, local copies, waits for them, and re-layouts  8.47 us
    ppermute x6, starting transfers between devices, gather_slots(): lax.ppermute(x, axis, [(i, (i + s) % count) for i in range(count)])  7.34 us
    ppermute x1, waiting for transfers between devices, body(): lax.ppermute(tail, 'wide', [(i, (i + 1) % count) for i in range(count)])  5.41 us
    ppermute x1, starting transfers between devices, own_rows(): other = lax.ppermute(mine, pairs, other_pairs)  2.62 us
    ppermute x1, starting transfers between devices, body(): lax.ppermute(tail, 'wide', [(i, (i + 1) % count) for i in range(count)])  2.25 us
  transfers between devices with their start and end apart: 12, of which 5 were waited for; matrix products, arithmetic and copies ran while one was open for 7% of the time, Pallas kernels for 16%

profile of v10, /device:TPU:13, one launch (start us, length us, event | category | flops | bytes accessed | tf_op | source)
XLA Modules:
  0.0 88.8 jit_solution(2633181193635579604)
XLA Ops:
  0.7 0.8 fusion.4
  1.5 0.7 copy-done.18
  2.3 0.7 copy-done.13
  3.5 2.3 %collective-permute-start.7 = (f32[32,5,128]{2,1,0:T(8,128)S(1)}, f32[32,5,128]{2,1,0:T(8,128)S(1)}, u32[]{:S(2)}, u32[]{:S(2)}) collective-permute-start(f32[32,5,128]{2,1,0:T(8,128)S(1)} %concatenate.27), channel_id=1, source_target_pairs={{0,8},{4,12},{8,0},{12,4},{1,9},{5,13},{9,1},{13,5},{2,10},{6,14},... | collective-permute-start | bytes 245768 | tf_op jit(solution)/shard_map/ppermute | solution.py:37
  7.3 2.2 %collective-permute-start = (f32[16,16,128]{2,1,0:T(8,128)S(1)}, f32[16,16,128]{2,1,0:T(8,128)S(1)}, u32[]{:S(2)}, u32[]{:S(2)}) collective-permute-start(f32[16,16,128]{2,1,0:T(8,128)S(1)} %get-tuple-element.7), channel_id=1, source_target_pairs={{0,4},{4,8},{8,12},{12,0},{1,5},{5,9},{9,13},{13,1},{2,6},{6,10},{... | collective-permute-start | bytes 393224 | tf_op jit(solution)/shard_map/ppermute | solution.py:325
  9.5 0.7 copy-done.19
  10.8 0.8 stack.48.refs_0_
  11.6 0.7 copy-done.17
  12.3 0.7 copy.30.tc_ref
  14.2 5.4 %collective-permute-done.refs_1_ = f32[16,16,128]{2,1,0:T(8,128)S(1)} collective-permute-done((f32[16,16,128]{2,1,0:T(8,128)S(1)}, f32[16,16,128]{2,1,0:T(8,128)S(1)}, u32[]{:S(2)}, u32[]{:S(2)}) %collective-permute-start) | collective-permute-done | bytes 131104 | tf_op jit(solution)/shard_map/ppermute | solution.py:325
  20.9 7.3 %shard_map.140.refs_7_ = f32[16,8,128]{2,1,0:T(8,128)} custom-call(s32[3]{0:T(128)} %pad_add_fusion.scal_ref, s32[32,4]{1,0:T(8,128)} %copy.30.tc_ref, s32[32]{0:T(128)} %sizes_ref.3, f32[8]{0:T(128)} %ridge_ref.3, f32[8]{0:T(128)} %huber_ref.3, f32[8]{0:T(128)} %step_ref.3, f32[32,8,128]{2,1,0:T(8,128)} %stack.48.refs_0_, f32[16,16,128]{2,1,0:T(8,128)} %copy-done.3, ...), custom_call_target="tpu_custom_call" | custom-call | tf_op jit(solution)/shard_map/pallas_call | solution.py:152
  28.1 2.2 %collective-permute-start.2 = (f32[16,8,128]{2,1,0:T(8,128)}, f32[16,8,128]{2,1,0:T(8,128)S(1)}, u32[]{:S(2)}, u32[]{:S(2)}) collective-permute-start(f32[16,8,128]{2,1,0:T(8,128)} %shard_map.140.refs_7_), channel_id=1, source_target_pairs={{0,12},{1,5},{4,0},{5,9},{8,4},{9,13},{12,8},{13,1},{2,14},{3,7},{... | collective-permute-start | bytes 196616 | tf_op jit(solution)/shard_map/ppermute | solution.py:341
  30.3 1.1 %collective-permute-start.3 = (f32[16,8,128]{2,1,0:T(8,128)}, f32[16,8,128]{2,1,0:T(8,128)S(1)}, u32[]{:S(2)}, u32[]{:S(2)}) collective-permute-start(f32[16,8,128]{2,1,0:T(8,128)} %shard_map.140.refs_7_), channel_id=1, source_target_pairs={{0,13},{1,4},{4,1},{5,8},{8,5},{9,12},{12,9},{13,0},{2,15},{3,6},{... | collective-permute-start | bytes 196616 | tf_op jit(solution)/shard_map/ppermute | solution.py:342
  32.1 1.8 %collective-permute-start.6 = (f32[32,5,128]{2,1,0:T(8,128)S(1)}, f32[32,5,128]{2,1,0:T(8,128)S(1)}, u32[]{:S(2)}, u32[]{:S(2)}) collective-permute-start(f32[32,5,128]{2,1,0:T(8,128)S(1)} %concatenate.27), channel_id=1, source_target_pairs={{0,4},{4,8},{8,12},{12,0},{1,5},{5,9},{9,13},{13,1},{2,6},{6,10},{... | collective-permute-start | bytes 245768 | tf_op jit(solution)/shard_map/ppermute | solution.py:37
  35.6 7.3 %shard_map.141 = f32[16,8,128]{2,1,0:T(8,128)} custom-call(s32[3]{0:T(128)} %pad_add_fusion.scal_ref, s32[32,4]{1,0:T(8,128)} %copy.30.tc_ref, s32[32]{0:T(128)} %sizes_ref.3, f32[8]{0:T(128)} %ridge_ref.3, f32[8]{0:T(128)} %huber_ref.3, f32[8]{0:T(128)} %step_ref.3, f32[32,8,128]{2,1,0:T(8,128)} %stack.48.refs_0_, f32[16,16,128]{2,1,0:T(8,128)} %copy-done.3, ...), custom_call_target="tpu_custom_call" | custom-call | tf_op jit(solution)/shard_map/pallas_call | solution.py:152
  42.9 2.6 %collective-permute-start.5 = (f32[16,8,128]{2,1,0:T(8,128)}, f32[16,8,128]{2,1,0:T(8,128)S(1)}, u32[]{:S(2)}, u32[]{:S(2)}) collective-permute-start(f32[16,8,128]{2,1,0:T(8,128)} %shard_map.141), channel_id=1, source_target_pairs={{0,1},{1,0},{4,5},{5,4},{8,9},{9,8},{12,13},{13,12},{2,3},{3,2},{6... | collective-permute-start | bytes 196616 | tf_op jit(solution)/shard_map/ppermute | solution.py:330
  45.8 0.7 stack.50.gsites_ref
  46.7 0.7 collective-permute-start.9
  47.6 2.3 %collective-permute-start.10 = (f32[32,8,128]{2,1,0:T(8,128)S(1)}, f32[32,8,128]{2,1,0:T(8,128)S(1)}, u32[]{:S(2)}, u32[]{:S(2)}) collective-permute-start(f32[32,8,128]{2,1,0:T(8,128)S(1)} %get-tuple-element.5), channel_id=1, source_target_pairs={{0,8},{4,12},{8,0},{12,4},{1,9},{5,13},{9,1},{13,5},{2,10},{6,14},... | collective-permute-start | bytes 393224 | tf_op jit(solution)/shard_map/ppermute | solution.py:37
  50.7 0.8 concatenate.29.sites_ref
  51.6 7.2 %collective-permute-done.10 = f32[32,8,128]{2,1,0:T(8,128)S(1)} collective-permute-done((f32[32,8,128]{2,1,0:T(8,128)S(1)}, f32[32,8,128]{2,1,0:T(8,128)S(1)}, u32[]{:S(2)}, u32[]{:S(2)}) %collective-permute-start.10) | collective-permute-done | bytes 131104 | tf_op jit(solution)/shard_map/ppermute | solution.py:37
  58.8 3.1 %collective-permute-done.11 = f32[32,8,128]{2,1,0:T(8,128)S(1)} collective-permute-done((f32[32,8,128]{2,1,0:T(8,128)S(1)}, f32[32,8,128]{2,1,0:T(8,128)S(1)}, u32[]{:S(2)}, u32[]{:S(2)}) %collective-permute-start.11) | collective-permute-done | bytes 131104 | tf_op jit(solution)/shard_map/ppermute | solution.py:37
  61.9 0.8 copy-done.2
  62.7 26.1 %shard_map.142 = f32[4,8,512]{2,1,0:T(8,128)} custom-call(s32[1]{0:T(128)} %bitcast.8.me_ref, s32[4]{0:T(128)} %copy-done.16, s32[512]{0:T(512)} %convert_element_type.31.list_ref, f32[136,8,128]{2,1,0:T(8,128)} %concatenate.29.sites_ref, f32[136,8,128]{2,1,0:T(8,128)} %copy-done.2, f32[4,8,512]{2,1,0:T(8,128)} %stack.50.gsites_ref), custom_call_target="tpu_custom_call" | custom-call | tf_op jit(solution)/shard_map/pallas_call | solution.py:249
  (80 shorter events, 9.0 us)
Async XLA Ops:
  0.6 12.3 %copy-start = (f32[32,512]{1,0:T(8,128)S(1)}, f32[32,512]{1,0:T(8,128)}, u32[]{:S(2)}) copy-start(f32[32,512]{1,0:T(8,128)} %param.21) | copy-start | bytes 196612
  1.5 0.7 copy-start.18
  2.3 0.7 copy-start.13
  3.1 2.7 %copy-start.6 = (f32[32,128]{1,0:T(8,128)S(1)}, f32[32,128]{1,0:T(8,128)}, u32[]{:S(2)}) copy-start(f32[32,128]{1,0:T(8,128)} %refs_4_.3) | copy-start | bytes 49156
  3.3 2.6 %copy-start.7 = (f32[32,128]{1,0:T(8,128)S(1)}, f32[32,128]{1,0:T(8,128)}, u32[]{:S(2)}) copy-start(f32[32,128]{1,0:T(8,128)} %refs_3_.3) | copy-start | bytes 49156
  3.3 2.6 %copy-start.14 = (s32[32]{0:T(128)S(1)}, s32[32]{0:T(128)}, u32[]{:S(2)}) copy-start(s32[32]{0:T(128)} %sizes_ref.3) | copy-start | bytes 388
  3.3 44.2 %collective-permute-start.8 = (f32[32,5,128]{2,1,0:T(8,128)S(1)}, f32[32,5,128]{2,1,0:T(8,128)S(1)}, u32[]{:S(2)}, u32[]{:S(2)}) collective-permute-start(f32[32,5,128]{2,1,0:T(8,128)S(1)} %concatenate.27), channel_id=1, source_target_pairs={{0,12},{4,0},{8,4},{12,8},{1,13},{5,1},{9,5},{13,9},{2,14},{6,2},{... | collective-permute-start | bytes 245768 | tf_op jit(solution)/shard_map/ppermute | solution.py:37
  3.5 43.9 %collective-permute-start.7 = (f32[32,5,128]{2,1,0:T(8,128)S(1)}, f32[32,5,128]{2,1,0:T(8,128)S(1)}, u32[]{:S(2)}, u32[]{:S(2)}) collective-permute-start(f32[32,5,128]{2,1,0:T(8,128)S(1)} %concatenate.27), channel_id=1, source_target_pairs={{0,8},{4,12},{8,0},{12,4},{1,9},{5,13},{9,1},{13,5},{2,10},{6,14},... | collective-permute-start | bytes 245768 | tf_op jit(solution)/shard_map/ppermute | solution.py:37
  7.3 12.3 %collective-permute-start = (f32[16,16,128]{2,1,0:T(8,128)S(1)}, f32[16,16,128]{2,1,0:T(8,128)S(1)}, u32[]{:S(2)}, u32[]{:S(2)}) collective-permute-start(f32[16,16,128]{2,1,0:T(8,128)S(1)} %get-tuple-element.7), channel_id=1, source_target_pairs={{0,4},{4,8},{8,12},{12,0},{1,5},{5,9},{9,13},{13,1},{2,6},{6,10},{... | collective-permute-start | bytes 393224 | tf_op jit(solution)/shard_map/ppermute | solution.py:325
  9.5 10.1 %collective-permute-start.1 = (f32[16,16,128]{2,1,0:T(8,128)S(1)}, f32[16,16,128]{2,1,0:T(8,128)S(1)}, u32[]{:S(2)}, u32[]{:S(2)}) collective-permute-start(f32[16,16,128]{2,1,0:T(8,128)S(1)} %get-tuple-element.6), channel_id=1, source_target_pairs={{4,0},{8,4},{12,8},{0,12},{5,1},{9,5},{13,9},{1,13},{6,2},{10,6},{... | collective-permute-start | bytes 393224 | tf_op jit(solution)/shard_map/ppermute | solution.py:326
  11.6 0.7 copy-start.17
  20.9 10.7 %copy-start.9 = (f32[32,512]{1,0:T(8,128)S(1)}, f32[32,512]{1,0:T(8,128)}, u32[]{:S(2)}) copy-start(f32[32,512]{1,0:T(8,128)} %param.22) | copy-start | bytes 196612
  28.1 4.0 %collective-permute-start.2 = (f32[16,8,128]{2,1,0:T(8,128)}, f32[16,8,128]{2,1,0:T(8,128)S(1)}, u32[]{:S(2)}, u32[]{:S(2)}) collective-permute-start(f32[16,8,128]{2,1,0:T(8,128)} %shard_map.140.refs_7_), channel_id=1, source_target_pairs={{0,12},{1,5},{4,0},{5,9},{8,4},{9,13},{12,8},{13,1},{2,14},{3,7},{... | collective-permute-start | bytes 196616 | tf_op jit(solution)/shard_map/ppermute | solution.py:341
  30.3 4.0 %collective-permute-start.3 = (f32[16,8,128]{2,1,0:T(8,128)}, f32[16,8,128]{2,1,0:T(8,128)S(1)}, u32[]{:S(2)}, u32[]{:S(2)}) collective-permute-start(f32[16,8,128]{2,1,0:T(8,128)} %shard_map.140.refs_7_), channel_id=1, source_target_pairs={{0,13},{1,4},{4,1},{5,8},{8,5},{9,12},{12,9},{13,0},{2,15},{3,6},{... | collective-permute-start | bytes 196616 | tf_op jit(solution)/shard_map/ppermute | solution.py:342
  31.5 2.9 %collective-permute-start.4 = (f32[16,8,128]{2,1,0:T(8,128)}, f32[16,8,128]{2,1,0:T(8,128)S(1)}, u32[]{:S(2)}, u32[]{:S(2)}) collective-permute-start(f32[16,8,128]{2,1,0:T(8,128)} %shard_map.140.refs_7_), channel_id=1, source_target_pairs={{0,1},{1,0},{4,5},{5,4},{8,9},{9,8},{12,13},{13,12},{2,3},{3,2},{6... | collective-permute-start | bytes 196616 | tf_op jit(solution)/shard_map/ppermute | solution.py:340
  32.1 2.2 %copy-start.10 = (f32[16,8,128]{2,1,0:T(8,128)}, f32[16,8,128]{2,1,0:T(8,128)S(1)}, u32[]{:S(2)}) copy-start(f32[16,8,128]{2,1,0:T(8,128)S(1)} %collective-permute-done.2.refs_5_) | copy-start | bytes 196612
  32.1 15.3 %collective-permute-start.6 = (f32[32,5,128]{2,1,0:T(8,128)S(1)}, f32[32,5,128]{2,1,0:T(8,128)S(1)}, u32[]{:S(2)}, u32[]{:S(2)}) collective-permute-start(f32[32,5,128]{2,1,0:T(8,128)S(1)} %concatenate.27), channel_id=1, source_target_pairs={{0,4},{4,8},{8,12},{12,0},{1,5},{5,9},{9,13},{13,1},{2,6},{6,10},{... | collective-permute-start | bytes 245768 | tf_op jit(solution)/shard_map/ppermute | solution.py:37
  42.9 3.7 %collective-permute-start.5 = (f32[16,8,128]{2,1,0:T(8,128)}, f32[16,8,128]{2,1,0:T(8,128)S(1)}, u32[]{:S(2)}, u32[]{:S(2)}) collective-permute-start(f32[16,8,128]{2,1,0:T(8,128)} %shard_map.141), channel_id=1, source_target_pairs={{0,1},{1,0},{4,5},{5,4},{8,9},{9,8},{12,13},{13,12},{2,3},{3,2},{6... | collective-permute-start | bytes 196616 | tf_op jit(solution)/shard_map/ppermute | solution.py:330
  45.8 0.8 copy-start.5
  46.7 4.9 %copy-start.8 = (f32[32,8,128]{2,1,0:T(8,128)}, f32[32,8,128]{2,1,0:T(8,128)S(1)}, u32[]{:S(2)}) copy-start(f32[32,8,128]{2,1,0:T(8,128)S(1)} %get-tuple-element.5) | copy-start | bytes 393220
  46.7 4.9 %collective-permute-start.9 = (f32[32,8,128]{2,1,0:T(8,128)S(1)}, f32[32,8,128]{2,1,0:T(8,128)S(1)}, u32[]{:S(2)}, u32[]{:S(2)}) collective-permute-start(f32[32,8,128]{2,1,0:T(8,128)S(1)} %get-tuple-element.5), channel_id=1, source_target_pairs={{0,4},{4,8},{8,12},{12,0},{1,5},{5,9},{9,13},{13,1},{2,6},{6,10},{... | collective-permute-start | bytes 393224 | tf_op jit(solution)/shard_map/ppermute | solution.py:37
  47.6 11.2 %collective-permute-start.10 = (f32[32,8,128]{2,1,0:T(8,128)S(1)}, f32[32,8,128]{2,1,0:T(8,128)S(1)}, u32[]{:S(2)}, u32[]{:S(2)}) collective-permute-start(f32[32,8,128]{2,1,0:T(8,128)S(1)} %get-tuple-element.5), channel_id=1, source_target_pairs={{0,8},{4,12},{8,0},{12,4},{1,9},{5,13},{9,1},{13,5},{2,10},{6,14},... | collective-permute-start | bytes 393224 | tf_op jit(solution)/shard_map/ppermute | solution.py:37
  51.6 10.3 %collective-permute-start.11 = (f32[32,8,128]{2,1,0:T(8,128)S(1)}, f32[32,8,128]{2,1,0:T(8,128)S(1)}, u32[]{:S(2)}, u32[]{:S(2)}) collective-permute-start(f32[32,8,128]{2,1,0:T(8,128)S(1)} %get-tuple-element.5), channel_id=1, source_target_pairs={{0,12},{4,0},{8,4},{12,8},{1,13},{5,1},{9,5},{13,9},{2,14},{6,2},{... | collective-permute-start | bytes 393224 | tf_op jit(solution)/shard_map/ppermute | solution.py:37
  61.9 0.8 copy-start.2
  (8 other events, 5.0 us)

commit v11 on v8

--- a/solution.py
+++ b/solution.py
@@ -13,7 +13,7 @@
 HIGHEST = lax.Precision.HIGHEST
 MATMUL_PRECISION = lax.Precision.HIGH
 ROWS = 8
-GROUP = 4
+GROUP = 2
 
 
 def with_halo(cells, axis, width):

time: 87.7 us -> 88.6 us (1.010)
  the two profiles are of different devices: /device:TPU:0 before, /device:TPU:12 now
where the time goes in v11:
time: 88.6 us; the launch traced here: 87.6 us
  Pallas kernels  39.6 us (45%)
  waiting for transfers between devices  17.2 us (19%)
  starting transfers between devices  14.4 us (16%)
  local copies, waits for them, and re-layouts  13.8 us (16%)
  other arithmetic  1.73 us (2%)
  between operations  0.89 us (1%)
    pallas_call x1, Pallas kernels, grid_stage(): pl.pallas_call(kernel, out_shape=jax.ShapeDtypeStruct((n_own, solves, gpt...  25 us
    pallas_call x2, Pallas kernels, update(): pl.pallas_call(make_update_kernel(margin, tile_scale, regions, first_swee...  14.6 us
    ppermute x6, waiting for transfers between devices, gather_slots(): lax.ppermute(x, axis, [(i, (i + s) % count) for i in range(count)])  10 us
    ppermute x6, starting transfers between devices, gather_slots(): lax.ppermute(x, axis, [(i, (i + s) % count) for i in range(count)])  9.3 us
    unnamed x44, local copies, waits for them, and re-layouts  8.39 us
    ppermute x1, waiting for transfers between devices, body(): lax.ppermute(tail, 'wide', [(i, (i + 1) % count) for i in range(count)])  5.11 us
    ppermute x1, starting transfers between devices, body(): lax.ppermute(tail, 'wide', [(i, (i + 1) % count) for i in range(count)])  2.53 us
    ppermute x1, starting transfers between devices, body(): other = lax.ppermute(mine, pairs, other_pairs)  1.96 us
  transfers between devices with their start and end apart: 12, of which 6 were waited for; matrix products, arithmetic and copies ran while one was open for 8% of the time, Pallas kernels for 17%

profile of v11, /device:TPU:12, one launch (start us, length us, event | category | flops | bytes accessed | tf_op | source)
XLA Modules:
  0.0 87.6 jit_solution(7258905780037539093)
XLA Ops:
  0.7 0.8 fusion.4
  1.5 0.7 copy-done.18
  2.3 0.7 copy-done.13
  3.8 2.6 %collective-permute-start.7 = (f32[32,5,128]{2,1,0:T(8,128)S(1)}, f32[32,5,128]{2,1,0:T(8,128)S(1)}, u32[]{:S(2)}, u32[]{:S(2)}) collective-permute-start(f32[32,5,128]{2,1,0:T(8,128)S(1)} %concatenate.27), channel_id=1, source_target_pairs={{0,8},{4,12},{8,0},{12,4},{1,9},{5,13},{9,1},{13,5},{2,10},{6,14},... | collective-permute-start | bytes 245768 | tf_op jit(solution)/shard_map/ppermute | solution.py:37
  7.8 2.5 %collective-permute-start = (f32[16,16,128]{2,1,0:T(8,128)S(1)}, f32[16,16,128]{2,1,0:T(8,128)S(1)}, u32[]{:S(2)}, u32[]{:S(2)}) collective-permute-start(f32[16,16,128]{2,1,0:T(8,128)S(1)} %get-tuple-element.7), channel_id=1, source_target_pairs={{0,4},{4,8},{8,12},{12,0},{1,5},{5,9},{9,13},{13,1},{2,6},{6,10},{... | collective-permute-start | bytes 393224 | tf_op jit(solution)/shard_map/ppermute | solution.py:321
  10.4 0.7 copy-done.19
  11.6 0.8 stack.48.refs_0_
  12.4 0.7 copy-done.17
  13.1 0.7 copy.30.tc_ref
  15.0 5.1 %collective-permute-done.refs_1_ = f32[16,16,128]{2,1,0:T(8,128)S(1)} collective-permute-done((f32[16,16,128]{2,1,0:T(8,128)S(1)}, f32[16,16,128]{2,1,0:T(8,128)S(1)}, u32[]{:S(2)}, u32[]{:S(2)}) %collective-permute-start) | collective-permute-done | bytes 131104 | tf_op jit(solution)/shard_map/ppermute | solution.py:321
  21.4 7.3 %shard_map.140.refs_7_ = f32[16,8,128]{2,1,0:T(8,128)} custom-call(s32[3]{0:T(128)} %pad_add_fusion.scal_ref, s32[32,4]{1,0:T(8,128)} %copy.30.tc_ref, s32[32]{0:T(128)} %sizes_ref.3, f32[8]{0:T(128)} %ridge_ref.3, f32[8]{0:T(128)} %huber_ref.3, f32[8]{0:T(128)} %step_ref.3, f32[32,8,128]{2,1,0:T(8,128)} %stack.48.refs_0_, f32[16,16,128]{2,1,0:T(8,128)} %copy-done.3, ...), custom_call_target="tpu_custom_call" | custom-call | tf_op jit(solution)/shard_map/pallas_call | solution.py:152
  29.3 2.0 %collective-permute-start.4 = (f32[16,8,128]{2,1,0:T(8,128)}, f32[16,8,128]{2,1,0:T(8,128)S(1)}, u32[]{:S(2)}, u32[]{:S(2)}) collective-permute-start(f32[16,8,128]{2,1,0:T(8,128)} %shard_map.140.refs_7_), channel_id=1, source_target_pairs={{0,1},{1,0},{4,5},{5,4},{8,9},{9,8},{12,13},{13,12},{2,3},{3,2},{6... | collective-permute-start | bytes 196616 | tf_op jit(solution)/shard_map/ppermute | solution.py:336
  31.9 1.7 %collective-permute-done.2.refs_5_ = f32[16,8,128]{2,1,0:T(8,128)S(1)} collective-permute-done((f32[16,8,128]{2,1,0:T(8,128)}, f32[16,8,128]{2,1,0:T(8,128)S(1)}, u32[]{:S(2)}, u32[]{:S(2)}) %collective-permute-start.2) | collective-permute-done | bytes 65568 | tf_op jit(solution)/shard_map/ppermute | solution.py:337
  33.6 2.6 %collective-permute-start.6 = (f32[32,5,128]{2,1,0:T(8,128)S(1)}, f32[32,5,128]{2,1,0:T(8,128)S(1)}, u32[]{:S(2)}, u32[]{:S(2)}) collective-permute-start(f32[32,5,128]{2,1,0:T(8,128)S(1)} %concatenate.27), channel_id=1, source_target_pairs={{0,4},{4,8},{8,12},{12,0},{1,5},{5,9},{9,13},{13,1},{2,6},{6,10},{... | collective-permute-start | bytes 245768 | tf_op jit(solution)/shard_map/ppermute | solution.py:37
  37.5 7.3 %shard_map.141 = f32[16,8,128]{2,1,0:T(8,128)} custom-call(s32[3]{0:T(128)} %pad_add_fusion.scal_ref, s32[32,4]{1,0:T(8,128)} %copy.30.tc_ref, s32[32]{0:T(128)} %sizes_ref.3, f32[8]{0:T(128)} %ridge_ref.3, f32[8]{0:T(128)} %huber_ref.3, f32[8]{0:T(128)} %step_ref.3, f32[32,8,128]{2,1,0:T(8,128)} %stack.48.refs_0_, f32[16,16,128]{2,1,0:T(8,128)} %copy-done.3, ...), custom_call_target="tpu_custom_call" | custom-call | tf_op jit(solution)/shard_map/pallas_call | solution.py:152
  45.2 0.7 stack.50.gsites_ref
  46.3 1.0 %collective-permute-start.9 = (f32[32,8,128]{2,1,0:T(8,128)S(1)}, f32[32,8,128]{2,1,0:T(8,128)S(1)}, u32[]{:S(2)}, u32[]{:S(2)}) collective-permute-start(f32[32,8,128]{2,1,0:T(8,128)S(1)} %get-tuple-element.5), channel_id=1, source_target_pairs={{0,4},{4,8},{8,12},{12,0},{1,5},{5,9},{9,13},{13,1},{2,6},{6,10},{... | collective-permute-start | bytes 393224 | tf_op jit(solution)/shard_map/ppermute | solution.py:37
  47.4 2.6 %collective-permute-start.10 = (f32[32,8,128]{2,1,0:T(8,128)S(1)}, f32[32,8,128]{2,1,0:T(8,128)S(1)}, u32[]{:S(2)}, u32[]{:S(2)}) collective-permute-start(f32[32,8,128]{2,1,0:T(8,128)S(1)} %get-tuple-element.5), channel_id=1, source_target_pairs={{0,8},{4,12},{8,0},{12,4},{1,9},{5,13},{9,1},{13,5},{2,10},{6,14},... | collective-permute-start | bytes 393224 | tf_op jit(solution)/shard_map/ppermute | solution.py:37
  50.9 0.8 concatenate.29.sites_ref
  51.7 1.0 %collective-permute-done.9 = f32[32,8,128]{2,1,0:T(8,128)S(1)} collective-permute-done((f32[32,8,128]{2,1,0:T(8,128)S(1)}, f32[32,8,128]{2,1,0:T(8,128)S(1)}, u32[]{:S(2)}, u32[]{:S(2)}) %collective-permute-start.9) | collective-permute-done | bytes 131104 | tf_op jit(solution)/shard_map/ppermute | solution.py:37
  52.7 6.2 %collective-permute-done.10 = f32[32,8,128]{2,1,0:T(8,128)S(1)} collective-permute-done((f32[32,8,128]{2,1,0:T(8,128)S(1)}, f32[32,8,128]{2,1,0:T(8,128)S(1)}, u32[]{:S(2)}, u32[]{:S(2)}) %collective-permute-start.10) | collective-permute-done | bytes 131104 | tf_op jit(solution)/shard_map/ppermute | solution.py:37
  58.9 2.8 %collective-permute-done.11 = f32[32,8,128]{2,1,0:T(8,128)S(1)} collective-permute-done((f32[32,8,128]{2,1,0:T(8,128)S(1)}, f32[32,8,128]{2,1,0:T(8,128)S(1)}, u32[]{:S(2)}, u32[]{:S(2)}) %collective-permute-start.11) | collective-permute-done | bytes 131104 | tf_op jit(solution)/shard_map/ppermute | solution.py:37
  61.8 0.8 copy-done.2
  62.6 25.0 %shard_map.142 = f32[4,8,512]{2,1,0:T(8,128)} custom-call(s32[1]{0:T(128)} %bitcast.8.me_ref, s32[4]{0:T(128)} %copy-done.16, s32[512]{0:T(512)} %convert_element_type.31.list_ref, f32[136,8,128]{2,1,0:T(8,128)} %concatenate.29.sites_ref, f32[136,8,128]{2,1,0:T(8,128)} %copy-done.2, f32[4,8,512]{2,1,0:T(8,128)} %stack.50.gsites_ref), custom_call_target="tpu_custom_call" | custom-call | tf_op jit(solution)/shard_map/pallas_call | solution.py:246
  (80 shorter events, 9.8 us)
Async XLA Ops:
  0.6 13.1 %copy-start = (f32[32,512]{1,0:T(8,128)S(1)}, f32[32,512]{1,0:T(8,128)}, u32[]{:S(2)}) copy-start(f32[32,512]{1,0:T(8,128)} %param.21) | copy-start | bytes 196612
  1.5 0.7 copy-start.18
  2.3 0.7 copy-start.13
  3.1 3.3 %copy-start.6 = (f32[32,128]{1,0:T(8,128)S(1)}, f32[32,128]{1,0:T(8,128)}, u32[]{:S(2)}) copy-start(f32[32,128]{1,0:T(8,128)} %refs_4_.3) | copy-start | bytes 49156
  3.3 3.1 %copy-start.7 = (f32[32,128]{1,0:T(8,128)S(1)}, f32[32,128]{1,0:T(8,128)}, u32[]{:S(2)}) copy-start(f32[32,128]{1,0:T(8,128)} %refs_3_.3) | copy-start | bytes 49156
  3.3 3.1 %copy-start.14 = (s32[32]{0:T(128)S(1)}, s32[32]{0:T(128)}, u32[]{:S(2)}) copy-start(s32[32]{0:T(128)} %sizes_ref.3) | copy-start | bytes 388
  3.3 44.0 %collective-permute-start.8 = (f32[32,5,128]{2,1,0:T(8,128)S(1)}, f32[32,5,128]{2,1,0:T(8,128)S(1)}, u32[]{:S(2)}, u32[]{:S(2)}) collective-permute-start(f32[32,5,128]{2,1,0:T(8,128)S(1)} %concatenate.27), channel_id=1, source_target_pairs={{0,12},{4,0},{8,4},{12,8},{1,13},{5,1},{9,5},{13,9},{2,14},{6,2},{... | collective-permute-start | bytes 245768 | tf_op jit(solution)/shard_map/ppermute | solution.py:37
  3.8 43.5 %collective-permute-start.7 = (f32[32,5,128]{2,1,0:T(8,128)S(1)}, f32[32,5,128]{2,1,0:T(8,128)S(1)}, u32[]{:S(2)}, u32[]{:S(2)}) collective-permute-start(f32[32,5,128]{2,1,0:T(8,128)S(1)} %concatenate.27), channel_id=1, source_target_pairs={{0,8},{4,12},{8,0},{12,4},{1,9},{5,13},{9,1},{13,5},{2,10},{6,14},... | collective-permute-start | bytes 245768 | tf_op jit(solution)/shard_map/ppermute | solution.py:37
  7.8 12.3 %collective-permute-start = (f32[16,16,128]{2,1,0:T(8,128)S(1)}, f32[16,16,128]{2,1,0:T(8,128)S(1)}, u32[]{:S(2)}, u32[]{:S(2)}) collective-permute-start(f32[16,16,128]{2,1,0:T(8,128)S(1)} %get-tuple-element.7), channel_id=1, source_target_pairs={{0,4},{4,8},{8,12},{12,0},{1,5},{5,9},{9,13},{13,1},{2,6},{6,10},{... | collective-permute-start | bytes 393224 | tf_op jit(solution)/shard_map/ppermute | solution.py:321
  10.4 9.7 %collective-permute-start.1 = (f32[16,16,128]{2,1,0:T(8,128)S(1)}, f32[16,16,128]{2,1,0:T(8,128)S(1)}, u32[]{:S(2)}, u32[]{:S(2)}) collective-permute-start(f32[16,16,128]{2,1,0:T(8,128)S(1)} %get-tuple-element.6), channel_id=1, source_target_pairs={{4,0},{8,4},{12,8},{0,12},{5,1},{9,5},{13,9},{1,13},{6,2},{10,6},{... | collective-permute-start | bytes 393224 | tf_op jit(solution)/shard_map/ppermute | solution.py:322
  12.4 0.7 copy-start.17
  21.4 10.0 %copy-start.9 = (f32[32,512]{1,0:T(8,128)S(1)}, f32[32,512]{1,0:T(8,128)}, u32[]{:S(2)}) copy-start(f32[32,512]{1,0:T(8,128)} %param.22) | copy-start | bytes 196612
  28.7 4.9 %collective-permute-start.2 = (f32[16,8,128]{2,1,0:T(8,128)}, f32[16,8,128]{2,1,0:T(8,128)S(1)}, u32[]{:S(2)}, u32[]{:S(2)}) collective-permute-start(f32[16,8,128]{2,1,0:T(8,128)} %shard_map.140.refs_7_), channel_id=1, source_target_pairs={{0,12},{1,5},{4,0},{5,9},{8,4},{9,13},{12,8},{13,1},{2,14},{3,7},{... | collective-permute-start | bytes 196616 | tf_op jit(solution)/shard_map/ppermute | solution.py:337
  28.7 7.6 %collective-permute-start.3 = (f32[16,8,128]{2,1,0:T(8,128)}, f32[16,8,128]{2,1,0:T(8,128)S(1)}, u32[]{:S(2)}, u32[]{:S(2)}) collective-permute-start(f32[16,8,128]{2,1,0:T(8,128)} %shard_map.140.refs_7_), channel_id=1, source_target_pairs={{0,13},{1,4},{4,1},{5,8},{8,5},{9,12},{12,9},{13,0},{2,15},{3,6},{... | collective-permute-start | bytes 196616 | tf_op jit(solution)/shard_map/ppermute | solution.py:338
  29.3 6.9 %collective-permute-start.4 = (f32[16,8,128]{2,1,0:T(8,128)}, f32[16,8,128]{2,1,0:T(8,128)S(1)}, u32[]{:S(2)}, u32[]{:S(2)}) collective-permute-start(f32[16,8,128]{2,1,0:T(8,128)} %shard_map.140.refs_7_), channel_id=1, source_target_pairs={{0,1},{1,0},{4,5},{5,4},{8,9},{9,8},{12,13},{13,12},{2,3},{3,2},{6... | collective-permute-start | bytes 196616 | tf_op jit(solution)/shard_map/ppermute | solution.py:336
  33.6 2.6 %copy-start.10 = (f32[16,8,128]{2,1,0:T(8,128)}, f32[16,8,128]{2,1,0:T(8,128)S(1)}, u32[]{:S(2)}) copy-start(f32[16,8,128]{2,1,0:T(8,128)S(1)} %collective-permute-done.2.refs_5_) | copy-start | bytes 196612
  33.6 13.7 %collective-permute-start.6 = (f32[32,5,128]{2,1,0:T(8,128)S(1)}, f32[32,5,128]{2,1,0:T(8,128)S(1)}, u32[]{:S(2)}, u32[]{:S(2)}) collective-permute-start(f32[32,5,128]{2,1,0:T(8,128)S(1)} %concatenate.27), channel_id=1, source_target_pairs={{0,4},{4,8},{8,12},{12,0},{1,5},{5,9},{9,13},{13,1},{2,6},{6,10},{... | collective-permute-start | bytes 245768 | tf_op jit(solution)/shard_map/ppermute | solution.py:37
  44.8 1.5 %collective-permute-start.5 = (f32[16,8,128]{2,1,0:T(8,128)}, f32[16,8,128]{2,1,0:T(8,128)S(1)}, u32[]{:S(2)}, u32[]{:S(2)}) collective-permute-start(f32[16,8,128]{2,1,0:T(8,128)} %shard_map.141), channel_id=1, source_target_pairs={{0,1},{1,0},{4,5},{5,4},{8,9},{9,8},{12,13},{13,12},{2,3},{3,2},{6... | collective-permute-start | bytes 196616 | tf_op jit(solution)/shard_map/ppermute | solution.py:326
  45.2 1.1 %copy-start.5 = (f32[16,8,128]{2,1,0:T(8,128)S(1)}, f32[16,8,128]{2,1,0:T(8,128)}, u32[]{:S(2)}) copy-start(f32[16,8,128]{2,1,0:T(8,128)} %shard_map.141) | copy-start | bytes 196612
  46.3 5.5 %copy-start.8 = (f32[32,8,128]{2,1,0:T(8,128)}, f32[32,8,128]{2,1,0:T(8,128)S(1)}, u32[]{:S(2)}) copy-start(f32[32,8,128]{2,1,0:T(8,128)S(1)} %get-tuple-element.5) | copy-start | bytes 393220
  46.3 6.4 %collective-permute-start.9 = (f32[32,8,128]{2,1,0:T(8,128)S(1)}, f32[32,8,128]{2,1,0:T(8,128)S(1)}, u32[]{:S(2)}, u32[]{:S(2)}) collective-permute-start(f32[32,8,128]{2,1,0:T(8,128)S(1)} %get-tuple-element.5), channel_id=1, source_target_pairs={{0,4},{4,8},{8,12},{12,0},{1,5},{5,9},{9,13},{13,1},{2,6},{6,10},{... | collective-permute-start | bytes 393224 | tf_op jit(solution)/shard_map/ppermute | solution.py:37
  47.4 11.5 %collective-permute-start.10 = (f32[32,8,128]{2,1,0:T(8,128)S(1)}, f32[32,8,128]{2,1,0:T(8,128)S(1)}, u32[]{:S(2)}, u32[]{:S(2)}) collective-permute-start(f32[32,8,128]{2,1,0:T(8,128)S(1)} %get-tuple-element.5), channel_id=1, source_target_pairs={{0,8},{4,12},{8,0},{12,4},{1,9},{5,13},{9,1},{13,5},{2,10},{6,14},... | collective-permute-start | bytes 393224 | tf_op jit(solution)/shard_map/ppermute | solution.py:37
  51.7 10.0 %collective-permute-start.11 = (f32[32,8,128]{2,1,0:T(8,128)S(1)}, f32[32,8,128]{2,1,0:T(8,128)S(1)}, u32[]{:S(2)}, u32[]{:S(2)}) collective-permute-start(f32[32,8,128]{2,1,0:T(8,128)S(1)} %get-tuple-element.5), channel_id=1, source_target_pairs={{0,12},{4,0},{8,4},{12,8},{1,13},{5,1},{9,5},{13,9},{2,14},{6,2},{... | collective-permute-start | bytes 393224 | tf_op jit(solution)/shard_map/ppermute | solution.py:37
  61.8 0.8 copy-start.2
  (8 other events, 5.0 us)
